TPU v7x, 32 devices: a whole 2x2x4 slice. The times are simulated.
32 devices in a mesh: dp: 4 (over z), ctx: 8 (over y, x, core).
Axes of the slice: x: 2, y: 2, z: 4, core: 2. Of those that a mesh axis runs over, the one named last changes fastest.
Arguments:
- tokens: bfloat16 [4, 1024, 6144], P('dp', 'ctx'), may hold values from -0.1875 to 0.1875
- cotangent: bfloat16 [4, 1024, 6144], P('dp', 'ctx'), may hold values from -6 to 6
- w_router: float32 [6144], replicated, may hold values from -2 to 2
- w_query: bfloat16 [6144, 4096], P(None, 'ctx'), may hold values from -0.078125 to 0.078125
- w_key: bfloat16 [6144, 4096], P(None, 'ctx'), may hold values from -0.078125 to 0.078125
- w_value: bfloat16 [6144, 4096], P(None, 'ctx'), may hold values from -0.078125 to 0.078125
- w_out: bfloat16 [4096, 6144], P('ctx'), may hold values from -0.09375 to 0.09375
- chosen: int32 [4, 160], P('dp', 'ctx'), may hold values from -1 to 1023, as said below
- counts: int32 [4, 8], P('dp', 'ctx'), may hold values from 12 to 20, as said below
Outputs:
- layer_out: bfloat16 [4, 1024, 6144], P('dp', 'ctx')
- grad_query: bfloat16 [6144, 4096], P('dp', 'ctx')
- grad_key: bfloat16 [6144, 4096], P('dp', 'ctx')
- grad_value: bfloat16 [6144, 4096], P('dp', 'ctx')
- grad_out: bfloat16 [4096, 6144], P('ctx', 'dp')
- grad_router: float32 [6144], replicated
Inputs may be any that keep to these rules, and one draw needn't show every extreme that they name: `chosen`: for every sequence b and device block c, the first counts[b, c] of the block's slots c * 20 to (c + 1) * 20 - 1 hold increasing positions of that device's tokens, c * 128 to (c + 1) * 128 - 1; the other slots hold -1. In every sequence the counts add up to 128, and some device's block has exactly 20 used slots.
All inputs are finite; a program needn't handle non-finite values.
Results may differ from a plain program's by a relative error of at most 0.018.
Values may be sent and summed in bfloat16 or wider, within the bound.
No kernel may reach another device: no remote copies, remote signals or barrier semaphores. Data moves between devices by JAX's collectives and lax.ppermute only.
A program may use at most 128 MiB of HBM per device.

v0:
```python
import math

import jax
import jax.numpy as jnp
from jax import lax
from jax.sharding import PartitionSpec as P

HDIM = 128


HIGHEST_PRECISION = lax.Precision.HIGHEST
ROW_CONTRACT = (((0,), (0,)), ((), ()))
COLUMN_CONTRACT = (((1,), (1,)), ((), ()))


def head_norm(values, width):
    shaped = values.reshape(values.shape[0], -1, width)
    inverse = lax.rsqrt(jnp.mean(shaped * shaped, axis=-1, keepdims=True) + 1e-06)
    return (shaped * inverse, inverse)


def norm_back(grad_hat, normal, inverse):
    return inverse * (grad_hat - normal * jnp.mean(grad_hat * normal, axis=-1, keepdims=True))


def rounded_term(part):
    return lax.optimization_barrier(part.astype(jnp.bfloat16)).astype(jnp.float32)


def body(tokens, cotangent, w_router, w_query, w_key, w_value, w_out, chosen, counts):
    length = tokens.shape[1]
    capacity = chosen.shape[1]
    inner = w_query.shape[1]
    heads_here = inner // HDIM
    scale = 1.0 / math.sqrt(HDIM)
    offset = lax.axis_index("ctx") * length
    slot_ids = lax.broadcasted_iota(jnp.int32, (capacity,), 0)
    local = chosen[0] - offset
    present = (slot_ids < counts[0, 0]) & (local >= 0) & (local < length)
    columns = lax.broadcasted_iota(jnp.int32, (capacity, length), 1)
    onehot = ((local[:, None] == columns) & present[:, None]).astype(jnp.bfloat16)
    rows = jnp.dot(onehot, tokens[0], preferred_element_type=jnp.float32)
    rows_back = jnp.dot(onehot, cotangent[0], preferred_element_type=jnp.float32)
    logits = jnp.dot(rows, w_router, precision=HIGHEST_PRECISION)
    weights = jax.nn.sigmoid(logits)
    normed = (rows * lax.rsqrt(jnp.mean(rows * rows, axis=-1, keepdims=True) + 1e-05)).astype(
        jnp.bfloat16
    )
    delta = (weights[:, None] * rows_back).astype(jnp.bfloat16)
    all_normed, all_delta, all_present = (
        lax.all_gather(normed, "ctx", axis=0, tiled=True),
        lax.all_gather(delta, "ctx", axis=0, tiled=True),
        lax.all_gather(present.astype(jnp.bfloat16), "ctx", axis=0, tiled=True),
    )
    slots = all_normed.shape[0]
    query_raw = jnp.dot(all_normed, w_query, preferred_element_type=jnp.float32)
    key_raw = jnp.dot(all_normed, w_key, preferred_element_type=jnp.float32)
    value_raw = jnp.dot(all_normed, w_value, preferred_element_type=jnp.float32)
    query_hat, query_scale = head_norm(query_raw, HDIM)
    key_hat, key_scale = head_norm(key_raw, HDIM)
    query_b = query_hat.astype(jnp.bfloat16)
    key_b = key_hat.astype(jnp.bfloat16)
    value_b = value_raw.reshape(slots, heads_here, HDIM).astype(jnp.bfloat16)
    current = lax.broadcasted_iota(jnp.int32, (slots, slots), 0)
    earlier = lax.broadcasted_iota(jnp.int32, (slots, slots), 1)
    allowed = (earlier <= current) & ((all_present[None, :] > 0.5) | (earlier == current))
    scores = jnp.einsum("ihd,jhd->hij", query_b, key_b, preferred_element_type=jnp.float32) * scale
    exponent = jnp.where(allowed[None], jnp.exp(scores), 0.0)
    attend = exponent / jnp.sum(exponent, axis=-1, keepdims=True)
    attend_b = attend.astype(jnp.bfloat16)
    mixed = jnp.einsum("hij,jhd->ihd", attend_b, value_b, preferred_element_type=jnp.float32)
    mixed = mixed.astype(jnp.bfloat16).reshape(slots, inner)
    update = lax.psum_scatter(
        rounded_term(jnp.dot(mixed, w_out, preferred_element_type=jnp.float32)).astype(
            jnp.bfloat16
        ),
        "ctx",
        scatter_dimension=0,
        tiled=True,
    ).astype(jnp.float32)
    scaled = weights[:, None] * update
    spread = jnp.dot(onehot.astype(jnp.float32).T, scaled, precision=HIGHEST_PRECISION)
    layer_out = (tokens[0].astype(jnp.float32) + spread).astype(jnp.bfloat16)[None]
    gate_back = jnp.sum(rows_back * update, axis=-1) * weights * (1.0 - weights)
    router_part = jnp.dot(gate_back, rows, precision=HIGHEST_PRECISION)
    grad_router = lax.psum(router_part, ("dp", "ctx"))
    out_term = rounded_term(
        lax.dot_general(mixed, all_delta, ROW_CONTRACT, preferred_element_type=jnp.float32)
    )
    mixed_back = lax.dot_general(
        all_delta, w_out, COLUMN_CONTRACT, preferred_element_type=jnp.float32
    )
    mixed_back = mixed_back.astype(jnp.bfloat16).reshape(slots, heads_here, HDIM)
    attend_back = jnp.einsum(
        "ihd,jhd->hij", mixed_back, value_b, preferred_element_type=jnp.float32
    )
    inner_sum = jnp.sum(attend * attend_back, axis=-1, keepdims=True)
    scores_back = (attend * (attend_back - inner_sum) * scale).astype(jnp.bfloat16)
    value_back = jnp.einsum(
        "hij,ihd->jhd", attend_b, mixed_back, preferred_element_type=jnp.float32
    )
    value_back = value_back.astype(jnp.bfloat16).reshape(slots, inner)
    qhat_back = jnp.einsum("hij,jhd->ihd", scores_back, key_b, preferred_element_type=jnp.float32)
    khat_back = jnp.einsum("hij,ihd->jhd", scores_back, query_b, preferred_element_type=jnp.float32)
    query_back = (
        norm_back(qhat_back, query_hat, query_scale).astype(jnp.bfloat16).reshape(slots, inner)
    )
    key_back = norm_back(khat_back, key_hat, key_scale).astype(jnp.bfloat16).reshape(slots, inner)
    query_term = rounded_term(
        lax.dot_general(all_normed, query_back, ROW_CONTRACT, preferred_element_type=jnp.float32)
    )
    key_term = rounded_term(
        lax.dot_general(all_normed, key_back, ROW_CONTRACT, preferred_element_type=jnp.float32)
    )
    value_term = rounded_term(
        lax.dot_general(all_normed, value_back, ROW_CONTRACT, preferred_element_type=jnp.float32)
    )
    grad_query, grad_key, grad_value, grad_out = (
        lax.psum_scatter(
            query_term.astype(jnp.bfloat16), "dp", scatter_dimension=0, tiled=True
        ).astype(jnp.float32),
        lax.psum_scatter(
            key_term.astype(jnp.bfloat16), "dp", scatter_dimension=0, tiled=True
        ).astype(jnp.float32),
        lax.psum_scatter(
            value_term.astype(jnp.bfloat16), "dp", scatter_dimension=0, tiled=True
        ).astype(jnp.float32),
        lax.psum_scatter(
            out_term.astype(jnp.bfloat16), "dp", scatter_dimension=1, tiled=True
        ).astype(jnp.float32),
    )
    return (
        layer_out,
        grad_query.astype(jnp.bfloat16),
        grad_key.astype(jnp.bfloat16),
        grad_value.astype(jnp.bfloat16),
        grad_out.astype(jnp.bfloat16),
        grad_router,
    )


def solution(mesh):
    in_specs = (
        P("dp", "ctx", None),
        P("dp", "ctx", None),
        P(),
        P(None, "ctx"),
        P(None, "ctx"),
        P(None, "ctx"),
        P("ctx", None),
        P("dp", "ctx"),
        P("dp", "ctx"),
    )
    out_specs = (
        P("dp", "ctx", None),
        P("dp", "ctx"),
        P("dp", "ctx"),
        P("dp", "ctx"),
        P("ctx", "dp"),
        P(),
    )
    return jax.shard_map(body, mesh=mesh, in_specs=in_specs, out_specs=out_specs, check_vma=False)
```

profile of v0, /device:TPU:2, one launch (start us, length us, event | category | flops | bytes accessed | tf_op | source)
XLA Modules:
  0.0 628.8 jit_solution(3186163892697100419)
XLA Ops:
  7.2 0.0 copy-start
  7.2 0.0 all-gather.5.cloned.1.call-start
  8.0 0.7 fusion.88
  8.7 1.9 multiply_reduce_fusion.1
  10.6 0.9 fusion.31
  11.5 0.0 all-gather.5.cloned.1.call-update
  11.5 0.0 all-gather.7.cloned.1.call-start
  11.6 0.7 fusion.89
  12.9 0.2 dynamic-update-slice
  13.1 11.1 %all-reduce = bf16[160]{0:T(256)(128)(2,1)S(1)} all-reduce(bf16[160]{0:T(256)(128)(2,1)S(1)} %dynamic-update-slice), channel_id=1, replica_groups=mesh['dp'=4,'ctx'=8] {'ctx'}, use_global_device_ids=true, to_apply=%add | all-reduce | flops 160 | bytes 640
  24.3 0.7 fusion.54
  25.0 17.0 %all-gather.5.cloned.1.call-done = bf16[8,20,6144]{2,1,0:T(8,128)(2,1)} async-done(((bf16[1,20,6144]{2,1,0:T(8,128)(2,1)}), bf16[8,20,6144]{2,1,0:T(8,128)(2,1)}) %all-gather.5.cloned.1.call-update) | async-done | bytes 1966096 | tf_op jit(solution)/shard_map/all_gather | solution.py:51
  42.0 2.6 reshape.127
  44.6 0.0 slice-start
  44.6 4.8 fusion.16
  49.4 4.8 fusion.103
  54.2 1.9 fusion.102
  56.1 1.8 reshape.116
  57.9 1.9 multiply_reduce_fusion.5
  59.8 1.0 copy.67
  60.8 1.8 reshape.117
  62.6 1.9 multiply_reduce_fusion.4
  64.4 1.0 copy.69
  65.4 2.4 fusion.28
  67.8 1.5 fusion.14
  69.3 0.6 copy-done.7
  69.9 5.4 convolution_convert_fusion.4
  75.3 29.5 %fusion = bf16[24,6144]{1,0:T(8,128)(2,1)} fusion(bf16[160,6144]{1,0:T(8,128)(2,1)} %convolution_convert_fusion.4), kind=kCustom, calls=%all-reduce-scatter | all-reduce-scatter fusion | flops 1179649 | bytes 2261504
  104.8 1.9 collective-permute-start
  106.7 1.5 slice
  108.2 4.2 collective-permute-start.1
  112.4 2.3 fusion.21
  115.4 9.6 %concatenate = bf16[52,6144]{1,0:T(8,128)(2,1)} concatenate(bf16[4,6144]{1,0:T(4,128)(2,1)} %collective-permute-done.1, bf16[24,6144]{1,0:T(8,128)(2,1)} %collective-permute-done, bf16[24,6144]{1,0:T(8,128)(2,1)} %fusion), dimensions={0} | concatenate | bytes 1277952
  125.0 2.8 fusion.26
  127.8 0.0 all-gather.7.cloned.1.call-update
  127.8 0.0 reduce-scatter.13.cloned.1.call-start
  127.9 30.0 %all-gather.7.cloned.1.call-done = bf16[8,20,6144]{2,1,0:T(8,128)(2,1)} async-done(((bf16[1,20,6144]{2,1,0:T(8,128)(2,1)}), bf16[8,20,6144]{2,1,0:T(8,128)(2,1)}) %all-gather.7.cloned.1.call-update) | async-done | bytes 1966096 | tf_op jit(solution)/shard_map/all_gather | solution.py:52
  157.8 4.0 reshape.129
  161.8 6.0 convolution_convert_fusion
  167.9 0.0 reduce-scatter.13.cloned.1.call-update
  167.9 0.2 reduce-scatter.7.cloned.1.call-start
  168.2 5.8 fusion.17
  174.0 0.7 copy-done.10
  174.7 1.1 fusion.48
  175.7 2.6 multiply_reduce_fusion.3
  178.4 5.6 convolution_convert_fusion.3
  184.0 0.0 reduce-scatter.7.cloned.1.call-update
  184.0 0.0 reduce-scatter.9.cloned.1.call-start
  184.1 2.4 multiply_reduce_fusion.2
  186.5 5.6 convolution_convert_fusion.2
  192.1 0.0 reduce-scatter.9.cloned.1.call-update
  192.1 0.0 reduce-scatter.11.cloned.1.call-start
  192.2 0.8 copy-done.11
  193.0 0.2 fusion.15
  193.2 4.4 convolution_convert_fusion.1
  197.7 0.0 reduce-scatter.11.cloned.1.call-update
  197.7 1.0 copy-done.3
  198.7 0.4 fusion.77
  199.1 47.8 %psum.7 = f32[6144]{0:T(1024)} all-reduce(f32[6144]{0:T(1024)S(1)} %bitcast.169), channel_id=1, replica_groups=mesh['dp'=4,'ctx'=8] {'dp','ctx'}, use_global_device_ids=true, to_apply=%region_13.14 | all-reduce | flops 6144 | bytes 49152 | tf_op jit(solution)/shard_map/psum | solution.py:86
  247.0 4.4 fusion.3
  251.3 28.5 %reduce-scatter.13.cloned.1.call-done = bf16[512,1536]{1,0:T(8,128)(2,1)} async-done(((bf16[512,6144]{1,0:T(8,128)(2,1)}), bf16[512,1536]{1,0:T(8,128)(2,1)}) %reduce-scatter.13.cloned.1.call-update) | async-done | bytes 1572880 | tf_op jit(solution)/shard_map/reduce_scatter | solution.py:128
  279.9 114.0 %reduce-scatter.7.cloned.1.call-done = bf16[1536,512]{1,0:T(8,128)(2,1)} async-done(((bf16[6144,512]{1,0:T(8,128)(2,1)}), bf16[1536,512]{1,0:T(8,128)(2,1)}) %reduce-scatter.7.cloned.1.call-update) | async-done | bytes 1572880 | tf_op jit(solution)/shard_map/reduce_scatter | solution.py:119
  393.8 114.0 %reduce-scatter.9.cloned.1.call-done = bf16[1536,512]{1,0:T(8,128)(2,1)} async-done(((bf16[6144,512]{1,0:T(8,128)(2,1)}), bf16[1536,512]{1,0:T(8,128)(2,1)}) %reduce-scatter.9.cloned.1.call-update) | async-done | bytes 1572880 | tf_op jit(solution)/shard_map/reduce_scatter | solution.py:122
  507.9 114.0 %reduce-scatter.11.cloned.1.call-done = bf16[1536,512]{1,0:T(8,128)(2,1)} async-done(((bf16[6144,512]{1,0:T(8,128)(2,1)}), bf16[1536,512]{1,0:T(8,128)(2,1)}) %reduce-scatter.11.cloned.1.call-update) | async-done | bytes 1572880 | tf_op jit(solution)/shard_map/reduce_scatter | solution.py:125
  (45 shorter events, 0.1 us)
Async XLA Ops:
  7.2 117.8 %copy-start = (bf16[1,128,6144]{2,1,0:T(8,128)(2,1)S(1)}, bf16[1,128,6144]{2,1,0:T(8,128)(2,1)}, u32[]{:S(2)}) copy-start(bf16[1,128,6144]{2,1,0:T(8,128)(2,1)} %param.10) | copy-start | bytes 4718596
  7.2 4.4 copy-start.18
  7.2 34.8 %all-gather.5.cloned.1.call-start = ((), (), s32[]{:S(2)}) async-start(), calls=%async_computation.8 | async-start | bytes 2654208 | tf_op jit(solution)/shard_map/all_gather | solution.py:51
  8.7 16.3 %copy-start.12 = (pred[20]{0:T(512)(128)(4,1)}, pred[20]{0:T(512)(128)(4,1)S(1)}, u32[]{:S(2)}) copy-start(pred[20]{0:T(512)(128)(4,1)S(1)} %get-tuple-element.7) | copy-start | bytes 64
  8.7 16.3 %copy-start.14 = (s32[20]{0:T(128)}, s32[20]{0:T(128)S(1)}, u32[]{:S(2)}) copy-start(s32[20]{0:T(128)S(1)} %get-tuple-element.8) | copy-start | bytes 244
  10.6 14.4 %copy-start.2 = (f32[20,6144]{1,0:T(8,128)}, f32[20,6144]{1,0:T(8,128)S(1)}, u32[]{:S(2)}) copy-start(f32[20,6144]{1,0:T(8,128)S(1)} %get-tuple-element.14) | copy-start | bytes 1474564
  11.5 146.3 %all-gather.7.cloned.1.call-start = ((), (), s32[]{:S(2)}) async-start(), calls=%async_computation.9 | async-start | bytes 2654208 | tf_op jit(solution)/shard_map/all_gather | solution.py:52
  44.6 9.6 %slice-start = ((s8[6291456]{0:T(1024)(128)(4,1)}), s8[4194304]{0:T(1024)(128)(4,1)S(1)}, s32[]{:S(2)}) async-start(s8[6291456]{0:T(1024)(128)(4,1)} %bitcast.167), calls=%async_computation.10 | async-start | bytes 8388608
  49.4 4.8 slice-start.1
  69.3 0.7 copy-start.7
  75.3 49.7 %copy-start.13 = (pred[20]{0:T(512)(128)(4,1)S(1)}, pred[20]{0:T(512)(128)(4,1)}, u32[]{:S(2)}) copy-start(pred[20]{0:T(512)(128)(4,1)} %copy-done.12) | copy-start | bytes 64
  75.3 49.7 %copy-start.15 = (s32[20]{0:T(128)S(1)}, s32[20]{0:T(128)}, u32[]{:S(2)}) copy-start(s32[20]{0:T(128)} %copy-done.14) | copy-start | bytes 244
  104.8 10.6 %collective-permute-start = (bf16[24,6144]{1,0:T(8,128)(2,1)}, bf16[24,6144]{1,0:T(8,128)(2,1)}, u32[]{:S(2)}, u32[]{:S(2)}) collective-permute-start(bf16[24,6144]{1,0:T(8,128)(2,1)} %fusion), channel_id=1, source_target_pairs={{0,1},{1,2},{2,3},{3,4},{4,5},{5,6},{6,7},{8,9},{9,10},{10,11},{11... | collective-permute-start | bytes 884744
  108.2 7.2 %collective-permute-start.1 = (bf16[4,6144]{1,0:T(4,128)(2,1)}, bf16[4,6144]{1,0:T(4,128)(2,1)}, u32[]{:S(2)}, u32[]{:S(2)}) collective-permute-start(bf16[4,6144]{1,0:T(4,128)(2,1)} %slice), channel_id=1, source_target_pairs={{0,2},{1,3},{2,4},{3,5},{4,6},{5,7},{8,10},{9,11},{10,12},{11,13},... | collective-permute-start | bytes 147464
  127.8 34.0 %copy-start.8 = (bf16[4,20,8,128]{3,2,1,0:T(8,128)(2,1)S(1)}, bf16[4,20,8,128]{3,2,1,0:T(8,128)(2,1)}, u32[]{:S(2)}) copy-start(bf16[4,20,8,128]{3,2,1,0:T(8,128)(2,1)} %copy-done.7) | copy-start | bytes 491524
  127.8 152.0 %reduce-scatter.13.cloned.1.call-start = ((), (), s32[]{:S(2)}) async-start(), calls=%async_computation.7 | async-start | bytes 7864320 | tf_op jit(solution)/shard_map/reduce_scatter | solution.py:128
  167.9 6.8 %copy-start.9 = (bf16[20,4,8,128]{3,2,1,0:T(8,128)(2,1)S(1)}, bf16[20,4,8,128]{3,2,1,0:T(8,128)(2,1)}, u32[]{:S(2)}) copy-start(bf16[20,4,8,128]{3,2,1,0:T(8,128)(2,1)} %fusion.16) | copy-start | bytes 491524
  167.9 7.8 %copy-start.4 = (f32[160,512]{1,0:T(8,128)S(1)}, f32[160,512]{1,0:T(8,128)}, u32[]{:S(2)}) copy-start(f32[160,512]{1,0:T(8,128)} %fusion.103) | copy-start | bytes 983044
  167.9 7.8 %copy-start.5 = (f32[160,512]{1,0:T(8,128)S(1)}, f32[160,512]{1,0:T(8,128)}, u32[]{:S(2)}) copy-start(f32[160,512]{1,0:T(8,128)} %fusion.102) | copy-start | bytes 983044
  167.9 7.8 %copy-start.6 = (f32[4,160,160]{1,2,0:T(8,128)S(1)}, f32[4,160,160]{1,2,0:T(8,128)}, u32[]{:S(2)}) copy-start(f32[4,160,160]{1,2,0:T(8,128)} %fusion.28) | copy-start | bytes 1228804
  167.9 225.9 %reduce-scatter.7.cloned.1.call-start = ((), (), s32[]{:S(2)}) async-start(), calls=%async_computation.4 | async-start | bytes 7864320 | tf_op jit(solution)/shard_map/reduce_scatter | solution.py:119
  174.0 0.7 copy-start.10
  184.0 323.8 %reduce-scatter.9.cloned.1.call-start = ((), (), s32[]{:S(2)}) async-start(), calls=%async_computation.5 | async-start | bytes 7864320 | tf_op jit(solution)/shard_map/reduce_scatter | solution.py:122
  192.1 0.9 copy-start.11
  192.1 429.8 %reduce-scatter.11.cloned.1.call-start = ((), (), s32[]{:S(2)}) async-start(), calls=%async_computation.6 | async-start | bytes 7864320 | tf_op jit(solution)/shard_map/reduce_scatter | solution.py:125
  197.7 1.1 copy-start.3
  197.7 1.1 copy-start.16
  197.7 1.1 copy-start.17
  197.7 424.2 %copy-start.1 = (bf16[1,128,6144]{2,1,0:T(8,128)(2,1)S(1)}, bf16[1,128,6144]{2,1,0:T(8,128)(2,1)}, u32[]{:S(2)}) copy-start(bf16[1,128,6144]{2,1,0:T(8,128)(2,1)} %param.10) | copy-start | bytes 4718596
Sparse Core Ops, SparseCore 0:
  11.6 30.2 all-gather.4
  127.9 29.8 all-gather.6
  168.0 111.7 reduce-scatter.12
  282.6 111.2 reduce-scatter.6
  396.6 111.2 reduce-scatter.8
  510.6 111.2 reduce-scatter.10
where the time goes:
time: 632 us; the launch traced here: 629 us
  waiting for transfers between devices  418 us (66%)
  blocking collectives  88.4 us (14%)
  matrix products  66.3 us (10%)
  local copies, waits for them, and re-layouts  27.4 us (4%)
  between operations  16.4 us (3%)
  starting transfers between devices  6.55 us (1%)
    reduce_scatter x1, waiting for transfers between devices, body(): lax.psum_scatter(value_term.astype(jnp.bfloat16), 'dp', scatter_dimension...  114 us
    reduce_scatter x1, waiting for transfers between devices, body(): lax.psum_scatter(key_term.astype(jnp.bfloat16), 'dp', scatter_dimension=0...  114 us
    reduce_scatter x1, waiting for transfers between devices, body(): lax.psum_scatter(query_term.astype(jnp.bfloat16), 'dp', scatter_dimension...  114 us
    psum x1, blocking collectives, body(): grad_router = lax.psum(router_part, ('dp', 'ctx'))  47.8 us
    unnamed x2, blocking collectives  40.6 us
    all_gather x1, waiting for transfers between devices, body(): lax.all_gather(delta, 'ctx', axis=0, tiled=True)  30 us
    reduce_scatter x1, waiting for transfers between devices, body(): lax.psum_scatter(out_term.astype(jnp.bfloat16), 'dp', scatter_dimension=1...  28.5 us
    unnamed x49, local copies, waits for them, and re-layouts  21.9 us
  transfers between devices with their start and end apart: 8, of which 6 were waited for; matrix products, arithmetic and copies ran while one was open for 6% of the time, Pallas kernels for 0%

commit v1 on v0

--- a/solution.py
+++ b/solution.py
@@ -9,8 +9,6 @@
 
 
 HIGHEST_PRECISION = lax.Precision.HIGHEST
-ROW_CONTRACT = (((0,), (0,)), ((), ()))
-COLUMN_CONTRACT = (((1,), (1,)), ((), ()))
 
 
 def head_norm(values, width):
@@ -27,8 +25,18 @@
     return lax.optimization_barrier(part.astype(jnp.bfloat16)).astype(jnp.float32)
 
 
-def body(tokens, cotangent, w_router, w_query, w_key, w_value, w_out, chosen, counts):
+def to_bf16_grid(values):
+    return lax.reduce_precision(values, exponent_bits=8, mantissa_bits=7)
+
+
+def summed_parts(left, right):
+    parts = jnp.einsum("bsm,bsn->bmn", left, right, preferred_element_type=jnp.float32)
+    return jnp.sum(to_bf16_grid(parts), axis=0).astype(jnp.bfloat16)
+
+
+def body(n_dp, n_ctx, tokens, cotangent, w_router, w_query, w_key, w_value, w_out, chosen, counts):
     length = tokens.shape[1]
+    width = tokens.shape[2]
     capacity = chosen.shape[1]
     inner = w_query.shape[1]
     heads_here = inner // HDIM
@@ -47,11 +55,15 @@
         jnp.bfloat16
     )
     delta = (weights[:, None] * rows_back).astype(jnp.bfloat16)
-    all_normed, all_delta, all_present = (
-        lax.all_gather(normed, "ctx", axis=0, tiled=True),
-        lax.all_gather(delta, "ctx", axis=0, tiled=True),
-        lax.all_gather(present.astype(jnp.bfloat16), "ctx", axis=0, tiled=True),
+    flag_row = jnp.zeros((1, width), jnp.bfloat16).at[0, :capacity].set(
+        present.astype(jnp.bfloat16)
     )
+    packed = lax.all_gather(
+        jnp.concatenate([normed, flag_row], axis=0), "ctx", axis=0, tiled=False
+    )
+    all_normed = packed[:, :capacity].reshape(n_ctx * capacity, width)
+    all_present = packed[:, capacity, :capacity].reshape(n_ctx * capacity)
+    all_delta = lax.all_gather(delta, "ctx", axis=0, tiled=True)
     slots = all_normed.shape[0]
     query_raw = jnp.dot(all_normed, w_query, preferred_element_type=jnp.float32)
     key_raw = jnp.dot(all_normed, w_key, preferred_element_type=jnp.float32)
@@ -83,12 +95,9 @@
     layer_out = (tokens[0].astype(jnp.float32) + spread).astype(jnp.bfloat16)[None]
     gate_back = jnp.sum(rows_back * update, axis=-1) * weights * (1.0 - weights)
     router_part = jnp.dot(gate_back, rows, precision=HIGHEST_PRECISION)
-    grad_router = lax.psum(router_part, ("dp", "ctx"))
-    out_term = rounded_term(
-        lax.dot_general(mixed, all_delta, ROW_CONTRACT, preferred_element_type=jnp.float32)
-    )
+    grad_router = jnp.sum(lax.all_gather(router_part, ("dp", "ctx"), axis=0), axis=0)
     mixed_back = lax.dot_general(
-        all_delta, w_out, COLUMN_CONTRACT, preferred_element_type=jnp.float32
+        all_delta, w_out, (((1,), (1,)), ((), ())), preferred_element_type=jnp.float32
     )
     mixed_back = mixed_back.astype(jnp.bfloat16).reshape(slots, heads_here, HDIM)
     attend_back = jnp.einsum(
@@ -106,40 +115,29 @@
         norm_back(qhat_back, query_hat, query_scale).astype(jnp.bfloat16).reshape(slots, inner)
     )
     key_back = norm_back(khat_back, key_hat, key_scale).astype(jnp.bfloat16).reshape(slots, inner)
-    query_term = rounded_term(
-        lax.dot_general(all_normed, query_back, ROW_CONTRACT, preferred_element_type=jnp.float32)
+    block = width // n_dp
+    factors = lax.all_gather(
+        jnp.stack([query_back, key_back, value_back, mixed]), "dp", axis=0, tiled=False
     )
-    key_term = rounded_term(
-        lax.dot_general(all_normed, key_back, ROW_CONTRACT, preferred_element_type=jnp.float32)
+    blocks = lax.all_to_all(
+        jnp.stack([all_normed, all_delta]).reshape(2, slots, n_dp, block).transpose(2, 0, 1, 3),
+        "dp",
+        0,
+        0,
+        tiled=True,
     )
-    value_term = rounded_term(
-        lax.dot_general(all_normed, value_back, ROW_CONTRACT, preferred_element_type=jnp.float32)
-    )
-    grad_query, grad_key, grad_value, grad_out = (
-        lax.psum_scatter(
-            query_term.astype(jnp.bfloat16), "dp", scatter_dimension=0, tiled=True
-        ).astype(jnp.float32),
-        lax.psum_scatter(
-            key_term.astype(jnp.bfloat16), "dp", scatter_dimension=0, tiled=True
-        ).astype(jnp.float32),
-        lax.psum_scatter(
-            value_term.astype(jnp.bfloat16), "dp", scatter_dimension=0, tiled=True
-        ).astype(jnp.float32),
-        lax.psum_scatter(
-            out_term.astype(jnp.bfloat16), "dp", scatter_dimension=1, tiled=True
-        ).astype(jnp.float32),
-    )
-    return (
-        layer_out,
-        grad_query.astype(jnp.bfloat16),
-        grad_key.astype(jnp.bfloat16),
-        grad_value.astype(jnp.bfloat16),
-        grad_out.astype(jnp.bfloat16),
-        grad_router,
-    )
+    normed_blocks = blocks[:, 0]
+    delta_blocks = blocks[:, 1]
+    grad_query = summed_parts(normed_blocks, factors[:, 0])
+    grad_key = summed_parts(normed_blocks, factors[:, 1])
+    grad_value = summed_parts(normed_blocks, factors[:, 2])
+    grad_out = summed_parts(factors[:, 3], delta_blocks)
+    return (layer_out, grad_query, grad_key, grad_value, grad_out, grad_router)
 
 
 def solution(mesh):
+    n_dp = mesh.shape["dp"]
+    n_ctx = mesh.shape["ctx"]
     in_specs = (
         P("dp", "ctx", None),
         P("dp", "ctx", None),
@@ -159,4 +157,8 @@
         P("ctx", "dp"),
         P(),
     )
-    return jax.shard_map(body, mesh=mesh, in_specs=in_specs, out_specs=out_specs, check_vma=False)
+
+    def run(*args):
+        return body(n_dp, n_ctx, *args)
+
+    return jax.shard_map(run, mesh=mesh, in_specs=in_specs, out_specs=out_specs, check_vma=False)

time: 632 us -> 364 us (0.58)
  waiting for transfers between devices: 418 us -> 30.2 us
  blocking collectives: 88.4 us -> 171 us
  local copies, waits for them, and re-layouts: 27.4 us -> 50.2 us
  other arithmetic: 6.04 us -> 13.7 us
    reduce_scatter x4 -> x0, waiting for transfers between devices: 371 us -> none  [the longest x1 114 us: body(): lax.psum_scatter(value_term.astype(jnp.bfloat16), 'dp', scatter_dimension...]
    all_gather x0 -> x1, blocking collectives: none -> 142 us  [body(): lax.all_gather(router_part, ('dp', 'ctx'), axis=0)]
    psum x1 -> x0, blocking collectives: 47.8 us -> none  [body(): grad_router = lax.psum(router_part, ('dp', 'ctx'))]
    dot_general x0 -> x3, local copies, waits for them, and re-layouts: none -> 26 us  [the longest x1 8.73 us: body(): key_raw = jnp.dot(all_normed, w_key, preferred_element_type=jnp.float32)]
    all_gather x2 -> x3, waiting for transfers between devices: 46.9 us -> 29.8 us  [the longest x1 25.4 us: body(): all_delta = lax.all_gather(delta, 'ctx', axis=0, tiled=True)]
    unnamed x49 -> x36, local copies, waits for them, and re-layouts: 21.9 us -> 8.05 us
    unnamed x2 -> x1, blocking collectives: 40.6 us -> 28.9 us
    another operation x0 -> x6, local copies, waits for them, and re-layouts: none -> 9.02 us  [the longest x2 8.75 us: body(): jnp.stack([all_normed, all_delta]).reshape(2, slots, n_dp, block)]
  transfers between devices with their start and end apart: 8 -> 6, of which waited for: 6 -> 4; matrix products, arithmetic and copies ran while one was open for 6% -> 13% of each run, Pallas kernels for 0% -> 0%
where the time goes in v1:
time: 364 us; the launch traced here: 356 us
  blocking collectives  171 us (47%)
  matrix products  64.3 us (18%)
  local copies, waits for them, and re-layouts  50.2 us (14%)
  waiting for transfers between devices  30.2 us (8%)
  between operations  15.4 us (4%)
  other arithmetic  13.7 us (4%)
  starting transfers between devices  11.4 us (3%)
    all_gather x1, blocking collectives, body(): lax.all_gather(router_part, ('dp', 'ctx'), axis=0)  142 us
    unnamed x1, blocking collectives  28.9 us
    all_gather x1, waiting for transfers between devices, body(): all_delta = lax.all_gather(delta, 'ctx', axis=0, tiled=True)  25.4 us
    dot_general x4, matrix products, summed_parts(): jnp.einsum('bsm,bsn->bmn', left, right, preferred_element_type=jnp.float32)  20.3 us
    another operation x2, local copies, waits for them, and re-layouts, body(): jnp.stack([all_normed, all_delta]).reshape(2, slots, n_dp, block)  8.75 us
    dot_general x1, local copies, waits for them, and re-layouts, body(): key_raw = jnp.dot(all_normed, w_key, preferred_element_type=jnp.float32)  8.73 us
    dot_general x1, local copies, waits for them, and re-layouts, body(): query_raw = jnp.dot(all_normed, w_query, preferred_element_type=jnp.float32)  8.7 us
    dot_general x1, local copies, waits for them, and re-layouts, body(): value_raw = jnp.dot(all_normed, w_value, preferred_element_type=jnp.float32)  8.57 us
  transfers between devices with their start and end apart: 6, of which 4 were waited for; matrix products, arithmetic and copies ran while one was open for 13% of the time, Pallas kernels for 0%

profile of v1, /device:TPU:2, one launch (start us, length us, event | category | flops | bytes accessed | tf_op | source)
XLA Modules:
  0.0 356.5 jit_solution(6842864941701883184)
XLA Ops:
  7.2 0.6 compare_reduce_fusion.1
  8.5 0.7 compare_and_fusion
  9.2 1.9 multiply_reduce_fusion.1
  11.1 0.1 multiply_convert_fusion.1
  11.2 0.7 broadcast_select_fusion
  11.9 0.7 fusion.31
  12.7 0.0 all-gather.13.cloned.1.call-start
  12.7 8.7 %copy.83 = bf16[512,6144]{1,0:T(8,128)(2,1)} copy(bf16[512,6144]{0,1:T(8,128)(2,1)} %bitcast.123) | data formatting | bytes 12582912 | tf_op jit(solution)/shard_map/dot_general | solution.py:68
  21.4 8.7 %copy.84 = bf16[512,6144]{1,0:T(8,128)(2,1)} copy(bf16[512,6144]{0,1:T(8,128)(2,1)} %bitcast.124) | data formatting | bytes 12582912 | tf_op jit(solution)/shard_map/dot_general | solution.py:69
  30.2 8.6 %copy.82 = bf16[512,6144]{1,0:T(8,128)(2,1)} copy(bf16[512,6144]{0,1:T(8,128)(2,1)} %bitcast.125) | data formatting | bytes 12582912 | tf_op jit(solution)/shard_map/dot_general | solution.py:70
  38.7 4.3 %all-gather.11.cloned.1.call-done = bf16[8,21,6144]{2,1,0:T(8,128)(2,1)} async-done(((bf16[1,21,6144]{2,1,0:T(8,128)(2,1)}), bf16[8,21,6144]{2,1,0:T(8,128)(2,1)}) %all-gather.11.cloned.1.call-update) | async-done | bytes 2064400 | tf_op jit(solution)/shard_map/all_gather | solution.py:61
  43.1 4.0 %reshape.167 = bf16[160,6144,1]{1,0,2:T(8,128)(2,1)} reshape(bf16[8,20,6144]{2,1,0:T(8,128)(2,1)} %bitcast.121) | data formatting | bytes 3932160 | tf_op jit(solution)/shard_map/reshape | solution.py:64
  47.0 5.9 %multiply_reduce_fusion.5 = (f32[160,4]{0,1:T(4,128)S(1)}, f32[160,4,128]{2,0,1:T(8,128)S(1)}) fusion(bf16[160,6144,1]{1,0,2:T(8,128)(2,1)} %reshape.167, bf16[4,128,6144]{2,1,0:T(8,128)(2,1)} %bitcast.128), kind=kOutput, calls=%fused_computation.61 | convolution fusion | flops 1006796160 | bytes 8587776 | tf_op jit(solution)/shard_map/dot_general | solution.py:68
  53.0 5.4 %multiply_reduce_fusion.4 = (f32[160,4]{0,1:T(4,128)S(1)}, f32[160,4,128]{2,0,1:T(8,128)S(1)}) fusion(bf16[160,6144,1]{1,0,2:T(8,128)(2,1)S(1)} %copy-done.4, bf16[4,128,6144]{2,1,0:T(8,128)(2,1)} %bitcast.127), kind=kOutput, calls=%fused_computation.60 | convolution fusion | flops 1006796160 | bytes 8587776 | tf_op jit(solution)/shard_map/dot_general | solution.py:69
  58.4 0.7 compare_reduce_fusion
  59.1 0.1 gt.16
  59.2 0.1 fusion.42
  59.3 6.3 %convolution_convert_fusion.4 = bf16[160,4,128]{2,0,1:T(8,128)(2,1)} fusion(bf16[160,6144,1]{1,0,2:T(8,128)(2,1)} %reshape.167, bf16[4,128,6144]{2,1,0:T(8,128)(2,1)} %bitcast.126), kind=kOutput, calls=%fused_computation.28 | convolution fusion | flops 1006714880 | bytes 8421376 | tf_op jit(solution)/shard_map/dot_general | solution.py:70
  65.6 0.4 fusion.12
  66.0 1.5 convolution_convert_fusion.2
  67.5 5.3 %convolution_convert_fusion = bf16[160,6144]{1,0:T(8,128)(2,1)} fusion(bf16[512,6144]{1,0:T(8,128)(2,1)} %param.17, bf16[4,128,160]{1,2,0:T(8,128)(2,1)S(1)} %convolution_convert_fusion.2), kind=kOutput, calls=%fused_computation.6 | convolution fusion | flops 1007616000 | bytes 8421376 | tf_op jit(solution)/shard_map/dot_general | solution.py:86
  72.9 28.9 %fusion = bf16[24,6144]{1,0:T(8,128)(2,1)S(1)} fusion(bf16[160,6144]{1,0:T(8,128)(2,1)} %convolution_convert_fusion), kind=kCustom, calls=%all-reduce-scatter | all-reduce-scatter fusion | flops 1179649 | bytes 2261504
  101.7 1.9 collective-permute-start
  103.7 4.4 %collective-permute-start.1 = (bf16[4,6144]{1,0:T(4,128)(2,1)S(1)}, bf16[4,6144]{1,0:T(4,128)(2,1)S(1)}, u32[]{:S(2)}, u32[]{:S(2)}) collective-permute-start(bf16[4,6144]{1,0:T(4,128)(2,1)S(1)} %slice.56), channel_id=1, source_target_pairs={{0,2},{1,3},{2,4},{3,5},{4,6},{5,7},{8,10},{9,11},{10,12},{11,13},... | collective-permute-start | bytes 147464
  108.1 0.7 fusion.19
  108.8 0.6 dynamic-slice.11
  110.0 0.2 collective-permute-done.1
  110.3 0.1 collective-permute-done
  110.4 3.3 concatenate.7
  113.8 1.2 fusion.24
  115.0 4.4 %stack.11 = bf16[1,160,4,1536]{3,2,1,0:T(4,128)(2,1)} reshape(bf16[8,20,6144]{2,1,0:T(8,128)(2,1)} %bitcast.122) | data formatting | bytes 3932160 | tf_op jit(solution)/shard_map/stack | solution.py:123
  119.4 0.1 copy.65
  119.5 0.1 stack_reshape.16
  119.6 0.9 fusion.27
  120.5 25.4 %all-gather.13.cloned.1.call-done = bf16[8,20,6144]{2,1,0:T(8,128)(2,1)} async-done(((bf16[1,20,6144]{2,1,0:T(8,128)(2,1)}), bf16[8,20,6144]{2,1,0:T(8,128)(2,1)}) %all-gather.13.cloned.1.call-update) | async-done | bytes 1966096 | tf_op jit(solution)/shard_map/all_gather | solution.py:66
  146.0 4.0 %reshape.162 = bf16[160,6144]{1,0:T(8,128)(2,1)} reshape(bf16[8,20,6144]{2,1,0:T(8,128)(2,1)} %all-gather.13.cloned.1.call-done) | data formatting | bytes 3932160
  150.0 5.6 %fusion.15 = bf16[20,4,8,128]{3,2,1,0:T(8,128)(2,1)S(1)} fusion(bf16[160,6144]{1,0:T(8,128)(2,1)} %reshape.162, bf16[512,6144]{1,0:T(8,128)(2,1)} %param.17), kind=kOutput, calls=%fused_computation.30 | convolution fusion | flops 1006714880 | bytes 8421376 | tf_op jit(solution)/shard_map/dot_general | solution.py:99
  155.6 4.4 %stack.12 = bf16[1,160,4,1536]{3,2,1,0:T(4,128)(2,1)} reshape(bf16[8,20,6144]{2,1,0:T(8,128)(2,1)} %all-gather.13.cloned.1.call-done) | data formatting | bytes 3932160 | tf_op jit(solution)/shard_map/stack | solution.py:123
  159.9 5.1 %maximum_bitcast_fusion = bf16[4,2,160,1536]{3,0,2,1:T(4,128)(2,1)S(1)} fusion(bf16[1,160,4,1536]{3,2,1,0:T(4,128)(2,1)} %stack.12, bf16[1,160,4,1536]{3,2,1,0:T(4,128)(2,1)} %stack.11), kind=kLoop, calls=%fused_computation.9 | loop fusion | flops 1966080 | bytes 7864320 | tf_op jit(solution)/shard_map/transpose | solution.py:123
  165.0 2.6 copy.66
  167.7 4.9 %all-to-all-start = ((bf16[4,2,160,1536]{3,2,1,0:T(8,128)(2,1)}), bf16[4,2,160,1536]{3,2,1,0:T(8,128)(2,1)}, u32[]{:S(2)}, u32[]{:S(2)}) async-start(bf16[4,2,160,1536]{3,2,1,0:T(8,128)(2,1)} %copy.66), calls=%async_computation | async-start | bytes 7864320 | tf_op jit(solution)/shard_map/all_to_all | solution.py:122
  172.6 0.0 all-gather.9.cloned.1.call-start
  172.7 0.2 fusion.38
  172.9 2.6 multiply_reduce_fusion.3
  175.5 1.2 multiply_convert_fusion.3
  176.8 0.1 copy.70
  176.9 0.1 stack_reshape.13
  176.9 2.4 multiply_reduce_fusion.2
  179.3 1.2 multiply_convert_fusion.2
  180.5 0.1 copy.71
  180.6 0.1 stack_reshape.14
  180.7 0.3 fusion.14
  181.0 0.1 copy.73
  181.1 0.1 stack_reshape.15
  181.2 0.9 pad_maximum_fusion
  182.1 0.4 fusion.57
  182.5 142.4 %all-gather.2 = f32[196608]{0:T(1024)S(1)} all-gather(f32[6144]{0:T(1024)S(1)} %bitcast.130), channel_id=4, replica_groups=mesh['dp'=4,'ctx'=8] {'dp','ctx'}, dimensions={0}, use_global_device_ids=true | all-gather | bytes 811008 | tf_op jit(solution)/shard_map/all_gather | solution.py:98
  324.9 0.1 reshape.158
  325.1 0.7 reduce_sum.129
  325.7 3.8 %fusion.3 = bf16[1,128,6144]{2,1,0:T(8,128)(2,1)} fusion(bf16[1,128,6144]{2,1,0:T(8,128)(2,1)S(1)} %copy-done.2, f32[20]{0:T(128)S(1)} %fusion.19, bf16[52,6144]{1,0:T(8,128)(2,1)} %copy-done.3, u32[]{:S(6)} %subtract, s32[20]{0:T(128)S(1)} %get-tuple-element.19, pred[20]{0:T(512)(128)(4,1)S(1)} %get-tuple-element.18), kind=kOutput, calls=%fused_computation.8 | convolution fusion | flops 191353856 | bytes 3440824 | tf_op jit(solution)/shard_map/dot_general | solution.py:94
  329.6 5.3 %reduce-precision_reduce_fusion = bf16[512,1536]{1,0:T(8,128)(2,1)} fusion(bf16[4,2,160,1536]{3,2,1,0:T(8,128)(2,1)} %all-to-all-done, bf16[4,4,160,512]{3,2,1,0:T(8,128)(2,1)} %bitcast.132), kind=kOutput, calls=%fused_computation.1 | convolution fusion | flops 1012137984 | bytes 4194304 | tf_op jit(solution)/shard_map/bsm,bsn->bmn/dot_general | solution.py:33
  334.8 5.0 %reduce-precision_reduce_fusion.1 = bf16[1536,512]{1,0:T(8,128)(2,1)} fusion(bf16[4,2,160,1536]{3,2,1,0:T(8,128)(2,1)} %all-to-all-done, bf16[4,4,160,512]{3,2,1,0:T(8,128)(2,1)S(1)} %bitcast.133), kind=kOutput, calls=%fused_computation.2 | convolution fusion | flops 1012137984 | bytes 4194304 | tf_op jit(solution)/shard_map/bsm,bsn->bmn/dot_general | solution.py:33
  339.8 5.0 %reduce-precision_reduce_fusion.2 = bf16[1536,512]{1,0:T(8,128)(2,1)} fusion(bf16[4,2,160,1536]{3,2,1,0:T(8,128)(2,1)} %all-to-all-done, bf16[4,4,160,512]{3,2,1,0:T(8,128)(2,1)S(1)} %bitcast.134), kind=kOutput, calls=%fused_computation.3 | convolution fusion | flops 1012137984 | bytes 4194304 | tf_op jit(solution)/shard_map/bsm,bsn->bmn/dot_general | solution.py:33
  344.8 5.1 %reduce-precision_reduce_fusion.3 = bf16[1536,512]{1,0:T(8,128)(2,1)} fusion(bf16[4,2,160,1536]{3,2,1,0:T(8,128)(2,1)} %all-to-all-done, bf16[4,4,160,512]{3,2,1,0:T(8,128)(2,1)S(1)} %bitcast.135), kind=kOutput, calls=%fused_computation.4 | convolution fusion | flops 1012137984 | bytes 4194304 | tf_op jit(solution)/shard_map/bsm,bsn->bmn/dot_general | solution.py:33
  (43 shorter events, 0.2 us)
Async XLA Ops:
  7.2 106.6 %copy-start = (bf16[1,128,6144]{2,1,0:T(8,128)(2,1)S(1)}, bf16[1,128,6144]{2,1,0:T(8,128)(2,1)}, u32[]{:S(2)}) copy-start(bf16[1,128,6144]{2,1,0:T(8,128)(2,1)} %param.12) | copy-start | bytes 4718596
  7.2 4.0 %copy-start.13 = (s32[1,20]{1,0:T(1,128)S(1)}, s32[1,20]{1,0:T(1,128)}, u32[]{:S(2)}) copy-start(s32[1,20]{1,0:T(1,128)} %param.18) | copy-start | bytes 244
  7.2 35.9 %all-gather.11.cloned.1.call-start = ((), (), s32[]{:S(2)}) async-start(), calls=%async_computation.2 | async-start | bytes 2654208 | tf_op jit(solution)/shard_map/all_gather | solution.py:61
  12.7 133.3 %all-gather.13.cloned.1.call-start = ((), (), s32[]{:S(2)}) async-start(), calls=%async_computation.3 | async-start | bytes 2654208 | tf_op jit(solution)/shard_map/all_gather | solution.py:66
  47.0 6.0 %copy-start.4 = (bf16[160,6144,1]{1,0,2:T(8,128)(2,1)S(1)}, bf16[160,6144,1]{1,0,2:T(8,128)(2,1)}, u32[]{:S(2)}) copy-start(bf16[160,6144,1]{1,0,2:T(8,128)(2,1)} %reshape.167) | copy-start | bytes 5898244
  53.0 12.7 %copy-start.5 = (f32[160,4,128]{2,0,1:T(8,128)}, f32[160,4,128]{2,0,1:T(8,128)S(1)}, u32[]{:S(2)}) copy-start(f32[160,4,128]{2,0,1:T(8,128)S(1)} %get-tuple-element.25) | copy-start | bytes 983044
  66.0 1.5 copy-start.9
  67.5 5.4 %copy-start.7 = (bf16[4,128,160]{1,2,0:T(8,128)(2,1)}, bf16[4,128,160]{1,2,0:T(8,128)(2,1)S(1)}, u32[]{:S(2)}) copy-start(bf16[4,128,160]{1,2,0:T(8,128)(2,1)S(1)} %convolution_convert_fusion.2) | copy-start | bytes 491524
  67.5 40.6 %copy-start.12 = (f32[6144]{0:T(1024)S(1)}, f32[6144]{0:T(1024)}, u32[]{:S(2)}) copy-start(f32[6144]{0:T(1024)} %param.13) | copy-start | bytes 73732
  72.9 35.9 %copy-start.14 = (u32[32]{0:T(128)S(1)}, u32[32]{0:T(128)}, u32[]{:S(2)}) copy-start(u32[32]{0:T(128)} %constant.68) | copy-start | bytes 388
  101.7 8.7 %collective-permute-start = (bf16[24,6144]{1,0:T(8,128)(2,1)S(1)}, bf16[24,6144]{1,0:T(8,128)(2,1)}, u32[]{:S(2)}, u32[]{:S(2)}) collective-permute-start(bf16[24,6144]{1,0:T(8,128)(2,1)S(1)} %fusion), channel_id=1, source_target_pairs={{0,1},{1,2},{2,3},{3,4},{4,5},{5,6},{6,7},{8,9},{9,10},{10,11},{11... | collective-permute-start | bytes 884744
  103.7 6.6 %collective-permute-start.1 = (bf16[4,6144]{1,0:T(4,128)(2,1)S(1)}, bf16[4,6144]{1,0:T(4,128)(2,1)S(1)}, u32[]{:S(2)}, u32[]{:S(2)}) collective-permute-start(bf16[4,6144]{1,0:T(4,128)(2,1)S(1)} %slice.56), channel_id=1, source_target_pairs={{0,2},{1,3},{2,4},{3,5},{4,6},{5,7},{8,10},{9,11},{10,12},{11,13},... | collective-permute-start | bytes 147464
  113.8 5.7 %copy-start.3 = (bf16[52,6144]{1,0:T(8,128)(2,1)}, bf16[52,6144]{1,0:T(8,128)(2,1)S(1)}, u32[]{:S(2)}) copy-start(bf16[52,6144]{1,0:T(8,128)(2,1)S(1)} %concatenate.7) | copy-start | bytes 1916932
  115.0 4.4 %copy-start.8 = (bf16[4,128,160]{1,2,0:T(8,128)(2,1)S(1)}, bf16[4,128,160]{1,2,0:T(8,128)(2,1)}, u32[]{:S(2)}) copy-start(bf16[4,128,160]{1,2,0:T(8,128)(2,1)} %copy-done.7) | copy-start | bytes 491524
  115.0 4.6 %copy-start.10 = (f32[4,160,160]{1,2,0:T(8,128)S(1)}, f32[4,160,160]{1,2,0:T(8,128)}, u32[]{:S(2)}) copy-start(f32[4,160,160]{1,2,0:T(8,128)} %copy-done.9) | copy-start | bytes 1228804
  167.7 5.0 %copy-start.11 = (bf16[160,4,128]{2,0,1:T(8,128)(2,1)S(1)}, bf16[160,4,128]{2,0,1:T(8,128)(2,1)}, u32[]{:S(2)}) copy-start(bf16[160,4,128]{2,0,1:T(8,128)(2,1)} %convolution_convert_fusion.4) | copy-start | bytes 491524
  167.7 5.3 %copy-start.6 = (f32[160,4,128]{2,0,1:T(8,128)S(1)}, f32[160,4,128]{2,0,1:T(8,128)}, u32[]{:S(2)}) copy-start(f32[160,4,128]{2,0,1:T(8,128)} %copy-done.5) | copy-start | bytes 983044
  167.7 161.9 %all-to-all-start = ((bf16[4,2,160,1536]{3,2,1,0:T(8,128)(2,1)}), bf16[4,2,160,1536]{3,2,1,0:T(8,128)(2,1)}, u32[]{:S(2)}, u32[]{:S(2)}) async-start(bf16[4,2,160,1536]{3,2,1,0:T(8,128)(2,1)} %copy.66), calls=%async_computation | async-start | bytes 7864320 | tf_op jit(solution)/shard_map/all_to_all | solution.py:122
  172.6 157.0 %all-gather.9.cloned.1.call-start = ((), (), s32[]{:S(2)}) async-start(), calls=%async_computation.1 | async-start | bytes 3276800 | tf_op jit(solution)/shard_map/all_gather | solution.py:119
  181.2 144.6 %copy-start.2 = (bf16[1,128,6144]{2,1,0:T(8,128)(2,1)S(1)}, bf16[1,128,6144]{2,1,0:T(8,128)(2,1)}, u32[]{:S(2)}) copy-start(bf16[1,128,6144]{2,1,0:T(8,128)(2,1)} %param.11) | copy-start | bytes 4718596
  329.6 5.3 %copy-start.15 = (bf16[16,160,512]{2,1,0:T(8,128)(2,1)S(1)}, bf16[16,160,512]{2,1,0:T(8,128)(2,1)}, u32[]{:S(2)}) copy-start(bf16[16,160,512]{2,1,0:T(8,128)(2,1)} %all-gather.9.cloned.1.call-done) | copy-start | bytes 7864324
  344.8 5.1 %copy-start.1 = (bf16[1,128,6144]{2,1,0:T(8,128)(2,1)S(1)}, bf16[1,128,6144]{2,1,0:T(8,128)(2,1)}, u32[]{:S(2)}) copy-start(bf16[1,128,6144]{2,1,0:T(8,128)(2,1)} %param.12) | copy-start | bytes 4718596
Sparse Core Ops, SparseCore 0:
  12.8 30.2 all-gather.10
  115.2 30.7 all-gather.12
  182.2 99.1 all-gather.8

commit v2 on v1

--- a/solution.py
+++ b/solution.py
@@ -25,15 +25,6 @@
     return lax.optimization_barrier(part.astype(jnp.bfloat16)).astype(jnp.float32)
 
 
-def to_bf16_grid(values):
-    return lax.reduce_precision(values, exponent_bits=8, mantissa_bits=7)
-
-
-def summed_parts(left, right):
-    parts = jnp.einsum("bsm,bsn->bmn", left, right, preferred_element_type=jnp.float32)
-    return jnp.sum(to_bf16_grid(parts), axis=0).astype(jnp.bfloat16)
-
-
 def body(n_dp, n_ctx, tokens, cotangent, w_router, w_query, w_key, w_value, w_out, chosen, counts):
     length = tokens.shape[1]
     width = tokens.shape[2]
@@ -55,15 +46,15 @@
         jnp.bfloat16
     )
     delta = (weights[:, None] * rows_back).astype(jnp.bfloat16)
-    flag_row = jnp.zeros((1, width), jnp.bfloat16).at[0, :capacity].set(
+    flag_cols = jnp.zeros((capacity, HDIM), jnp.bfloat16).at[:, 0].set(
         present.astype(jnp.bfloat16)
     )
     packed = lax.all_gather(
-        jnp.concatenate([normed, flag_row], axis=0), "ctx", axis=0, tiled=False
+        jnp.concatenate([normed, delta, flag_cols], axis=1), "ctx", axis=0, tiled=True
     )
-    all_normed = packed[:, :capacity].reshape(n_ctx * capacity, width)
-    all_present = packed[:, capacity, :capacity].reshape(n_ctx * capacity)
-    all_delta = lax.all_gather(delta, "ctx", axis=0, tiled=True)
+    all_normed = packed[:, :width]
+    all_delta = packed[:, width : 2 * width]
+    all_present = packed[:, 2 * width]
     slots = all_normed.shape[0]
     query_raw = jnp.dot(all_normed, w_query, preferred_element_type=jnp.float32)
     key_raw = jnp.dot(all_normed, w_key, preferred_element_type=jnp.float32)
@@ -82,20 +73,24 @@
     attend_b = attend.astype(jnp.bfloat16)
     mixed = jnp.einsum("hij,jhd->ihd", attend_b, value_b, preferred_element_type=jnp.float32)
     mixed = mixed.astype(jnp.bfloat16).reshape(slots, inner)
-    update = lax.psum_scatter(
-        rounded_term(jnp.dot(mixed, w_out, preferred_element_type=jnp.float32)).astype(
-            jnp.bfloat16
-        ),
-        "ctx",
-        scatter_dimension=0,
-        tiled=True,
-    ).astype(jnp.float32)
+    contributions = jnp.dot(mixed, w_out, preferred_element_type=jnp.float32).astype(jnp.bfloat16)
+    received = lax.all_to_all(
+        contributions.reshape(n_ctx, capacity, width), "ctx", 0, 0, tiled=True
+    )
+    update = jnp.sum(received.astype(jnp.float32), axis=0)
     scaled = weights[:, None] * update
     spread = jnp.dot(onehot.astype(jnp.float32).T, scaled, precision=HIGHEST_PRECISION)
     layer_out = (tokens[0].astype(jnp.float32) + spread).astype(jnp.bfloat16)[None]
     gate_back = jnp.sum(rows_back * update, axis=-1) * weights * (1.0 - weights)
     router_part = jnp.dot(gate_back, rows, precision=HIGHEST_PRECISION)
-    grad_router = jnp.sum(lax.all_gather(router_part, ("dp", "ctx"), axis=0), axis=0)
+    router_split = jnp.stack(
+        [router_part.astype(jnp.bfloat16), (router_part - router_part.astype(jnp.bfloat16).astype(jnp.float32)).astype(jnp.bfloat16)]
+    )
+    router_group = jnp.sum(
+        lax.all_gather(router_split, "ctx", axis=0, tiled=False).astype(jnp.float32), axis=(0, 1)
+    )
+    router_high = router_group.astype(jnp.bfloat16)
+    router_low = (router_group - router_high.astype(jnp.float32)).astype(jnp.bfloat16)
     mixed_back = lax.dot_general(
         all_delta, w_out, (((1,), (1,)), ((), ())), preferred_element_type=jnp.float32
     )
@@ -115,23 +110,38 @@
         norm_back(qhat_back, query_hat, query_scale).astype(jnp.bfloat16).reshape(slots, inner)
     )
     key_back = norm_back(khat_back, key_hat, key_scale).astype(jnp.bfloat16).reshape(slots, inner)
-    block = width // n_dp
-    factors = lax.all_gather(
-        jnp.stack([query_back, key_back, value_back, mixed]), "dp", axis=0, tiled=False
+    router_rows = width // inner
+    local_factors = jnp.concatenate(
+        [
+            query_back,
+            key_back,
+            value_back,
+            mixed,
+            router_high.reshape(router_rows, inner),
+            router_low.reshape(router_rows, inner),
+        ],
+        axis=0,
     )
-    blocks = lax.all_to_all(
-        jnp.stack([all_normed, all_delta]).reshape(2, slots, n_dp, block).transpose(2, 0, 1, 3),
-        "dp",
-        0,
-        0,
-        tiled=True,
+    factors = lax.all_to_all(
+        jnp.broadcast_to(local_factors[None], (n_dp,) + local_factors.shape), "dp", 0, 0, tiled=True
     )
-    normed_blocks = blocks[:, 0]
-    delta_blocks = blocks[:, 1]
-    grad_query = summed_parts(normed_blocks, factors[:, 0])
-    grad_key = summed_parts(normed_blocks, factors[:, 1])
-    grad_value = summed_parts(normed_blocks, factors[:, 2])
-    grad_out = summed_parts(factors[:, 3], delta_blocks)
+    normed_blocks = lax.all_to_all(all_normed, "dp", 1, 0, tiled=True)
+    delta_blocks = lax.all_to_all(all_delta, "dp", 1, 0, tiled=True)
+
+    def gathered(index):
+        return factors[:, index * slots : (index + 1) * slots].reshape(n_dp * slots, inner)
+
+    def contract(left, right):
+        return lax.dot_general(
+            left, right, (((0,), (0,)), ((), ())), preferred_element_type=jnp.float32
+        ).astype(jnp.bfloat16)
+
+    grad_query = contract(normed_blocks, gathered(0))
+    grad_key = contract(normed_blocks, gathered(1))
+    grad_value = contract(normed_blocks, gathered(2))
+    grad_out = contract(gathered(3), delta_blocks)
+    router_pieces = factors[:, 4 * slots :].astype(jnp.float32).reshape(n_dp, 2, width)
+    grad_router = jnp.sum(router_pieces[:, 0] + router_pieces[:, 1], axis=0)
     return (layer_out, grad_query, grad_key, grad_value, grad_out, grad_router)
 
 

time: 364 us -> 298 us (0.82); the launches traced: 356 us -> 297 us
  blocking collectives: 171 us -> 9.28 us
  waiting for transfers between devices: 30.2 us -> 169 us
  local copies, waits for them, and re-layouts: 50.2 us -> 21 us
  matrix products: 64.3 us -> 52.4 us
  starting transfers between devices: 11.4 us -> 18.7 us
    all_gather x1, blocking collectives: 142 us -> 9.28 us  [body(): lax.all_gather(router_split, 'ctx', axis=0, tiled=False).astype(jnp.float32)]
    all_to_all x1 -> x4, waiting for transfers between devices: 0.01 us -> 129 us  [the longest x1 59.6 us: body(): lax.all_to_all(jnp.broadcast_to(local_factors[None], (n_dp,) + local_fact...]
    unnamed x1 -> x0, blocking collectives: 28.9 us -> none
    dot_general x3 -> x0, local copies, waits for them, and re-layouts: 26 us -> none  [the longest x1 8.73 us: body(): key_raw = jnp.dot(all_normed, w_key, preferred_element_type=jnp.float32)]
    all_to_all x1 -> x4, starting transfers between devices: 4.92 us -> 18.7 us  [the longest x1 4.8 us: body(): lax.all_to_all(contributions.reshape(n_ctx, capacity, width), 'ctx', 0, 0...]
    all_gather x3 -> x1, waiting for transfers between devices: 29.8 us -> 40.5 us  [body(): lax.all_gather(jnp.concatenate([normed, delta, flag_cols], axis=1), 'ctx'...]
    another operation x6 -> x2, local copies, waits for them, and re-layouts: 9.02 us -> 0.03 us  [body(): jnp.stack([router_part.astype(jnp.bfloat16), (router_part - router_part.a...]
    unnamed x2 -> x0, starting transfers between devices: 6.32 us -> none
  transfers between devices with their start and end apart: 6 -> 5, of which waited for: 4 -> 5; matrix products, arithmetic and copies ran while one was open for 13% -> 14% of each run, Pallas kernels for 0% -> 0%
where the time goes in v2:
time: 298 us; the launch traced here: 297 us
  waiting for transfers between devices  169 us (57%)
  matrix products  52.4 us (18%)
  local copies, waits for them, and re-layouts  21 us (7%)
  starting transfers between devices  18.7 us (6%)
  between operations  15.1 us (5%)
  other arithmetic  11.1 us (4%)
  blocking collectives  9.28 us (3%)
    all_to_all x1, waiting for transfers between devices, body(): lax.all_to_all(jnp.broadcast_to(local_factors[None], (n_dp,) + local_fact...  59.6 us
    all_gather x1, waiting for transfers between devices, body(): lax.all_gather(jnp.concatenate([normed, delta, flag_cols], axis=1), 'ctx'...  40.5 us
    all_to_all x1, waiting for transfers between devices, body(): delta_blocks = lax.all_to_all(all_delta, 'dp', 1, 0, tiled=True)  27.6 us
    all_to_all x1, waiting for transfers between devices, body(): normed_blocks = lax.all_to_all(all_normed, 'dp', 1, 0, tiled=True)  26.6 us
    dot_general x4, matrix products, contract(): lax.dot_general(left, right, (((0,), (0,)), ((), ())), preferred_element_...  17.2 us
    all_to_all x1, waiting for transfers between devices, body(): lax.all_to_all(contributions.reshape(n_ctx, capacity, width), 'ctx', 0, 0...  15.1 us
    all_gather x1, blocking collectives, body(): lax.all_gather(router_split, 'ctx', axis=0, tiled=False).astype(jnp.float32)  9.28 us
  transfers between devices with their start and end apart: 5, of which 5 were waited for; matrix products, arithmetic and copies ran while one was open for 14% of the time, Pallas kernels for 0%

profile of v2, /device:TPU:2, one launch (start us, length us, event | category | flops | bytes accessed | tf_op | source)
XLA Modules:
  0.0 297.1 jit_solution(10917437216605401890)
XLA Ops:
  7.2 0.6 compare_reduce_fusion.1
  8.5 0.7 compare_and_fusion
  9.2 1.9 multiply_reduce_fusion.2
  11.1 0.7 fusion.29
  11.8 0.1 multiply_convert_fusion.1
  11.9 0.1 copy.81
  12.0 0.1 copy.82
  12.1 0.4 multiply_convert_fusion
  12.5 0.7 fusion.75
  13.2 0.9 fusion.39
  14.1 40.5 %all-gather.5.cloned.1.call-done = bf16[8,20,12416]{2,1,0:T(8,128)(2,1)} async-done(((bf16[1,20,12416]{2,1,0:T(8,128)(2,1)}), bf16[8,20,12416]{2,1,0:T(8,128)(2,1)}) %all-gather.5.cloned.1.call-update) | async-done | bytes 3973136 | tf_op jit(solution)/shard_map/all_gather | solution.py:52
  54.6 5.2 %reshape.219 = bf16[160,12416]{1,0:T(8,128)(2,1)} reshape(bf16[8,20,12416]{2,1,0:T(8,128)(2,1)} %all-gather.5.cloned.1.call-done) | data formatting | bytes 7946240
  59.8 0.9 compare_reduce_fusion
  60.7 4.6 %fusion.96 = f32[160,512]{1,0:T(8,128)S(1)} fusion(bf16[6144,512]{1,0:T(8,128)(2,1)} %param.14, bf16[160,12416]{1,0:T(8,128)(2,1)} %reshape.219), kind=kOutput, calls=%fused_computation.143 | convolution fusion | flops 1006632960 | bytes 8585216 | tf_op jit(solution)/shard_map/dot_general | solution.py:59
  65.3 0.1 reshape.204
  65.4 0.2 multiply_reduce_fusion.6
  65.6 0.1 copy.83
  65.7 4.6 %fusion.94 = f32[160,512]{1,0:T(8,128)S(1)} fusion(bf16[6144,512]{1,0:T(8,128)(2,1)} %param.15, bf16[160,12416]{1,0:T(8,128)(2,1)} %reshape.219), kind=kOutput, calls=%fused_computation.141 | convolution fusion | flops 1006632960 | bytes 8585216 | tf_op jit(solution)/shard_map/dot_general | solution.py:60
  70.3 0.1 reshape.205
  70.4 0.2 multiply_reduce_fusion.5
  70.7 0.1 copy.85
  70.7 0.1 fusion.57
  70.8 4.6 %fusion.24 = bf16[20,4,8,128]{3,2,1,0:T(8,128)(2,1)S(1)} fusion(bf16[6144,512]{1,0:T(8,128)(2,1)} %param.16, bf16[160,12416]{1,0:T(8,128)(2,1)} %reshape.219), kind=kOutput, calls=%fused_computation.41 | convolution fusion | flops 1006714880 | bytes 8421376 | tf_op jit(solution)/shard_map/dot_general | solution.py:61
  75.4 0.4 fusion.42
  75.9 0.3 fusion.22
  76.2 5.3 %convolution_convert_fusion = bf16[160,6144]{1,0:T(8,128)(2,1)} fusion(bf16[512,6144]{1,0:T(8,128)(2,1)} %param.17, bf16[4,20,8,128]{3,2,1,0:T(8,128)(2,1)S(1)} %fusion.22), kind=kOutput, calls=%fused_computation.2 | convolution fusion | flops 1007616000 | bytes 8421376 | tf_op jit(solution)/shard_map/dot_general | solution.py:76
  81.5 4.0 %reshape.207 = bf16[8,20,6144]{2,1,0:T(8,128)(2,1)} reshape(bf16[160,6144]{1,0:T(8,128)(2,1)} %convolution_convert_fusion) | data formatting | bytes 3932160 | tf_op jit(solution)/shard_map/reshape | solution.py:78
  85.5 4.8 %all-to-all-start = ((bf16[8,20,6144]{2,1,0:T(8,128)(2,1)}), bf16[8,20,6144]{2,1,0:T(8,128)(2,1)}, u32[]{:S(2)}, u32[]{:S(2)}) async-start(bf16[8,20,6144]{2,1,0:T(8,128)(2,1)} %reshape.207), calls=%async_computation | async-start | bytes 4718592 | tf_op jit(solution)/shard_map/all_to_all | solution.py:77
  90.3 3.8 %fusion.99 = (bf16[160,6144]{1,0:T(8,128)(2,1)}, bf16[160,6144]{1,0:T(8,128)(2,1)S(1)}) fusion(bf16[160,12416]{1,0:T(8,128)(2,1)} %reshape.219), kind=kLoop, calls=%fused_computation.146 | loop fusion | bytes 7864320 | tf_op jit(solution)/shard_map/slice | solution.py:56
  94.1 1.4 copy.167
  95.5 5.7 %fusion.25 = bf16[20,4,8,128]{3,2,1,0:T(8,128)(2,1)S(1)} fusion(bf16[512,6144]{1,0:T(8,128)(2,1)} %param.17, bf16[160,12416]{1,0:T(8,128)(2,1)} %reshape.219), kind=kOutput, calls=%fused_computation.42 | convolution fusion | flops 1006714880 | bytes 8421376 | tf_op jit(solution)/shard_map/dot_general | solution.py:94
  101.2 0.7 copy-done.10
  101.8 0.3 fusion.51
  102.1 1.1 multiply_reduce_fusion.3
  103.2 15.1 %all-to-all-done = bf16[8,20,6144]{2,1,0:T(8,128)(2,1)} async-done(((bf16[8,20,6144]{2,1,0:T(8,128)(2,1)}), bf16[8,20,6144]{2,1,0:T(8,128)(2,1)}, u32[]{:S(2)}, u32[]{:S(2)}) %all-to-all-start) | async-done | bytes 1966112 | tf_op jit(solution)/shard_map/all_to_all | solution.py:77
  118.3 4.6 %all-to-all-start.1 = ((bf16[160,4,1536]{2,0,1:T(8,128)(2,1)}), bf16[160,4,1536]{2,0,1:T(8,128)(2,1)}, u32[]{:S(2)}, u32[]{:S(2)}) async-start(bf16[160,4,1536]{2,0,1:T(8,128)(2,1)} %bitcast.184), calls=%async_computation.1 | async-start | bytes 3932160 | tf_op jit(solution)/shard_map/all_to_all | solution.py:128
  123.0 1.1 fusion.23
  124.1 0.7 copy.169
  124.8 0.7 copy.168
  125.5 1.3 multiply_reduce_fusion.4
  126.8 1.2 copy_bitcast_fusion.3
  128.0 1.2 copy_bitcast_fusion.4
  129.3 2.1 convert_reduce_fusion
  131.4 0.2 multiply_reduce_fusion.1
  131.6 0.4 fusion.82
  132.0 0.1 maximum_bitcast_fusion
  132.1 9.3 %all-gather.2 = bf16[8,2,6144]{2,1,0:T(2,128)(2,1)S(1)} all-gather(bf16[1,2,6144]{2,1,0:T(2,128)(2,1)S(1)} %maximum_bitcast_fusion), channel_id=2, replica_groups=mesh['dp'=4,'ctx'=8] {'ctx'}, dimensions={0}, use_global_device_ids=true | all-gather | bytes 221184 | tf_op jit(solution)/shard_map/all_gather | solution.py:90
  141.4 0.2 convert_reduce_fusion.1
  141.6 0.5 concatenate.9
  142.1 26.6 %all-to-all-done.1 = bf16[160,4,1536]{2,0,1:T(8,128)(2,1)} async-done(((bf16[160,4,1536]{2,0,1:T(8,128)(2,1)}), bf16[160,4,1536]{2,0,1:T(8,128)(2,1)}, u32[]{:S(2)}, u32[]{:S(2)}) %all-to-all-start.1) | async-done | bytes 1966112 | tf_op jit(solution)/shard_map/all_to_all | solution.py:128
  168.7 1.7 broadcast_in_dim.19
  170.5 4.7 %all-to-all-start.2 = ((bf16[4,664,512]{2,1,0:T(8,128)(2,1)}), bf16[4,664,512]{2,1,0:T(8,128)(2,1)}, u32[]{:S(2)}, u32[]{:S(2)}) async-start(bf16[4,664,512]{2,1,0:T(8,128)(2,1)} %broadcast_in_dim.19), calls=%async_computation.2 | async-start | bytes 5439488 | tf_op jit(solution)/shard_map/all_to_all | solution.py:125
  175.2 1.5 copy.166
  176.7 59.6 %all-to-all-done.2 = bf16[4,664,512]{2,1,0:T(8,128)(2,1)} async-done(((bf16[4,664,512]{2,1,0:T(8,128)(2,1)}), bf16[4,664,512]{2,1,0:T(8,128)(2,1)}, u32[]{:S(2)}, u32[]{:S(2)}) %all-to-all-start.2) | async-done | bytes 2719776 | tf_op jit(solution)/shard_map/all_to_all | solution.py:125
  236.3 4.6 %all-to-all-start.3 = ((bf16[160,4,1536]{2,0,1:T(8,128)(2,1)}), bf16[160,4,1536]{2,0,1:T(8,128)(2,1)}, u32[]{:S(2)}, u32[]{:S(2)}) async-start(bf16[160,4,1536]{2,0,1:T(8,128)(2,1)} %bitcast.178), calls=%async_computation.3 | async-start | bytes 3932160 | tf_op jit(solution)/shard_map/all_to_all | solution.py:129
  240.9 2.8 fusion.2
  243.7 0.9 slice_convert_fusion
  244.6 0.2 reshape.215
  244.8 0.8 fusion.63
  245.5 4.2 %fusion.5 = bf16[1536,512]{1,0:T(8,128)(2,1)} fusion(bf16[160,4,1536]{2,0,1:T(8,128)(2,1)} %all-to-all-done.1, bf16[4,664,512]{2,1,0:T(8,128)(2,1)} %all-to-all-done.2), kind=kOutput, calls=%fused_computation.12 | convolution fusion | flops 1007419392 | bytes 4194304 | tf_op jit(solution)/shard_map/dot_general | solution.py:135
  249.8 4.2 %fusion.4 = bf16[1536,512]{1,0:T(8,128)(2,1)} fusion(bf16[160,4,1536]{2,0,1:T(8,128)(2,1)} %all-to-all-done.1, bf16[4,664,512]{2,1,0:T(8,128)(2,1)} %all-to-all-done.2), kind=kOutput, calls=%fused_computation.11 | convolution fusion | flops 1007419392 | bytes 4194304 | tf_op jit(solution)/shard_map/dot_general | solution.py:135
  254.0 4.2 %fusion.3 = bf16[1536,512]{1,0:T(8,128)(2,1)} fusion(bf16[160,4,1536]{2,0,1:T(8,128)(2,1)} %all-to-all-done.1, bf16[4,664,512]{2,1,0:T(8,128)(2,1)} %all-to-all-done.2), kind=kOutput, calls=%fused_computation.10 | convolution fusion | flops 1007419392 | bytes 4194304 | tf_op jit(solution)/shard_map/dot_general | solution.py:135
  258.3 27.6 %all-to-all-done.3 = bf16[160,4,1536]{2,0,1:T(8,128)(2,1)} async-done(((bf16[160,4,1536]{2,0,1:T(8,128)(2,1)}), bf16[160,4,1536]{2,0,1:T(8,128)(2,1)}, u32[]{:S(2)}, u32[]{:S(2)}) %all-to-all-start.3) | async-done | bytes 1966112 | tf_op jit(solution)/shard_map/all_to_all | solution.py:129
  285.8 4.4 %fusion.6 = bf16[512,1536]{1,0:T(8,128)(2,1)} fusion(bf16[160,4,1536]{2,0,1:T(8,128)(2,1)} %all-to-all-done.3, bf16[4,664,512]{2,1,0:T(8,128)(2,1)} %all-to-all-done.2), kind=kOutput, calls=%fused_computation.13 | convolution fusion | flops 1007419392 | bytes 4194304 | tf_op jit(solution)/shard_map/dot_general | solution.py:135
  (35 shorter events, 0.2 us)
Async XLA Ops:
  7.2 5.0 %copy-start = (bf16[1,128,6144]{2,1,0:T(8,128)(2,1)S(1)}, bf16[1,128,6144]{2,1,0:T(8,128)(2,1)}, u32[]{:S(2)}) copy-start(bf16[1,128,6144]{2,1,0:T(8,128)(2,1)} %param.12) | copy-start | bytes 4718596
  7.2 3.9 %copy-start.11 = (f32[6144]{0:T(1024)S(1)}, f32[6144]{0:T(1024)}, u32[]{:S(2)}) copy-start(f32[6144]{0:T(1024)} %param.13) | copy-start | bytes 73732
  7.2 47.4 %all-gather.5.cloned.1.call-start = ((), (), s32[]{:S(2)}) async-start(), calls=%async_computation.4 | async-start | bytes 5363712 | tf_op jit(solution)/shard_map/all_gather | solution.py:52
  75.4 0.8 copy-start.8
  85.5 32.9 %all-to-all-start = ((bf16[8,20,6144]{2,1,0:T(8,128)(2,1)}), bf16[8,20,6144]{2,1,0:T(8,128)(2,1)}, u32[]{:S(2)}, u32[]{:S(2)}) async-start(bf16[8,20,6144]{2,1,0:T(8,128)(2,1)} %reshape.207), calls=%async_computation | async-start | bytes 4718592 | tf_op jit(solution)/shard_map/all_to_all | solution.py:77
  95.5 6.3 %copy-start.9 = (bf16[20,4,8,128]{3,2,1,0:T(8,128)(2,1)S(1)}, bf16[20,4,8,128]{3,2,1,0:T(8,128)(2,1)}, u32[]{:S(2)}) copy-start(bf16[20,4,8,128]{3,2,1,0:T(8,128)(2,1)} %copy-done.8) | copy-start | bytes 491524
  101.2 0.7 copy-start.10
  118.3 50.4 %all-to-all-start.1 = ((bf16[160,4,1536]{2,0,1:T(8,128)(2,1)}), bf16[160,4,1536]{2,0,1:T(8,128)(2,1)}, u32[]{:S(2)}, u32[]{:S(2)}) async-start(bf16[160,4,1536]{2,0,1:T(8,128)(2,1)} %bitcast.184), calls=%async_computation.1 | async-start | bytes 3932160 | tf_op jit(solution)/shard_map/all_to_all | solution.py:128
  131.4 10.8 %copy-start.4 = (f32[20,6144]{1,0:T(8,128)}, f32[20,6144]{1,0:T(8,128)S(1)}, u32[]{:S(2)}) copy-start(f32[20,6144]{1,0:T(8,128)S(1)} %convert_reduce_fusion) | copy-start | bytes 1474564
  131.4 10.3 %copy-start.6 = (bf16[4,20,8,128]{3,2,0,1:T(8,128)(2,1)S(1)}, bf16[4,20,8,128]{3,2,0,1:T(8,128)(2,1)}, u32[]{:S(2)}) copy-start(bf16[4,20,8,128]{3,2,0,1:T(8,128)(2,1)} %copy.169) | copy-start | bytes 491524
  131.4 10.3 %copy-start.7 = (bf16[4,20,8,128]{3,2,0,1:T(8,128)(2,1)S(1)}, bf16[4,20,8,128]{3,2,0,1:T(8,128)(2,1)}, u32[]{:S(2)}) copy-start(bf16[4,20,8,128]{3,2,0,1:T(8,128)(2,1)} %copy.168) | copy-start | bytes 491524
  170.5 4.7 %copy-start.2 = (bf16[160,6144]{1,0:T(8,128)(2,1)S(1)}, bf16[160,6144]{1,0:T(8,128)(2,1)}, u32[]{:S(2)}) copy-start(bf16[160,6144]{1,0:T(8,128)(2,1)} %get-tuple-element.24) | copy-start | bytes 5898244
  170.5 65.8 %all-to-all-start.2 = ((bf16[4,664,512]{2,1,0:T(8,128)(2,1)}), bf16[4,664,512]{2,1,0:T(8,128)(2,1)}, u32[]{:S(2)}, u32[]{:S(2)}) async-start(bf16[4,664,512]{2,1,0:T(8,128)(2,1)} %broadcast_in_dim.19), calls=%async_computation.2 | async-start | bytes 5439488 | tf_op jit(solution)/shard_map/all_to_all | solution.py:125
  236.3 4.6 %copy-start.3 = (bf16[1,128,6144]{2,1,0:T(8,128)(2,1)S(1)}, bf16[1,128,6144]{2,1,0:T(8,128)(2,1)}, u32[]{:S(2)}) copy-start(bf16[1,128,6144]{2,1,0:T(8,128)(2,1)} %param.11) | copy-start | bytes 4718596
  236.3 4.6 %copy-start.5 = (f32[20,6144]{1,0:T(8,128)S(1)}, f32[20,6144]{1,0:T(8,128)}, u32[]{:S(2)}) copy-start(f32[20,6144]{1,0:T(8,128)} %copy-done.4) | copy-start | bytes 1474564
  236.3 49.5 %all-to-all-start.3 = ((bf16[160,4,1536]{2,0,1:T(8,128)(2,1)}), bf16[160,4,1536]{2,0,1:T(8,128)(2,1)}, u32[]{:S(2)}, u32[]{:S(2)}) async-start(bf16[160,4,1536]{2,0,1:T(8,128)(2,1)} %bitcast.178), calls=%async_computation.3 | async-start | bytes 3932160 | tf_op jit(solution)/shard_map/all_to_all | solution.py:129
  285.8 4.4 %copy-start.1 = (bf16[1,128,6144]{2,1,0:T(8,128)(2,1)S(1)}, bf16[1,128,6144]{2,1,0:T(8,128)(2,1)}, u32[]{:S(2)}) copy-start(bf16[1,128,6144]{2,1,0:T(8,128)(2,1)} %param.12) | copy-start | bytes 4718596
Sparse Core Ops, SparseCore 0:
  14.2 40.3 all-gather.4

commit v3 on v2

--- a/solution.py
+++ b/solution.py
@@ -56,6 +56,15 @@
     all_delta = packed[:, width : 2 * width]
     all_present = packed[:, 2 * width]
     slots = all_normed.shape[0]
+    block = width // n_dp
+    own_blocks = lax.all_to_all(
+        jnp.concatenate([normed, delta], axis=0), "dp", 1, 0, tiled=True
+    )
+    pieces = lax.all_gather(own_blocks, "ctx", axis=0, tiled=False).reshape(
+        n_ctx, n_dp, 2, capacity, block
+    )
+    normed_blocks = pieces[:, :, 0].transpose(1, 0, 2, 3).reshape(n_dp * slots, block)
+    delta_blocks = pieces[:, :, 1].transpose(1, 0, 2, 3).reshape(n_dp * slots, block)
     query_raw = jnp.dot(all_normed, w_query, preferred_element_type=jnp.float32)
     key_raw = jnp.dot(all_normed, w_key, preferred_element_type=jnp.float32)
     value_raw = jnp.dot(all_normed, w_value, preferred_element_type=jnp.float32)
@@ -84,7 +93,12 @@
     gate_back = jnp.sum(rows_back * update, axis=-1) * weights * (1.0 - weights)
     router_part = jnp.dot(gate_back, rows, precision=HIGHEST_PRECISION)
     router_split = jnp.stack(
-        [router_part.astype(jnp.bfloat16), (router_part - router_part.astype(jnp.bfloat16).astype(jnp.float32)).astype(jnp.bfloat16)]
+        [
+            router_part.astype(jnp.bfloat16),
+            (router_part - router_part.astype(jnp.bfloat16).astype(jnp.float32)).astype(
+                jnp.bfloat16
+            ),
+        ]
     )
     router_group = jnp.sum(
         lax.all_gather(router_split, "ctx", axis=0, tiled=False).astype(jnp.float32), axis=(0, 1)
@@ -110,23 +124,20 @@
         norm_back(qhat_back, query_hat, query_scale).astype(jnp.bfloat16).reshape(slots, inner)
     )
     key_back = norm_back(khat_back, key_hat, key_scale).astype(jnp.bfloat16).reshape(slots, inner)
-    router_rows = width // inner
-    local_factors = jnp.concatenate(
-        [
-            query_back,
-            key_back,
-            value_back,
-            mixed,
-            router_high.reshape(router_rows, inner),
-            router_low.reshape(router_rows, inner),
-        ],
+    factors = lax.all_gather(
+        jnp.concatenate(
+            [
+                query_back,
+                key_back,
+                value_back,
+                mixed,
+            ],
+            axis=0,
+        ),
+        "dp",
         axis=0,
+        tiled=False,
     )
-    factors = lax.all_to_all(
-        jnp.broadcast_to(local_factors[None], (n_dp,) + local_factors.shape), "dp", 0, 0, tiled=True
-    )
-    normed_blocks = lax.all_to_all(all_normed, "dp", 1, 0, tiled=True)
-    delta_blocks = lax.all_to_all(all_delta, "dp", 1, 0, tiled=True)
 
     def gathered(index):
         return factors[:, index * slots : (index + 1) * slots].reshape(n_dp * slots, inner)
@@ -140,7 +151,9 @@
     grad_key = contract(normed_blocks, gathered(1))
     grad_value = contract(normed_blocks, gathered(2))
     grad_out = contract(gathered(3), delta_blocks)
-    router_pieces = factors[:, 4 * slots :].astype(jnp.float32).reshape(n_dp, 2, width)
+    router_pieces = lax.all_gather(
+        jnp.stack([router_high, router_low]), "dp", axis=0, tiled=False
+    ).astype(jnp.float32)
     grad_router = jnp.sum(router_pieces[:, 0] + router_pieces[:, 1], axis=0)
     return (layer_out, grad_query, grad_key, grad_value, grad_out, grad_router)
 

time: 298 us -> 184 us (0.62)
  waiting for transfers between devices: 169 us -> 29.2 us
  blocking collectives: 9.28 us -> 42.1 us
  starting transfers between devices: 18.7 us -> 4.85 us
  local copies, waits for them, and re-layouts: 21 us -> 31.8 us
  matrix products: 52.4 us -> 48.8 us
    all_to_all x3 -> x0, waiting for transfers between devices: 114 us -> none  [the longest x1 59.6 us: body(): lax.all_to_all(jnp.broadcast_to(local_factors[None], (n_dp,) + local_fact...]
    all_gather x1, waiting for transfers between devices: 40.5 us -> 21.7 us  [body(): lax.all_gather(jnp.concatenate([normed, delta, flag_cols], axis=1), 'ctx'...]
    all_to_all x0 -> x1, blocking collectives: none -> 18.6 us  [body(): lax.all_to_all(jnp.concatenate([normed, delta], axis=0), 'dp', 1, 0, tile...]
    all_to_all x1, waiting for transfers between devices: 15.1 us -> 0.01 us  [body(): lax.all_to_all(contributions.reshape(n_ctx, capacity, width), 'ctx', 0, 0...]
    all_gather x0 -> x1, blocking collectives: none -> 14.3 us  [body(): lax.all_gather(jnp.stack([router_high, router_low]), 'dp', axis=0, tiled=...]
    all_to_all x3 -> x0, starting transfers between devices: 13.9 us -> none  [the longest x1 4.7 us: body(): lax.all_to_all(jnp.broadcast_to(local_factors[None], (n_dp,) + local_fact...]
    reshape x1 -> x2, local copies, waits for them, and re-layouts: 0.16 us -> 8.04 us  [the longest x1 4.09 us: body(): pieces[:, :, 1].transpose(1, 0, 2, 3).reshape(n_dp * slots, block)]
    all_gather x0 -> x2, waiting for transfers between devices: none -> 7.45 us  [the longest x1 7.43 us: body(): lax.all_gather(jnp.concatenate([query_back, key_back, value_back, mixed],...]
  transfers between devices with their start and end apart: 5 -> 4, of which waited for: 5 -> 2; matrix products, arithmetic and copies ran while one was open for 14% -> 40% of each run, Pallas kernels for 0% -> 0%
where the time goes in v3:
time: 184 us; the launch traced here: 182 us
  matrix products  48.8 us (27%)
  blocking collectives  42.1 us (23%)
  local copies, waits for them, and re-layouts  31.8 us (17%)
  waiting for transfers between devices  29.2 us (16%)
  between operations  14.7 us (8%)
  other arithmetic  10.4 us (6%)
  starting transfers between devices  4.85 us (3%)
    all_gather x1, waiting for transfers between devices, body(): lax.all_gather(jnp.concatenate([normed, delta, flag_cols], axis=1), 'ctx'...  21.7 us
    all_to_all x1, blocking collectives, body(): lax.all_to_all(jnp.concatenate([normed, delta], axis=0), 'dp', 1, 0, tile...  18.6 us
    all_gather x1, blocking collectives, body(): lax.all_gather(jnp.stack([router_high, router_low]), 'dp', axis=0, tiled=...  14.3 us
    dot_general x4, matrix products, contract(): lax.dot_general(left, right, (((0,), (0,)), ((), ())), preferred_element_...  10.3 us
    all_gather x1, blocking collectives, body(): lax.all_gather(router_split, 'ctx', axis=0, tiled=False).astype(jnp.float32)  9.22 us
    all_gather x1, waiting for transfers between devices, body(): lax.all_gather(jnp.concatenate([query_back, key_back, value_back, mixed],...  7.43 us
    dot_general x1, matrix products, body(): jnp.dot(mixed, w_out, preferred_element_type=jnp.float32)  5.89 us
    dot_general x1, matrix products, body(): lax.dot_general(all_delta, w_out, (((1,), (1,)), ((), ())), preferred_ele...  5.66 us
  transfers between devices with their start and end apart: 4, of which 2 were waited for; matrix products, arithmetic and copies ran while one was open for 40% of the time, Pallas kernels for 0%

profile of v3, /device:TPU:2, one launch (start us, length us, event | category | flops | bytes accessed | tf_op | source)
XLA Modules:
  0.0 181.8 jit_solution(13713857075044631218)
XLA Ops:
  7.2 0.0 all-gather.14.cloned.1.call-start
  7.2 0.6 compare_reduce_fusion.1
  8.5 0.7 compare_and_fusion
  9.2 1.9 %multiply_reduce_fusion.2 = (f32[20]{0:T(128)S(1)}, f32[20,6144]{1,0:T(8,128)S(1)}) fusion(bf16[1,128,6144]{2,1,0:T(8,128)(2,1)} %param.11, s32[20]{0:T(128)S(1)} %bitcast.197, pred[20]{0:T(512)(128)(4,1)S(1)} %get-tuple-element.20), kind=kOutput, calls=%fused_computation.58 | convolution fusion | flops 31708140 | bytes 2064564 | tf_op jit(solution)/shard_map/dot_general | solution.py:41
  11.1 0.7 fusion.39
  11.8 0.1 multiply_convert_fusion.1
  11.9 0.1 copy.87
  12.0 0.1 copy.88
  12.1 0.4 multiply_convert_fusion
  12.5 0.7 fusion.81
  13.2 0.9 fusion.45
  14.1 0.0 all-gather.10.cloned.1.call-start
  14.1 0.1 pad_maximum_fusion.1
  14.3 18.6 %all_to_all.21 = bf16[40,4,1536]{2,0,1:T(8,128)(2,1)} all-to-all(bf16[40,4,1536]{2,0,1:T(8,128)(2,1)S(1)} %bitcast.186), channel_id=1, replica_groups=mesh['dp'=4,'ctx'=8] {'dp'}, dimensions={1} | all-to-all | bytes 983040 | tf_op jit(solution)/shard_map/all_to_all | solution.py:60
  32.9 21.7 %all-gather.14.cloned.1.call-done = bf16[8,20,12416]{2,1,0:T(8,128)(2,1)} async-done(((bf16[1,20,12416]{2,1,0:T(8,128)(2,1)}), bf16[8,20,12416]{2,1,0:T(8,128)(2,1)}) %all-gather.14.cloned.1.call-update) | async-done | bytes 3973136 | tf_op jit(solution)/shard_map/all_gather | solution.py:52
  54.6 5.1 %reshape.249 = bf16[160,12416]{1,0:T(8,128)(2,1)} reshape(bf16[8,20,12416]{2,1,0:T(8,128)(2,1)} %all-gather.14.cloned.1.call-done) | data formatting | bytes 7946240
  59.7 4.6 %fusion.11 = f32[160,512]{1,0:T(8,128)S(1)} fusion(bf16[6144,512]{1,0:T(8,128)(2,1)} %param.14, bf16[160,12416]{1,0:T(8,128)(2,1)} %reshape.249), kind=kOutput, calls=%fused_computation.20 | convolution fusion | flops 1006632960 | bytes 8585216 | tf_op jit(solution)/shard_map/dot_general | solution.py:68
  64.3 0.1 reshape.228
  64.4 0.2 multiply_reduce_fusion.6
  64.7 0.1 copy.89
  64.7 4.7 %fusion.9 = f32[160,512]{1,0:T(8,128)S(1)} fusion(bf16[6144,512]{1,0:T(8,128)(2,1)} %param.15, bf16[160,12416]{1,0:T(8,128)(2,1)} %reshape.249), kind=kOutput, calls=%fused_computation.18 | convolution fusion | flops 1006632960 | bytes 8585216 | tf_op jit(solution)/shard_map/dot_general | solution.py:69
  69.4 0.1 reshape.229
  69.5 0.2 multiply_reduce_fusion.5
  69.8 0.1 copy.91
  69.8 0.9 compare_reduce_fusion
  70.8 0.1 fusion.63
  70.9 0.4 fusion.48
  71.3 4.6 %fusion.33 = bf16[20,4,8,128]{3,2,1,0:T(8,128)(2,1)S(1)} fusion(bf16[6144,512]{1,0:T(8,128)(2,1)} %param.16, bf16[160,12416]{1,0:T(8,128)(2,1)} %reshape.249), kind=kOutput, calls=%fused_computation.42 | convolution fusion | flops 1006714880 | bytes 8421376 | tf_op jit(solution)/shard_map/dot_general | solution.py:70
  75.9 0.3 fusion.28
  76.2 5.9 %convolution_convert_fusion = bf16[160,6144]{1,0:T(8,128)(2,1)} fusion(bf16[512,6144]{1,0:T(8,128)(2,1)} %param.17, bf16[4,20,8,128]{3,2,1,0:T(8,128)(2,1)S(1)} %fusion.28), kind=kOutput, calls=%fused_computation.2 | convolution fusion | flops 1007616000 | bytes 8421376 | tf_op jit(solution)/shard_map/dot_general | solution.py:85
  82.1 4.0 %reshape.231 = bf16[8,20,6144]{2,1,0:T(8,128)(2,1)} reshape(bf16[160,6144]{1,0:T(8,128)(2,1)} %convolution_convert_fusion) | data formatting | bytes 3932160 | tf_op jit(solution)/shard_map/reshape | solution.py:87
  86.1 4.8 %all-to-all-start = ((bf16[8,20,6144]{2,1,0:T(8,128)(2,1)}), bf16[8,20,6144]{2,1,0:T(8,128)(2,1)}, u32[]{:S(2)}, u32[]{:S(2)}) async-start(bf16[8,20,6144]{2,1,0:T(8,128)(2,1)} %reshape.231), calls=%async_computation | async-start | bytes 4718592 | tf_op jit(solution)/shard_map/all_to_all | solution.py:86
  90.8 5.7 %fusion.30 = bf16[20,4,8,128]{3,2,1,0:T(8,128)(2,1)S(1)} fusion(bf16[512,6144]{1,0:T(8,128)(2,1)} %param.17, bf16[160,12416]{1,0:T(8,128)(2,1)} %reshape.249), kind=kOutput, calls=%fused_computation.41 | convolution fusion | flops 1006714880 | bytes 8421376 | tf_op jit(solution)/shard_map/dot_general | solution.py:108
  96.5 1.1 fusion.57
  97.6 2.6 %multiply_reduce_fusion.4 = (f32[160,4]{0,1:T(4,128)S(1)}, f32[160,4,128]{2,0,1:T(8,128)}) fusion(f32[160,4]{0,1:T(4,128)S(1)} %get-tuple-element.39, f32[4,160,160]{1,2,0:T(8,128)S(1)} %fusion.48, f32[4,160,160]{1,2,0:T(8,128)} %fusion.57, f32[160,4]{0,1:T(4,128)S(1)} %get-tuple-element.38, f32[160,512]{1,0:T(8,128)S(1)} %fusion.9, f32[160,512]{1,0:T(8,128)S(1)} %fusion.11), kind=kOutput, calls=%fused_computation.67 | convolution fusion | flops 27136160 | bytes 1809920 | tf_op jit(solution)/shard_map/hij,jhd->ihd/dot_general | solution.py:121
  100.2 2.4 %multiply_reduce_fusion.3 = (f32[160,4]{0,1:T(4,128)S(1)}, f32[160,4,128]{2,0,1:T(8,128)}) fusion(f32[160,4]{0,1:T(4,128)S(1)} %get-tuple-element.38, f32[160,4]{0,1:T(4,128)S(1)} %get-tuple-element.39, f32[4,160,160]{1,2,0:T(8,128)S(1)} %fusion.48, f32[4,160,160]{1,2,0:T(8,128)} %fusion.57, f32[160,512]{1,0:T(8,128)S(1)} %fusion.9, f32[160,512]{1,0:T(8,128)S(1)} %fusion.11), kind=kOutput, calls=%fused_computation.65 | convolution fusion | flops 27136160 | bytes 1809920 | tf_op jit(solution)/shard_map/hij,ihd->jhd/dot_general | solution.py:122
  102.6 0.2 fusion.29
  102.9 1.2 copy_bitcast_fusion.3
  104.2 0.2 copy_bitcast_fusion.2
  104.4 0.9 pad_maximum_fusion
  105.3 4.3 %copy.97 = bf16[8,160,1536]{2,0,1:T(8,128)(2,1)S(1)} copy(bf16[8,160,1536]{2,1,0:T(8,128)(2,1)} %all-gather.10.cloned.1.call-done) | data formatting | bytes 7864320 | tf_op jit(solution)/shard_map/all_gather | solution.py:63
  109.6 1.5 slice_bitcast_fusion
  111.1 2.1 %copy.106 = bf16[4,8,20,1536]{3,2,1,0:T(8,128)(2,1)} copy(bf16[4,8,20,1536]{3,1,2,0:T(8,128)(2,1)S(1)} %get-tuple-element.22) | data formatting | bytes 3932160 | tf_op jit(solution)/shard_map/transpose | solution.py:67
  113.3 4.1 %reshape.242 = bf16[640,1536]{1,0:T(8,128)(2,1)} reshape(bf16[4,8,20,1536]{3,2,1,0:T(8,128)(2,1)} %copy.106) | data formatting | bytes 3932160 | tf_op jit(solution)/shard_map/reshape | solution.py:67
  117.3 3.7 %copy.98 = bf16[4,8,20,1536]{3,2,1,0:T(8,128)(2,1)} copy(bf16[4,8,20,1536]{3,1,2,0:T(8,128)(2,1)} %get-tuple-element.23) | data formatting | bytes 3932160 | tf_op jit(solution)/shard_map/transpose | solution.py:66
  121.0 4.0 %reshape.233 = bf16[640,1536]{1,0:T(8,128)(2,1)} reshape(bf16[4,8,20,1536]{3,2,1,0:T(8,128)(2,1)} %copy.98) | data formatting | bytes 3932160 | tf_op jit(solution)/shard_map/reshape | solution.py:66
  125.0 2.1 %convert_reduce_fusion = f32[20,6144]{1,0:T(8,128)S(1)} fusion(bf16[8,20,6144]{2,1,0:T(8,128)(2,1)} %all-to-all-done), kind=kLoop, calls=%fused_computation.5 | loop fusion | flops 1843200 | bytes 2457600 | tf_op jit(solution)/shard_map/reduce_sum | solution.py:89
  127.1 0.2 multiply_reduce_fusion.1
  127.3 0.4 fusion.88
  127.8 0.1 maximum_bitcast_fusion
  127.8 9.2 %all-gather.4 = bf16[8,2,6144]{2,1,0:T(2,128)(2,1)S(1)} all-gather(bf16[1,2,6144]{2,1,0:T(2,128)(2,1)S(1)} %maximum_bitcast_fusion), channel_id=3, replica_groups=mesh['dp'=4,'ctx'=8] {'ctx'}, dimensions={0}, use_global_device_ids=true | all-gather | bytes 221184 | tf_op jit(solution)/shard_map/all_gather | solution.py:104
  137.0 0.2 convert_reduce_fusion.1
  137.3 0.1 maximum_bitcast_fusion.1
  137.4 14.3 %all-gather.5 = bf16[4,2,6144]{2,1,0:T(2,128)(2,1)S(1)} all-gather(bf16[1,2,6144]{2,1,0:T(2,128)(2,1)S(1)} %maximum_bitcast_fusion.1), channel_id=4, replica_groups=mesh['dp'=4,'ctx'=8] {'dp'}, dimensions={0}, use_global_device_ids=true | all-gather | bytes 122880 | tf_op jit(solution)/shard_map/all_gather | solution.py:154
  151.7 0.1 convert_element_type.164
  151.7 0.8 fusion.69
  152.5 2.8 %fusion.2 = bf16[1,128,6144]{2,1,0:T(8,128)(2,1)} fusion(bf16[1,128,6144]{2,1,0:T(8,128)(2,1)S(1)} %copy-done.2, f32[20,6144]{1,0:T(8,128)S(1)} %convert_reduce_fusion, f32[20]{0:T(128)S(1)} %fusion.39, s32[20]{0:T(128)S(1)} %bitcast.199, pred[20]{0:T(512)(128)(4,1)S(1)} %get-tuple-element.20), kind=kOutput, calls=%fused_computation.4 | convolution fusion | flops 191230976 | bytes 3637428 | tf_op jit(solution)/shard_map/dot_general | solution.py:91
  155.3 7.4 %all-gather.12.cloned.1.call-done = bf16[2560,512]{1,0:T(8,128)(2,1)} async-done(((bf16[640,512]{1,0:T(8,128)(2,1)}), bf16[2560,512]{1,0:T(8,128)(2,1)}) %all-gather.12.cloned.1.call-update) | async-done | bytes 2621456 | tf_op jit(solution)/shard_map/all_gather | solution.py:127
  162.7 2.1 %fusion.99 = (bf16[4,160,512]{2,1,0:T(8,128)(2,1)S(1)}, bf16[4,160,512]{2,1,0:T(8,128)(2,1)S(1)}, bf16[4,160,512]{2,1,0:T(8,128)(2,1)S(1)}, bf16[4,160,512]{2,1,0:T(8,128)(2,1)S(1)}) fusion(bf16[4,640,512]{2,1,0:T(8,128)(2,1)} %bitcast.183), kind=kLoop, calls=%fused_computation.139 | loop fusion | bytes 5242880 | tf_op jit(solution)/shard_map/slice | solution.py:143
  164.8 0.3 copy-done.4
  165.0 2.6 %convolution_convert_fusion.2 = bf16[1536,512]{1,0:T(8,128)(2,1)} fusion(bf16[640,1536]{1,0:T(8,128)(2,1)S(1)} %copy-done.4, bf16[640,512]{1,0:T(8,128)(2,1)S(1)} %bitcast.190), kind=kOutput, calls=%fused_computation.7 | convolution fusion | flops 1007419392 | bytes 4194304 | tf_op jit(solution)/shard_map/dot_general | solution.py:146
  167.6 2.6 %convolution_convert_fusion.3 = bf16[1536,512]{1,0:T(8,128)(2,1)} fusion(bf16[640,1536]{1,0:T(8,128)(2,1)S(1)} %copy-done.4, bf16[640,512]{1,0:T(8,128)(2,1)S(1)} %bitcast.189), kind=kOutput, calls=%fused_computation.8 | convolution fusion | flops 1007419392 | bytes 4194304 | tf_op jit(solution)/shard_map/dot_general | solution.py:146
  170.2 2.6 %convolution_convert_fusion.4 = bf16[1536,512]{1,0:T(8,128)(2,1)} fusion(bf16[640,1536]{1,0:T(8,128)(2,1)S(1)} %copy-done.4, bf16[640,512]{1,0:T(8,128)(2,1)S(1)} %bitcast.188), kind=kOutput, calls=%fused_computation.9 | convolution fusion | flops 1007419392 | bytes 4194304 | tf_op jit(solution)/shard_map/dot_general | solution.py:146
  172.7 2.6 %convolution_convert_fusion.1 = bf16[512,1536]{1,0:T(8,128)(2,1)} fusion(bf16[640,512]{1,0:T(8,128)(2,1)S(1)} %bitcast.187, bf16[640,1536]{1,0:T(8,128)(2,1)S(1)} %copy-done.3), kind=kOutput, calls=%fused_computation.6 | convolution fusion | flops 1007419392 | bytes 4194304 | tf_op jit(solution)/shard_map/dot_general | solution.py:146
  (32 shorter events, 0.3 us)
Async XLA Ops:
  7.2 5.0 %copy-start = (bf16[1,128,6144]{2,1,0:T(8,128)(2,1)S(1)}, bf16[1,128,6144]{2,1,0:T(8,128)(2,1)}, u32[]{:S(2)}) copy-start(bf16[1,128,6144]{2,1,0:T(8,128)(2,1)} %param.12) | copy-start | bytes 4718596
  7.2 3.9 %copy-start.6 = (f32[6144]{0:T(1024)S(1)}, f32[6144]{0:T(1024)}, u32[]{:S(2)}) copy-start(f32[6144]{0:T(1024)} %param.13) | copy-start | bytes 73732
  7.2 47.4 %all-gather.14.cloned.1.call-start = ((), (), s32[]{:S(2)}) async-start(), calls=%async_computation.4 | async-start | bytes 5363712 | tf_op jit(solution)/shard_map/all_gather | solution.py:52
  14.1 91.3 %all-gather.10.cloned.1.call-start = ((), (), s32[]{:S(2)}) async-start(), calls=%async_computation.2 | async-start | bytes 4423680 | tf_op jit(solution)/shard_map/all_gather | solution.py:63
  86.1 38.9 %all-to-all-start = ((bf16[8,20,6144]{2,1,0:T(8,128)(2,1)}), bf16[8,20,6144]{2,1,0:T(8,128)(2,1)}, u32[]{:S(2)}, u32[]{:S(2)}) async-start(bf16[8,20,6144]{2,1,0:T(8,128)(2,1)} %reshape.231), calls=%async_computation | async-start | bytes 4718592 | tf_op jit(solution)/shard_map/all_to_all | solution.py:86
  90.8 71.9 %all-gather.12.cloned.1.call-start = ((), (), s32[]{:S(2)}) async-start(), calls=%async_computation.3 | async-start | bytes 3276800 | tf_op jit(solution)/shard_map/all_gather | solution.py:127
  102.6 1.6 copy-start.5
  127.1 25.4 %copy-start.2 = (bf16[1,128,6144]{2,1,0:T(8,128)(2,1)S(1)}, bf16[1,128,6144]{2,1,0:T(8,128)(2,1)}, u32[]{:S(2)}) copy-start(bf16[1,128,6144]{2,1,0:T(8,128)(2,1)} %param.11) | copy-start | bytes 4718596
  162.7 2.3 %copy-start.4 = (bf16[640,1536]{1,0:T(8,128)(2,1)S(1)}, bf16[640,1536]{1,0:T(8,128)(2,1)}, u32[]{:S(2)}) copy-start(bf16[640,1536]{1,0:T(8,128)(2,1)} %reshape.233) | copy-start | bytes 5898244
  170.2 2.6 %copy-start.3 = (bf16[640,1536]{1,0:T(8,128)(2,1)S(1)}, bf16[640,1536]{1,0:T(8,128)(2,1)}, u32[]{:S(2)}) copy-start(bf16[640,1536]{1,0:T(8,128)(2,1)} %reshape.242) | copy-start | bytes 5898244
  172.7 2.6 %copy-start.1 = (bf16[1,128,6144]{2,1,0:T(8,128)(2,1)S(1)}, bf16[1,128,6144]{2,1,0:T(8,128)(2,1)}, u32[]{:S(2)}) copy-start(bf16[1,128,6144]{2,1,0:T(8,128)(2,1)} %param.12) | copy-start | bytes 4718596
Sparse Core Ops, SparseCore 0:
  14.2 40.3 all-gather.13
  56.5 35.8 all-gather.9
  105.4 57.2 all-gather.11

commit v4 on v3

--- a/solution.py
+++ b/solution.py
@@ -50,12 +50,12 @@
         present.astype(jnp.bfloat16)
     )
     packed = lax.all_gather(
-        jnp.concatenate([normed, delta, flag_cols], axis=1), "ctx", axis=0, tiled=True
+        jnp.concatenate([normed, delta, flag_cols], axis=1), "ctx", axis=0, tiled=False
     )
-    all_normed = packed[:, :width]
-    all_delta = packed[:, width : 2 * width]
-    all_present = packed[:, 2 * width]
-    slots = all_normed.shape[0]
+    chunk_normed = packed[:, :, :width]
+    chunk_delta = packed[:, :, width : 2 * width]
+    all_present = packed[:, :, 2 * width].reshape(n_ctx * capacity)
+    slots = n_ctx * capacity
     block = width // n_dp
     own_blocks = lax.all_to_all(
         jnp.concatenate([normed, delta], axis=0), "dp", 1, 0, tiled=True
@@ -65,9 +65,15 @@
     )
     normed_blocks = pieces[:, :, 0].transpose(1, 0, 2, 3).reshape(n_dp * slots, block)
     delta_blocks = pieces[:, :, 1].transpose(1, 0, 2, 3).reshape(n_dp * slots, block)
-    query_raw = jnp.dot(all_normed, w_query, preferred_element_type=jnp.float32)
-    key_raw = jnp.dot(all_normed, w_key, preferred_element_type=jnp.float32)
-    value_raw = jnp.dot(all_normed, w_value, preferred_element_type=jnp.float32)
+    def project(weight):
+        raw = lax.dot_general(
+            chunk_normed, weight, (((2,), (0,)), ((), ())), preferred_element_type=jnp.float32
+        )
+        return raw.reshape(slots, inner)
+
+    query_raw = project(w_query)
+    key_raw = project(w_key)
+    value_raw = project(w_value)
     query_hat, query_scale = head_norm(query_raw, HDIM)
     key_hat, key_scale = head_norm(key_raw, HDIM)
     query_b = query_hat.astype(jnp.bfloat16)
@@ -82,9 +88,14 @@
     attend_b = attend.astype(jnp.bfloat16)
     mixed = jnp.einsum("hij,jhd->ihd", attend_b, value_b, preferred_element_type=jnp.float32)
     mixed = mixed.astype(jnp.bfloat16).reshape(slots, inner)
-    contributions = jnp.dot(mixed, w_out, preferred_element_type=jnp.float32).astype(jnp.bfloat16)
+    contributions = lax.dot_general(
+        mixed.reshape(n_ctx, capacity, inner),
+        w_out,
+        (((2,), (0,)), ((), ())),
+        preferred_element_type=jnp.float32,
+    ).astype(jnp.bfloat16)
     received = lax.all_to_all(
-        contributions.reshape(n_ctx, capacity, width), "ctx", 0, 0, tiled=True
+        contributions, "ctx", 0, 0, tiled=True
     )
     update = jnp.sum(received.astype(jnp.float32), axis=0)
     scaled = weights[:, None] * update
@@ -106,7 +117,7 @@
     router_high = router_group.astype(jnp.bfloat16)
     router_low = (router_group - router_high.astype(jnp.float32)).astype(jnp.bfloat16)
     mixed_back = lax.dot_general(
-        all_delta, w_out, (((1,), (1,)), ((), ())), preferred_element_type=jnp.float32
+        chunk_delta, w_out, (((2,), (1,)), ((), ())), preferred_element_type=jnp.float32
     )
     mixed_back = mixed_back.astype(jnp.bfloat16).reshape(slots, heads_here, HDIM)
     attend_back = jnp.einsum(

time: 184 us -> 186 us (1.011)
  matrix products: 48.8 us -> 55.4 us
  local copies, waits for them, and re-layouts: 31.8 us -> 25.8 us
    unnamed x15 -> x18, local copies, waits for them, and re-layouts: 5.44 us -> 0.95 us
    reshape x3 -> x1, local copies, waits for them, and re-layouts: 4.19 us -> 1.65 us  [body(): mixed_back.astype(jnp.bfloat16).reshape(slots, heads_here, HDIM)]
  transfers between devices with their start and end apart: 4 -> 4, of which waited for: 2 -> 2; matrix products, arithmetic and copies ran while one was open for 40% -> 39% of each run, Pallas kernels for 0% -> 0%
where the time goes in v4:
time: 186 us; the launch traced here: 183 us
  matrix products  55.4 us (30%)
  blocking collectives  41.9 us (23%)
  waiting for transfers between devices  30.4 us (16%)
  local copies, waits for them, and re-layouts  25.8 us (14%)
  between operations  14.7 us (8%)
  other arithmetic  10.8 us (6%)
  starting transfers between devices  4.21 us (2%)
    all_gather x1, waiting for transfers between devices, body(): lax.all_gather(jnp.concatenate([normed, delta, flag_cols], axis=1), 'ctx'...  21.7 us
    all_to_all x1, blocking collectives, body(): lax.all_to_all(jnp.concatenate([normed, delta], axis=0), 'dp', 1, 0, tile...  18.6 us
    dot_general x3, matrix products, project(): lax.dot_general(chunk_normed, weight, (((2,), (0,)), ((), ())), preferred...  14.8 us
    all_gather x1, blocking collectives, body(): lax.all_gather(jnp.stack([router_high, router_low]), 'dp', axis=0, tiled=...  14.2 us
    dot_general x4, matrix products, contract(): lax.dot_general(left, right, (((0,), (0,)), ((), ())), preferred_element_...  10.3 us
    all_gather x1, blocking collectives, body(): lax.all_gather(router_split, 'ctx', axis=0, tiled=False).astype(jnp.float32)  9.19 us
    all_gather x1, waiting for transfers between devices, body(): lax.all_gather(jnp.concatenate([query_back, key_back, value_back, mixed],...  8.66 us
    dot_general x1, matrix products, body(): lax.dot_general(chunk_delta, w_out, (((2,), (1,)), ((), ())), preferred_e...  6.45 us
  transfers between devices with their start and end apart: 4, of which 2 were waited for; matrix products, arithmetic and copies ran while one was open for 39% of the time, Pallas kernels for 0%

profile of v4, /device:TPU:2, one launch (start us, length us, event | category | flops | bytes accessed | tf_op | source)
XLA Modules:
  0.0 183.2 jit_solution(14341050652866015723)
XLA Ops:
  7.2 0.6 compare_reduce_fusion.1
  8.5 0.7 compare_and_fusion
  9.2 1.9 %multiply_reduce_fusion.2 = (f32[20]{0:T(128)S(1)}, f32[20,6144]{1,0:T(8,128)S(1)}) fusion(bf16[1,128,6144]{2,1,0:T(8,128)(2,1)} %param.11, s32[20]{0:T(128)S(1)} %bitcast.136, pred[20]{0:T(512)(128)(4,1)S(1)} %get-tuple-element.20), kind=kOutput, calls=%fused_computation.60 | convolution fusion | flops 31708140 | bytes 2064564 | tf_op jit(solution)/shard_map/dot_general | solution.py:41
  11.1 1.4 fusion.41
  12.5 0.1 multiply_convert_fusion.1
  12.6 0.1 copy.90
  12.8 0.1 copy.91
  12.9 1.2 multiply_convert_fusion
  14.1 0.7 fusion.79
  14.7 0.9 fusion.47
  15.7 0.1 pad_maximum_fusion.1
  15.8 18.6 %all_to_all.21 = bf16[40,4,1536]{2,0,1:T(8,128)(2,1)} all-to-all(bf16[40,4,1536]{2,0,1:T(8,128)(2,1)S(1)} %bitcast.125), channel_id=1, replica_groups=mesh['dp'=4,'ctx'=8] {'dp'}, dimensions={1} | all-to-all | bytes 983040 | tf_op jit(solution)/shard_map/all_to_all | solution.py:60
  34.4 21.7 %all-gather.15.cloned.1.call-done = bf16[8,20,12416]{2,1,0:T(8,128)(2,1)} async-done(((bf16[1,20,12416]{2,1,0:T(8,128)(2,1)}), bf16[8,20,12416]{2,1,0:T(8,128)(2,1)}) %all-gather.15.cloned.1.call-update) | async-done | bytes 3973136 | tf_op jit(solution)/shard_map/all_gather | solution.py:52
  56.1 4.9 %fusion.8 = f32[8,20,512]{2,1,0:T(8,128)S(1)} fusion(bf16[6144,512]{1,0:T(8,128)(2,1)} %param.14, bf16[8,20,12416]{2,1,0:T(8,128)(2,1)} %all-gather.15.cloned.1.call-done), kind=kOutput, calls=%fused_computation.10 | convolution fusion | flops 1006632960 | bytes 8978432 | tf_op jit(solution)/shard_map/dot_general | solution.py:69
  61.0 0.1 reshape_reshape.10
  61.1 0.2 multiply_reduce_fusion.6
  61.4 0.1 copy.92
  61.4 4.9 %fusion.6 = f32[8,20,512]{2,1,0:T(8,128)S(1)} fusion(bf16[6144,512]{1,0:T(8,128)(2,1)} %param.15, bf16[8,20,12416]{2,1,0:T(8,128)(2,1)} %all-gather.15.cloned.1.call-done), kind=kOutput, calls=%fused_computation.8 | convolution fusion | flops 1006632960 | bytes 8978432 | tf_op jit(solution)/shard_map/dot_general | solution.py:69
  66.4 0.1 reshape_reshape.11
  66.5 0.2 multiply_reduce_fusion.5
  66.8 0.1 copy.94
  66.9 1.0 compare_reduce_fusion
  67.9 0.1 gt.16
  68.0 4.9 %fusion.27 = bf16[8,20,512]{2,1,0:T(8,128)(2,1)S(1)} fusion(bf16[6144,512]{1,0:T(8,128)(2,1)} %param.16, bf16[8,20,12416]{2,1,0:T(8,128)(2,1)} %all-gather.15.cloned.1.call-done), kind=kOutput, calls=%fused_computation.40 | convolution fusion | flops 1006714880 | bytes 8814592 | tf_op jit(solution)/shard_map/dot_general | solution.py:69
  73.0 0.1 fusion.60
  73.1 0.4 fusion.50
  73.5 0.3 convolution_convert_fusion.6
  73.9 0.1 copy.98
  74.0 0.1 reshape_reshape.12
  74.1 5.7 %convolution_convert_fusion = bf16[8,20,6144]{2,1,0:T(8,128)(2,1)} fusion(bf16[8,20,512]{2,1,0:T(8,128)(2,1)S(1)} %reshape_reshape.12, bf16[512,6144]{1,0:T(8,128)(2,1)} %param.17), kind=kOutput, calls=%fused_computation.1 | convolution fusion | flops 1007616000 | bytes 8421376 | tf_op jit(solution)/shard_map/dot_general | solution.py:91
  79.8 4.1 %all-to-all-start = ((bf16[8,20,6144]{2,1,0:T(8,128)(2,1)}), bf16[8,20,6144]{2,1,0:T(8,128)(2,1)S(1)}, u32[]{:S(2)}, u32[]{:S(2)}) async-start(bf16[8,20,6144]{2,1,0:T(8,128)(2,1)} %convolution_convert_fusion), calls=%async_computation | async-start | bytes 4718592 | tf_op jit(solution)/shard_map/all_to_all | solution.py:97
  83.9 6.4 %fusion.32 = bf16[8,20,512]{2,1,0:T(8,128)(2,1)} fusion(bf16[512,6144]{1,0:T(8,128)(2,1)} %param.17, bf16[8,20,12416]{2,1,0:T(8,128)(2,1)} %all-gather.15.cloned.1.call-done), kind=kOutput, calls=%fused_computation.41 | convolution fusion | flops 1006714880 | bytes 8814592 | tf_op jit(solution)/shard_map/dot_general | solution.py:119
  90.3 1.6 reshape.220
  92.0 1.3 fusion.37
  93.3 0.7 copy.164
  94.0 2.1 %fusion.63 = f32[4,160,160]{1,2,0:T(8,128)} fusion(bf16[160,4,128]{2,1,0:T(4,128)(2,1)} %reshape.220, bf16[160,4,128]{2,1,0:T(4,128)(2,1)} %copy-done.8), kind=kOutput, calls=%fused_computation.92 | convolution fusion | flops 26214400 | bytes 737280 | tf_op jit(solution)/shard_map/ihd,jhd->hij/dot_general | solution.py:123
  96.1 3.3 %multiply_reduce_fusion.4 = (f32[160,4]{0,1:T(4,128)S(1)}, f32[160,4,128]{2,0,1:T(8,128)}) fusion(f32[160,4,128]{2,1,0:T(4,128)S(1)} %reshape_reshape.10, f32[160,4]{0,1:T(4,128)S(1)} %get-tuple-element.39, f32[4,160,160]{1,2,0:T(8,128)} %copy-done.4, f32[4,160,160]{1,2,0:T(8,128)} %fusion.63, f32[160,4,128]{2,1,0:T(4,128)} %copy-done.3, ...), kind=kOutput, calls=%fused_computation.69 | convolution fusion | flops 27136160 | bytes 1809920 | tf_op jit(solution)/shard_map/hij,jhd->ihd/dot_general | solution.py:132
  99.4 3.0 %multiply_reduce_fusion.3 = (f32[160,4]{0,1:T(4,128)S(1)}, f32[160,4,128]{2,0,1:T(8,128)}) fusion(f32[160,4,128]{2,1,0:T(4,128)} %copy-done.3, f32[160,4]{0,1:T(4,128)S(1)} %get-tuple-element.38, f32[160,4,128]{2,1,0:T(4,128)S(1)} %reshape_reshape.10, f32[160,4]{0,1:T(4,128)S(1)} %get-tuple-element.39, f32[4,160,160]{1,2,0:T(8,128)} %copy-done.4, ...), kind=kOutput, calls=%fused_computation.67 | convolution fusion | flops 27136160 | bytes 1809920 | tf_op jit(solution)/shard_map/hij,ihd->jhd/dot_general | solution.py:133
  102.4 1.2 copy_bitcast_fusion.4
  103.7 1.3 copy_bitcast_fusion.3
  105.0 1.8 pad_maximum_fusion
  106.8 4.3 %copy.100 = bf16[8,160,1536]{2,0,1:T(8,128)(2,1)S(1)} copy(bf16[8,160,1536]{2,1,0:T(8,128)(2,1)} %all-gather.11.cloned.1.call-done) | data formatting | bytes 7864320 | tf_op jit(solution)/shard_map/all_gather | solution.py:63
  111.1 1.6 slice_bitcast_fusion
  112.6 2.0 %copy.110 = bf16[4,8,20,1536]{3,2,1,0:T(8,128)(2,1)} copy(bf16[4,8,20,1536]{3,1,2,0:T(8,128)(2,1)S(1)} %get-tuple-element.22) | data formatting | bytes 3932160 | tf_op jit(solution)/shard_map/transpose | solution.py:67
  114.7 4.1 %reshape.229 = bf16[640,1536]{1,0:T(8,128)(2,1)} reshape(bf16[4,8,20,1536]{3,2,1,0:T(8,128)(2,1)} %copy.110) | data formatting | bytes 3932160 | tf_op jit(solution)/shard_map/reshape | solution.py:67
  118.7 3.6 %copy.101 = bf16[4,8,20,1536]{3,2,1,0:T(8,128)(2,1)} copy(bf16[4,8,20,1536]{3,1,2,0:T(8,128)(2,1)} %get-tuple-element.23) | data formatting | bytes 3932160 | tf_op jit(solution)/shard_map/transpose | solution.py:66
  122.3 4.0 %reshape.219 = bf16[640,1536]{1,0:T(8,128)(2,1)} reshape(bf16[4,8,20,1536]{3,2,1,0:T(8,128)(2,1)} %copy.101) | data formatting | bytes 3932160 | tf_op jit(solution)/shard_map/reshape | solution.py:66
  126.3 0.4 convert_reduce_fusion
  126.7 0.7 copy-done.5
  127.3 0.2 multiply_reduce_fusion.1
  127.5 0.4 fusion.86
  128.1 9.2 %all-gather.5 = bf16[8,2,6144]{2,1,0:T(2,128)(2,1)S(1)} all-gather(bf16[1,2,6144]{2,1,0:T(2,128)(2,1)S(1)} %maximum_bitcast_fusion), channel_id=4, replica_groups=mesh['dp'=4,'ctx'=8] {'ctx'}, dimensions={0}, use_global_device_ids=true | all-gather | bytes 221184 | tf_op jit(solution)/shard_map/all_gather | solution.py:115
  137.3 0.2 convert_reduce_fusion.1
  137.6 14.2 %all-gather.6 = bf16[4,2,6144]{2,1,0:T(2,128)(2,1)S(1)} all-gather(bf16[1,2,6144]{2,1,0:T(2,128)(2,1)S(1)} %maximum_bitcast_fusion.1), channel_id=5, replica_groups=mesh['dp'=4,'ctx'=8] {'dp'}, dimensions={0}, use_global_device_ids=true | all-gather | bytes 122880 | tf_op jit(solution)/shard_map/all_gather | solution.py:165
  151.7 0.1 convert_element_type.164
  151.8 0.8 fusion.67
  152.6 2.8 %fusion.2 = bf16[1,128,6144]{2,1,0:T(8,128)(2,1)} fusion(bf16[1,128,6144]{2,1,0:T(8,128)(2,1)S(1)} %copy-done.2, f32[20,6144]{1,0:T(8,128)S(1)} %convert_reduce_fusion, f32[20]{0:T(128)S(1)} %fusion.41, s32[20]{0:T(128)S(1)} %bitcast.138, pred[20]{0:T(512)(128)(4,1)S(1)} %get-tuple-element.20), kind=kOutput, calls=%fused_computation.4 | convolution fusion | flops 191230976 | bytes 3637428 | tf_op jit(solution)/shard_map/dot_general | solution.py:102
  155.4 8.7 %all-gather.13.cloned.1.call-done = bf16[2560,512]{1,0:T(8,128)(2,1)} async-done(((bf16[640,512]{1,0:T(8,128)(2,1)}), bf16[2560,512]{1,0:T(8,128)(2,1)}) %all-gather.13.cloned.1.call-update) | async-done | bytes 2621456 | tf_op jit(solution)/shard_map/all_gather | solution.py:138
  164.1 2.1 %fusion.97 = (bf16[4,160,512]{2,1,0:T(8,128)(2,1)S(1)}, bf16[4,160,512]{2,1,0:T(8,128)(2,1)S(1)}, bf16[4,160,512]{2,1,0:T(8,128)(2,1)S(1)}, bf16[4,160,512]{2,1,0:T(8,128)(2,1)S(1)}) fusion(bf16[4,640,512]{2,1,0:T(8,128)(2,1)} %bitcast.122), kind=kLoop, calls=%fused_computation.137 | loop fusion | bytes 5242880 | tf_op jit(solution)/shard_map/slice | solution.py:154
  166.2 0.2 copy-done.7
  166.4 2.6 %convolution_convert_fusion.2 = bf16[1536,512]{1,0:T(8,128)(2,1)} fusion(bf16[640,1536]{1,0:T(8,128)(2,1)S(1)} %copy-done.7, bf16[640,512]{1,0:T(8,128)(2,1)S(1)} %bitcast.130), kind=kOutput, calls=%fused_computation.16 | convolution fusion | flops 1007419392 | bytes 4194304 | tf_op jit(solution)/shard_map/dot_general | solution.py:157
  169.0 2.6 %convolution_convert_fusion.3 = bf16[1536,512]{1,0:T(8,128)(2,1)} fusion(bf16[640,1536]{1,0:T(8,128)(2,1)S(1)} %copy-done.7, bf16[640,512]{1,0:T(8,128)(2,1)S(1)} %bitcast.129), kind=kOutput, calls=%fused_computation.17 | convolution fusion | flops 1007419392 | bytes 4194304 | tf_op jit(solution)/shard_map/dot_general | solution.py:157
  171.6 2.6 %convolution_convert_fusion.4 = bf16[1536,512]{1,0:T(8,128)(2,1)} fusion(bf16[640,1536]{1,0:T(8,128)(2,1)S(1)} %copy-done.7, bf16[640,512]{1,0:T(8,128)(2,1)S(1)} %bitcast.128), kind=kOutput, calls=%fused_computation.18 | convolution fusion | flops 1007419392 | bytes 4194304 | tf_op jit(solution)/shard_map/dot_general | solution.py:157
  174.1 2.6 %convolution_convert_fusion.1 = bf16[512,1536]{1,0:T(8,128)(2,1)} fusion(bf16[640,512]{1,0:T(8,128)(2,1)S(1)} %bitcast.127, bf16[640,1536]{1,0:T(8,128)(2,1)S(1)} %copy-done.6), kind=kOutput, calls=%fused_computation.15 | convolution fusion | flops 1007419392 | bytes 4194304 | tf_op jit(solution)/shard_map/dot_general | solution.py:157
  (39 shorter events, 0.5 us)
Async XLA Ops:
  7.2 5.7 %copy-start = (bf16[1,128,6144]{2,1,0:T(8,128)(2,1)S(1)}, bf16[1,128,6144]{2,1,0:T(8,128)(2,1)}, u32[]{:S(2)}) copy-start(bf16[1,128,6144]{2,1,0:T(8,128)(2,1)} %param.12) | copy-start | bytes 4718596
  7.2 48.9 %all-gather.15.cloned.1.call-start = ((), (), s32[]{:S(2)}) async-start(), calls=%async_computation.4 | async-start | bytes 5363712 | tf_op jit(solution)/shard_map/all_gather | solution.py:52
  15.6 91.2 %all-gather.11.cloned.1.call-start = ((), (), s32[]{:S(2)}) async-start(), calls=%async_computation.2 | async-start | bytes 4423680 | tf_op jit(solution)/shard_map/all_gather | solution.py:63
  66.5 6.6 %copy-start.3 = (f32[160,4,128]{2,1,0:T(4,128)}, f32[160,4,128]{2,1,0:T(4,128)S(1)}, u32[]{:S(2)}) copy-start(f32[160,4,128]{2,1,0:T(4,128)S(1)} %reshape_reshape.11) | copy-start | bytes 983044
  73.0 1.0 copy-start.8
  73.5 6.2 %copy-start.4 = (f32[4,160,160]{1,2,0:T(8,128)}, f32[4,160,160]{1,2,0:T(8,128)S(1)}, u32[]{:S(2)}) copy-start(f32[4,160,160]{1,2,0:T(8,128)S(1)} %fusion.50) | copy-start | bytes 1228804
  79.8 46.5 %all-to-all-start = ((bf16[8,20,6144]{2,1,0:T(8,128)(2,1)}), bf16[8,20,6144]{2,1,0:T(8,128)(2,1)S(1)}, u32[]{:S(2)}, u32[]{:S(2)}) async-start(bf16[8,20,6144]{2,1,0:T(8,128)(2,1)} %convolution_convert_fusion), calls=%async_computation | async-start | bytes 4718592 | tf_op jit(solution)/shard_map/all_to_all | solution.py:97
  83.9 80.2 %all-gather.13.cloned.1.call-start = ((), (), s32[]{:S(2)}) async-start(), calls=%async_computation.3 | async-start | bytes 3276800 | tf_op jit(solution)/shard_map/all_gather | solution.py:138
  126.3 1.1 copy-start.5
  126.7 25.9 %copy-start.2 = (bf16[1,128,6144]{2,1,0:T(8,128)(2,1)S(1)}, bf16[1,128,6144]{2,1,0:T(8,128)(2,1)}, u32[]{:S(2)}) copy-start(bf16[1,128,6144]{2,1,0:T(8,128)(2,1)} %param.11) | copy-start | bytes 4718596
  164.1 2.3 %copy-start.7 = (bf16[640,1536]{1,0:T(8,128)(2,1)S(1)}, bf16[640,1536]{1,0:T(8,128)(2,1)}, u32[]{:S(2)}) copy-start(bf16[640,1536]{1,0:T(8,128)(2,1)} %reshape.219) | copy-start | bytes 5898244
  171.5 2.6 %copy-start.6 = (bf16[640,1536]{1,0:T(8,128)(2,1)S(1)}, bf16[640,1536]{1,0:T(8,128)(2,1)}, u32[]{:S(2)}) copy-start(bf16[640,1536]{1,0:T(8,128)(2,1)} %reshape.229) | copy-start | bytes 5898244
  174.1 2.6 %copy-start.1 = (bf16[1,128,6144]{2,1,0:T(8,128)(2,1)S(1)}, bf16[1,128,6144]{2,1,0:T(8,128)(2,1)}, u32[]{:S(2)}) copy-start(bf16[1,128,6144]{2,1,0:T(8,128)(2,1)} %param.12) | copy-start | bytes 4718596
Sparse Core Ops, SparseCore 0:
  15.7 40.3 all-gather.14
  58.0 47.4 all-gather.10
  107.6 56.4 all-gather.12

commit v5 on v4

--- a/solution.py
+++ b/solution.py
@@ -88,8 +88,30 @@
     attend_b = attend.astype(jnp.bfloat16)
     mixed = jnp.einsum("hij,jhd->ihd", attend_b, value_b, preferred_element_type=jnp.float32)
     mixed = mixed.astype(jnp.bfloat16).reshape(slots, inner)
+    mixed_back = lax.dot_general(
+        chunk_delta, w_out, (((2,), (1,)), ((), ())), preferred_element_type=jnp.float32
+    )
+    mixed_back = mixed_back.astype(jnp.bfloat16).reshape(slots, heads_here, HDIM)
+    attend_back = jnp.einsum(
+        "ihd,jhd->hij", mixed_back, value_b, preferred_element_type=jnp.float32
+    )
+    inner_sum = jnp.sum(attend * attend_back, axis=-1, keepdims=True)
+    scores_back = (attend * (attend_back - inner_sum) * scale).astype(jnp.bfloat16)
+    value_back = jnp.einsum(
+        "hij,ihd->jhd", attend_b, mixed_back, preferred_element_type=jnp.float32
+    )
+    value_back = value_back.astype(jnp.bfloat16).reshape(slots, inner)
+    qhat_back = jnp.einsum("hij,jhd->ihd", scores_back, key_b, preferred_element_type=jnp.float32)
+    khat_back = jnp.einsum("hij,ihd->jhd", scores_back, query_b, preferred_element_type=jnp.float32)
+    query_back = (
+        norm_back(qhat_back, query_hat, query_scale).astype(jnp.bfloat16).reshape(slots, inner)
+    )
+    key_back = norm_back(khat_back, key_hat, key_scale).astype(jnp.bfloat16).reshape(slots, inner)
+    mixed_late, query_back, key_back, value_back = lax.optimization_barrier(
+        (mixed, query_back, key_back, value_back)
+    )
     contributions = lax.dot_general(
-        mixed.reshape(n_ctx, capacity, inner),
+        mixed_late.reshape(n_ctx, capacity, inner),
         w_out,
         (((2,), (0,)), ((), ())),
         preferred_element_type=jnp.float32,
@@ -116,32 +138,12 @@
     )
     router_high = router_group.astype(jnp.bfloat16)
     router_low = (router_group - router_high.astype(jnp.float32)).astype(jnp.bfloat16)
-    mixed_back = lax.dot_general(
-        chunk_delta, w_out, (((2,), (1,)), ((), ())), preferred_element_type=jnp.float32
-    )
-    mixed_back = mixed_back.astype(jnp.bfloat16).reshape(slots, heads_here, HDIM)
-    attend_back = jnp.einsum(
-        "ihd,jhd->hij", mixed_back, value_b, preferred_element_type=jnp.float32
-    )
-    inner_sum = jnp.sum(attend * attend_back, axis=-1, keepdims=True)
-    scores_back = (attend * (attend_back - inner_sum) * scale).astype(jnp.bfloat16)
-    value_back = jnp.einsum(
-        "hij,ihd->jhd", attend_b, mixed_back, preferred_element_type=jnp.float32
-    )
-    value_back = value_back.astype(jnp.bfloat16).reshape(slots, inner)
-    qhat_back = jnp.einsum("hij,jhd->ihd", scores_back, key_b, preferred_element_type=jnp.float32)
-    khat_back = jnp.einsum("hij,ihd->jhd", scores_back, query_b, preferred_element_type=jnp.float32)
-    query_back = (
-        norm_back(qhat_back, query_hat, query_scale).astype(jnp.bfloat16).reshape(slots, inner)
-    )
-    key_back = norm_back(khat_back, key_hat, key_scale).astype(jnp.bfloat16).reshape(slots, inner)
     factors = lax.all_gather(
         jnp.concatenate(
             [
                 query_back,
                 key_back,
                 value_back,
-                mixed,
             ],
             axis=0,
         ),
@@ -161,7 +163,24 @@
     grad_query = contract(normed_blocks, gathered(0))
     grad_key = contract(normed_blocks, gathered(1))
     grad_value = contract(normed_blocks, gathered(2))
-    grad_out = contract(gathered(3), delta_blocks)
+    dp_index = lax.axis_index("dp")
+    delta_by_seq = delta_blocks.reshape(n_dp, slots, block)
+    out_total = lax.dot_general(
+        mixed,
+        lax.dynamic_index_in_dim(delta_by_seq, dp_index, 0, keepdims=False),
+        (((0,), (0,)), ((), ())),
+        preferred_element_type=jnp.float32,
+    )
+    for shift in range(1, n_dp):
+        arrived = lax.ppermute(mixed, "dp", [(i, (i + shift) % n_dp) for i in range(n_dp)])
+        source = (dp_index + n_dp - shift) % n_dp
+        out_total = out_total + lax.dot_general(
+            arrived,
+            lax.dynamic_index_in_dim(delta_by_seq, source, 0, keepdims=False),
+            (((0,), (0,)), ((), ())),
+            preferred_element_type=jnp.float32,
+        )
+    grad_out = out_total.astype(jnp.bfloat16)
     router_pieces = lax.all_gather(
         jnp.stack([router_high, router_low]), "dp", axis=0, tiled=False
     ).astype(jnp.float32)

time: 186 us -> 174 us (0.935)
  waiting for transfers between devices: 30.4 us -> 25.2 us
  starting transfers between devices: 4.21 us -> 9.37 us
  local copies, waits for them, and re-layouts: 25.8 us -> 20.9 us
  matrix products: 55.4 us -> 50.6 us
    all_gather x1, waiting for transfers between devices: 8.66 us -> 0.01 us  [body(): lax.all_gather(jnp.concatenate([query_back, key_back, value_back], axis=0...]
    dot_general x1 -> x5, matrix products: 5.7 us -> 11.6 us  [the longest x1 5.71 us: body(): lax.dot_general(mixed_late.reshape(n_ctx, capacity, inner), w_out, (((2,)...]
    dynamic_slice x0 -> x1, local copies, waits for them, and re-layouts: none -> 5.04 us  [body(): lax.dynamic_index_in_dim(delta_by_seq, source, 0, keepdims=False)]
    ppermute x0 -> x3, starting transfers between devices: none -> 4.49 us  [body(): lax.ppermute(mixed, 'dp', [(i, (i + shift) % n_dp) for i in range(n_dp)])]
    reshape x1, local copies, waits for them, and re-layouts: 4.05 us -> 0.04 us  [body(): mixed_late.reshape(n_ctx, capacity, inner)]
    all_to_all x1, waiting for transfers between devices: 0.01 us -> 3.41 us  [body(): received = lax.all_to_all(contributions, 'ctx', 0, 0, tiled=True)]
    dot_general x1, matrix products: 3.28 us -> 0.69 us  [body(): jnp.einsum('hij,jhd->ihd', scores_back, key_b, preferred_element_type=jnp...]
    dot_general x4 -> x3, matrix products: 10.3 us -> 7.73 us  [contract(): lax.dot_general(left, right, (((0,), (0,)), ((), ())), preferred_element_...]
  transfers between devices with their start and end apart: 4 -> 7, of which waited for: 2 -> 2; matrix products, arithmetic and copies ran while one was open for 39% -> 37% of each run, Pallas kernels for 0% -> 0%
where the time goes in v5:
time: 174 us; the launch traced here: 172 us
  matrix products  50.6 us (29%)
  blocking collectives  41.4 us (24%)
  waiting for transfers between devices  25.2 us (14%)
  local copies, waits for them, and re-layouts  20.9 us (12%)
  between operations  14.8 us (9%)
  other arithmetic  9.49 us (5%)
  starting transfers between devices  9.37 us (5%)
    all_gather x1, waiting for transfers between devices, body(): lax.all_gather(jnp.concatenate([normed, delta, flag_cols], axis=1), 'ctx'...  21.7 us
    all_to_all x1, blocking collectives, body(): lax.all_to_all(jnp.concatenate([normed, delta], axis=0), 'dp', 1, 0, tile...  18.6 us
    dot_general x3, matrix products, project(): lax.dot_general(chunk_normed, weight, (((2,), (0,)), ((), ())), preferred...  14.8 us
    all_gather x1, blocking collectives, body(): lax.all_gather(jnp.stack([router_high, router_low]), 'dp', axis=0, tiled=...  13.6 us
    all_gather x1, blocking collectives, body(): lax.all_gather(router_split, 'ctx', axis=0, tiled=False).astype(jnp.float32)  9.27 us
    dot_general x3, matrix products, contract(): lax.dot_general(left, right, (((0,), (0,)), ((), ())), preferred_element_...  7.73 us
    dot_general x1, matrix products, body(): lax.dot_general(chunk_delta, w_out, (((2,), (1,)), ((), ())), preferred_e...  6.34 us
    dot_general x1, matrix products, body(): lax.dot_general(mixed_late.reshape(n_ctx, capacity, inner), w_out, (((2,)...  5.71 us
  transfers between devices with their start and end apart: 7, of which 2 were waited for; matrix products, arithmetic and copies ran while one was open for 37% of the time, Pallas kernels for 0%

profile of v5, /device:TPU:2, one launch (start us, length us, event | category | flops | bytes accessed | tf_op | source)
XLA Modules:
  0.0 171.8 jit_solution(2881763374839805336)
XLA Ops:
  7.2 0.6 compare_reduce_fusion.1
  8.5 0.7 compare_and_fusion
  9.2 1.9 %multiply_reduce_fusion.2 = (f32[20]{0:T(128)S(1)}, f32[20,6144]{1,0:T(8,128)S(1)}) fusion(bf16[1,128,6144]{2,1,0:T(8,128)(2,1)} %param.11, s32[20]{0:T(128)S(1)} %bitcast.153, pred[20]{0:T(512)(128)(4,1)S(1)} %get-tuple-element.28), kind=kOutput, calls=%fused_computation.63 | convolution fusion | flops 31708140 | bytes 2064564 | tf_op jit(solution)/shard_map/dot_general | solution.py:41
  11.1 1.4 fusion.44
  12.6 0.1 multiply_convert_fusion.1
  12.7 0.1 copy.105
  12.8 0.1 copy.106
  12.9 1.2 multiply_convert_fusion
  14.1 0.7 fusion.92
  14.8 0.9 fusion.50
  15.7 0.1 pad_maximum_fusion
  15.8 18.6 %all_to_all.21 = bf16[40,4,1536]{2,0,1:T(8,128)(2,1)} all-to-all(bf16[40,4,1536]{2,0,1:T(8,128)(2,1)S(1)} %bitcast.140), channel_id=1, replica_groups=mesh['dp'=4,'ctx'=8] {'dp'}, dimensions={1} | all-to-all | bytes 983040 | tf_op jit(solution)/shard_map/all_to_all | solution.py:60
  34.5 21.7 %all-gather.15.cloned.1.call-done = bf16[8,20,12416]{2,1,0:T(8,128)(2,1)} async-done(((bf16[1,20,12416]{2,1,0:T(8,128)(2,1)}), bf16[8,20,12416]{2,1,0:T(8,128)(2,1)}) %all-gather.15.cloned.1.call-update) | async-done | bytes 3973136 | tf_op jit(solution)/shard_map/all_gather | solution.py:52
  56.2 4.9 %fusion.8 = f32[8,20,512]{2,1,0:T(8,128)S(1)} fusion(bf16[6144,512]{1,0:T(8,128)(2,1)} %param.14, bf16[8,20,12416]{2,1,0:T(8,128)(2,1)} %all-gather.15.cloned.1.call-done), kind=kOutput, calls=%fused_computation.10 | convolution fusion | flops 1006632960 | bytes 8978432 | tf_op jit(solution)/shard_map/dot_general | solution.py:69
  61.1 0.1 reshape_reshape.10
  61.2 0.2 multiply_reduce_fusion.6
  61.5 4.9 %fusion.6 = f32[8,20,512]{2,1,0:T(8,128)S(1)} fusion(bf16[6144,512]{1,0:T(8,128)(2,1)} %param.15, bf16[8,20,12416]{2,1,0:T(8,128)(2,1)} %all-gather.15.cloned.1.call-done), kind=kOutput, calls=%fused_computation.8 | convolution fusion | flops 1006632960 | bytes 8978432 | tf_op jit(solution)/shard_map/dot_general | solution.py:69
  66.4 0.1 reshape_reshape.11
  66.6 0.2 multiply_reduce_fusion.5
  66.8 0.1 copy.109
  66.9 1.0 compare_reduce_fusion
  67.9 0.1 gt.16
  68.0 4.9 %fusion.29 = bf16[8,20,512]{2,1,0:T(8,128)(2,1)S(1)} fusion(bf16[6144,512]{1,0:T(8,128)(2,1)} %param.16, bf16[8,20,12416]{2,1,0:T(8,128)(2,1)} %all-gather.15.cloned.1.call-done), kind=kOutput, calls=%fused_computation.43 | convolution fusion | flops 1006714880 | bytes 8814592 | tf_op jit(solution)/shard_map/dot_general | solution.py:69
  73.0 0.1 fusion.73
  73.1 0.4 fusion.63
  73.6 0.3 fusion.39
  73.9 1.5 collective-permute-start
  75.5 2.3 %collective-permute-start.2 = (bf16[160,512]{1,0:T(8,128)(2,1)S(1)}, bf16[160,512]{1,0:T(8,128)(2,1)}, u32[]{:S(2)}, u32[]{:S(2)}) collective-permute-start(bf16[160,512]{1,0:T(8,128)(2,1)S(1)} %bitcast.142), channel_id=1, source_target_pairs={{0,24},{8,0},{16,8},{24,16},{1,25},{9,1},{17,9},{25,17},{2,26},{10... | collective-permute-start | bytes 491528 | tf_op jit(solution)/shard_map/ppermute | solution.py:175
  77.8 0.6 collective-permute-start.1
  78.4 6.3 %fusion.34 = bf16[8,20,512]{2,1,0:T(8,128)(2,1)S(1)} fusion(bf16[512,6144]{1,0:T(8,128)(2,1)} %param.17, bf16[8,20,12416]{2,1,0:T(8,128)(2,1)} %all-gather.15.cloned.1.call-done), kind=kOutput, calls=%fused_computation.44 | convolution fusion | flops 1006714880 | bytes 8814592 | tf_op jit(solution)/shard_map/dot_general | solution.py:91
  84.8 0.2 fusion.40
  85.1 0.3 fusion.76
  85.3 0.5 multiply_reduce_fusion.3
  85.9 0.7 multiply_reduce_fusion.4
  86.6 0.2 copy_bitcast_fusion.2
  86.8 0.2 copy_bitcast_fusion.3
  87.1 5.7 %convolution_convert_fusion = bf16[8,20,6144]{2,1,0:T(8,128)(2,1)} fusion(bf16[8,20,512]{2,1,0:T(8,128)(2,1)S(1)} %reshape.220, bf16[512,6144]{1,0:T(8,128)(2,1)} %param.17), kind=kOutput, calls=%fused_computation.1 | convolution fusion | flops 1007616000 | bytes 8421376 | tf_op jit(solution)/shard_map/dot_general | solution.py:113
  92.8 4.8 %all-to-all-start = ((bf16[8,20,6144]{2,1,0:T(8,128)(2,1)}), bf16[8,20,6144]{2,1,0:T(8,128)(2,1)}, u32[]{:S(2)}, u32[]{:S(2)}) async-start(bf16[8,20,6144]{2,1,0:T(8,128)(2,1)} %convolution_convert_fusion), calls=%async_computation | async-start | bytes 4718592 | tf_op jit(solution)/shard_map/all_to_all | solution.py:119
  97.6 0.8 pad_maximum_fusion.1
  98.5 4.3 %copy.122 = bf16[8,160,1536]{2,0,1:T(8,128)(2,1)S(1)} copy(bf16[8,160,1536]{2,1,0:T(8,128)(2,1)} %all-gather.11.cloned.1.call-done) | data formatting | bytes 7864320 | tf_op jit(solution)/shard_map/all_gather | solution.py:63
  102.8 0.3 slice_bitcast_fusion
  103.0 1.5 copy.124
  104.6 5.0 %constant_dynamic-slice_fusion.1 = (bf16[1,160,1536]{2,0,1:T(2,128)(2,1)}, bf16[1,160,1536]{2,0,1:T(2,128)(2,1)}, bf16[1,160,1536]{2,0,1:T(2,128)(2,1)S(1)}, bf16[1,160,1536]{2,0,1:T(2,128)(2,1)S(1)}) fusion(bf16[4,160,1536]{2,0,1:T(4,128)(2,1)S(1)} %bitcast.135, s32[]{:T(128)S(6)} %select_n.37, s32[]{:T(128)S(6)} %select_n.39, s32[]{:T(128)S(6)} %select_n.35, ...), kind=kLoop, calls=%fused_computation.139 | loop fusion | bytes 3932176 | tf_op jit(solution)/shard_map/jit(dynamic_index_in_dim)/dynamic_slice | solution.py:179
  109.6 0.6 fusion.59
  110.2 0.7 copy-done.8
  110.9 1.5 convolution_add_fusion.2
  112.4 2.0 %copy.123 = bf16[4,8,20,1536]{3,2,1,0:T(8,128)(2,1)} copy(bf16[4,8,20,1536]{3,1,2,0:T(8,128)(2,1)S(1)} %get-tuple-element.31) | data formatting | bytes 3932160 | tf_op jit(solution)/shard_map/transpose | solution.py:66
  114.5 4.0 %reshape.222 = bf16[640,1536]{1,0:T(8,128)(2,1)} reshape(bf16[4,8,20,1536]{3,2,1,0:T(8,128)(2,1)} %copy.123) | data formatting | bytes 3932160 | tf_op jit(solution)/shard_map/reshape | solution.py:66
  118.4 2.0 %fusion.52 = f32[512,1536]{1,0:T(8,128)S(1)} fusion(bf16[160,512]{1,0:T(8,128)(2,1)} %collective-permute-done.2, bf16[1,160,1536]{2,0,1:T(2,128)(2,1)} %get-tuple-element.33), kind=kOutput, calls=%fused_computation.67 | convolution fusion | flops 251658240 | bytes 3801088 | tf_op jit(solution)/shard_map/dot_general | solution.py:177
  120.5 1.8 %fusion.13 = bf16[512,1536]{1,0:T(8,128)(2,1)} fusion(f32[512,1536]{1,0:T(8,128)S(1)} %fusion.52, f32[512,1536]{1,0:T(8,128)S(1)} %convolution_add_fusion.2, bf16[160,512]{1,0:T(8,128)(2,1)S(1)} %collective-permute-done.1, bf16[1,160,1536]{2,0,1:T(2,128)(2,1)S(1)} %copy-done.6), kind=kOutput, calls=%fused_computation.18 | convolution fusion | flops 254017536 | bytes 8519680 | tf_op jit(solution)/shard_map/dot_general | solution.py:177
  122.3 3.4 %all-to-all-done = bf16[8,20,6144]{2,1,0:T(8,128)(2,1)} async-done(((bf16[8,20,6144]{2,1,0:T(8,128)(2,1)}), bf16[8,20,6144]{2,1,0:T(8,128)(2,1)}, u32[]{:S(2)}, u32[]{:S(2)}) %all-to-all-start) | async-done | bytes 1966112 | tf_op jit(solution)/shard_map/all_to_all | solution.py:119
  125.7 2.1 %convert_reduce_fusion = f32[20,6144]{1,0:T(8,128)S(1)} fusion(bf16[8,20,6144]{2,1,0:T(8,128)(2,1)} %all-to-all-done), kind=kLoop, calls=%fused_computation.14 | loop fusion | flops 1843200 | bytes 2457600 | tf_op jit(solution)/shard_map/reduce_sum | solution.py:122
  127.8 0.2 multiply_reduce_fusion.1
  128.0 0.4 fusion.99
  128.6 9.3 %all-gather.5 = bf16[8,2,6144]{2,1,0:T(2,128)(2,1)S(1)} all-gather(bf16[1,2,6144]{2,1,0:T(2,128)(2,1)S(1)} %maximum_bitcast_fusion), channel_id=4, replica_groups=mesh['dp'=4,'ctx'=8] {'ctx'}, dimensions={0}, use_global_device_ids=true | all-gather | bytes 221184 | tf_op jit(solution)/shard_map/all_gather | solution.py:137
  137.8 0.2 convert_reduce_fusion.1
  138.2 13.6 %all-gather.6 = bf16[4,2,6144]{2,1,0:T(2,128)(2,1)S(1)} all-gather(bf16[1,2,6144]{2,1,0:T(2,128)(2,1)S(1)} %maximum_bitcast_fusion.1), channel_id=5, replica_groups=mesh['dp'=4,'ctx'=8] {'dp'}, dimensions={0}, use_global_device_ids=true | all-gather | bytes 122880 | tf_op jit(solution)/shard_map/all_gather | solution.py:184
  151.8 0.8 fusion.80
  152.6 2.8 %fusion.2 = bf16[1,128,6144]{2,1,0:T(8,128)(2,1)} fusion(bf16[1,128,6144]{2,1,0:T(8,128)(2,1)S(1)} %copy-done.4, f32[20,6144]{1,0:T(8,128)S(1)} %convert_reduce_fusion, f32[20]{0:T(128)S(1)} %fusion.44, s32[20]{0:T(128)S(1)} %bitcast.155, pred[20]{0:T(512)(128)(4,1)S(1)} %get-tuple-element.28), kind=kOutput, calls=%fused_computation.4 | convolution fusion | flops 191230976 | bytes 3637428 | tf_op jit(solution)/shard_map/dot_general | solution.py:124
  155.4 1.8 %fusion.110 = (bf16[4,160,512]{2,1,0:T(8,128)(2,1)S(1)}, bf16[4,160,512]{2,1,0:T(8,128)(2,1)S(1)}, bf16[4,160,512]{2,1,0:T(8,128)(2,1)S(1)}) fusion(bf16[4,480,512]{2,1,0:T(8,128)(2,1)} %bitcast.137), kind=kLoop, calls=%fused_computation.155 | loop fusion | bytes 3932160 | tf_op jit(solution)/shard_map/slice | solution.py:156
  157.2 0.4 copy-done.7
  157.6 2.6 %convolution_convert_fusion.1 = bf16[1536,512]{1,0:T(8,128)(2,1)} fusion(bf16[640,1536]{1,0:T(8,128)(2,1)S(1)} %copy-done.7, bf16[640,512]{1,0:T(8,128)(2,1)S(1)} %bitcast.148), kind=kOutput, calls=%fused_computation.19 | convolution fusion | flops 1007419392 | bytes 4194304 | tf_op jit(solution)/shard_map/dot_general | solution.py:159
  160.2 2.6 %convolution_convert_fusion.2 = bf16[1536,512]{1,0:T(8,128)(2,1)} fusion(bf16[640,1536]{1,0:T(8,128)(2,1)S(1)} %copy-done.7, bf16[640,512]{1,0:T(8,128)(2,1)S(1)} %bitcast.147), kind=kOutput, calls=%fused_computation.20 | convolution fusion | flops 1007419392 | bytes 4194304 | tf_op jit(solution)/shard_map/dot_general | solution.py:159
  162.7 2.6 %convolution_convert_fusion.3 = bf16[1536,512]{1,0:T(8,128)(2,1)} fusion(bf16[640,1536]{1,0:T(8,128)(2,1)S(1)} %copy-done.7, bf16[640,512]{1,0:T(8,128)(2,1)S(1)} %bitcast.146), kind=kOutput, calls=%fused_computation.21 | convolution fusion | flops 1007419392 | bytes 4194304 | tf_op jit(solution)/shard_map/dot_general | solution.py:159
  (47 shorter events, 0.8 us)
Async XLA Ops:
  7.2 5.8 %copy-start = (bf16[1,128,6144]{2,1,0:T(8,128)(2,1)S(1)}, bf16[1,128,6144]{2,1,0:T(8,128)(2,1)}, u32[]{:S(2)}) copy-start(bf16[1,128,6144]{2,1,0:T(8,128)(2,1)} %param.12) | copy-start | bytes 4718596
  7.2 49.0 %all-gather.15.cloned.1.call-start = ((), (), s32[]{:S(2)}) async-start(), calls=%async_computation.4 | async-start | bytes 5363712 | tf_op jit(solution)/shard_map/all_gather | solution.py:52
  11.1 1.5 copy-start.2
  15.7 82.8 %all-gather.11.cloned.1.call-start = ((), (), s32[]{:S(2)}) async-start(), calls=%async_computation.2 | async-start | bytes 4423680 | tf_op jit(solution)/shard_map/all_gather | solution.py:63
  73.9 36.3 %collective-permute-start = (bf16[160,512]{1,0:T(8,128)(2,1)S(1)}, bf16[160,512]{1,0:T(8,128)(2,1)S(1)}, u32[]{:S(2)}, u32[]{:S(2)}) collective-permute-start(bf16[160,512]{1,0:T(8,128)(2,1)S(1)} %bitcast.141), channel_id=1, source_target_pairs={{0,8},{8,16},{16,24},{24,0},{1,9},{9,17},{17,25},{25,1},{2,10},{10... | collective-permute-start | bytes 491528 | tf_op jit(solution)/shard_map/ppermute | solution.py:175
  75.5 43.0 %collective-permute-start.2 = (bf16[160,512]{1,0:T(8,128)(2,1)S(1)}, bf16[160,512]{1,0:T(8,128)(2,1)}, u32[]{:S(2)}, u32[]{:S(2)}) collective-permute-start(bf16[160,512]{1,0:T(8,128)(2,1)S(1)} %bitcast.142), channel_id=1, source_target_pairs={{0,24},{8,0},{16,8},{24,16},{1,25},{9,1},{17,9},{25,17},{2,26},{10... | collective-permute-start | bytes 491528 | tf_op jit(solution)/shard_map/ppermute | solution.py:175
  77.8 42.6 %collective-permute-start.1 = (bf16[160,512]{1,0:T(8,128)(2,1)S(1)}, bf16[160,512]{1,0:T(8,128)(2,1)S(1)}, u32[]{:S(2)}, u32[]{:S(2)}) collective-permute-start(bf16[160,512]{1,0:T(8,128)(2,1)S(1)} %bitcast.143), channel_id=1, source_target_pairs={{0,16},{8,24},{16,0},{24,8},{1,17},{9,25},{17,1},{25,9},{2,18},{10... | collective-permute-start | bytes 491528 | tf_op jit(solution)/shard_map/ppermute | solution.py:175
  92.8 32.9 %all-to-all-start = ((bf16[8,20,6144]{2,1,0:T(8,128)(2,1)}), bf16[8,20,6144]{2,1,0:T(8,128)(2,1)}, u32[]{:S(2)}, u32[]{:S(2)}) async-start(bf16[8,20,6144]{2,1,0:T(8,128)(2,1)} %convolution_convert_fusion), calls=%async_computation | async-start | bytes 4718592 | tf_op jit(solution)/shard_map/all_to_all | solution.py:119
  97.6 57.8 %all-gather.13.cloned.1.call-start = ((), (), s32[]{:S(2)}) async-start(), calls=%async_computation.3 | async-start | bytes 2457600 | tf_op jit(solution)/shard_map/all_gather | solution.py:141
  110.2 0.7 copy-start.8
  118.4 2.0 %copy-start.6 = (bf16[1,160,1536]{2,0,1:T(2,128)(2,1)S(1)}, bf16[1,160,1536]{2,0,1:T(2,128)(2,1)}, u32[]{:S(2)}) copy-start(bf16[1,160,1536]{2,0,1:T(2,128)(2,1)} %get-tuple-element.32) | copy-start | bytes 1474564
  122.3 5.5 %copy-start.5 = (f32[20,6144]{1,0:T(8,128)S(1)}, f32[20,6144]{1,0:T(8,128)}, u32[]{:S(2)}) copy-start(f32[20,6144]{1,0:T(8,128)} %get-tuple-element.42) | copy-start | bytes 1474564
  122.3 5.8 %copy-start.3 = (f32[20,6144]{1,0:T(8,128)S(1)}, f32[20,6144]{1,0:T(8,128)}, u32[]{:S(2)}) copy-start(f32[20,6144]{1,0:T(8,128)} %copy-done.2) | copy-start | bytes 1474564
  127.8 24.8 %copy-start.4 = (bf16[1,128,6144]{2,1,0:T(8,128)(2,1)S(1)}, bf16[1,128,6144]{2,1,0:T(8,128)(2,1)}, u32[]{:S(2)}) copy-start(bf16[1,128,6144]{2,1,0:T(8,128)(2,1)} %param.11) | copy-start | bytes 4718596
  155.4 2.1 %copy-start.7 = (bf16[640,1536]{1,0:T(8,128)(2,1)S(1)}, bf16[640,1536]{1,0:T(8,128)(2,1)}, u32[]{:S(2)}) copy-start(bf16[640,1536]{1,0:T(8,128)(2,1)} %reshape.222) | copy-start | bytes 5898244
  162.7 2.6 %copy-start.1 = (bf16[1,128,6144]{2,1,0:T(8,128)(2,1)S(1)}, bf16[1,128,6144]{2,1,0:T(8,128)(2,1)}, u32[]{:S(2)}) copy-start(bf16[1,128,6144]{2,1,0:T(8,128)(2,1)} %param.12) | copy-start | bytes 4718596
Sparse Core Ops, SparseCore 0:
  15.8 40.3 all-gather.14
  58.0 35.6 all-gather.10
  100.0 43.6 all-gather.12

commit v6 on v5

--- a/solution.py
+++ b/solution.py
@@ -181,9 +181,16 @@
             preferred_element_type=jnp.float32,
         )
     grad_out = out_total.astype(jnp.bfloat16)
-    router_pieces = lax.all_gather(
-        jnp.stack([router_high, router_low]), "dp", axis=0, tiled=False
-    ).astype(jnp.float32)
+    router_pair = jnp.stack([router_high, router_low])
+    router_pieces = lax.dynamic_update_index_in_dim(
+        jnp.zeros((n_dp,) + router_pair.shape, jnp.bfloat16), router_pair, dp_index, 0
+    )
+    for shift in range(1, n_dp):
+        arrived = lax.ppermute(router_pair, "dp", [(i, (i + shift) % n_dp) for i in range(n_dp)])
+        router_pieces = lax.dynamic_update_index_in_dim(
+            router_pieces, arrived, (dp_index + n_dp - shift) % n_dp, 0
+        )
+    router_pieces = router_pieces.astype(jnp.float32)
     grad_router = jnp.sum(router_pieces[:, 0] + router_pieces[:, 1], axis=0)
     return (layer_out, grad_query, grad_key, grad_value, grad_out, grad_router)
 

time: 174 us -> 167 us (0.960)
  blocking collectives: 41.4 us -> 27.8 us
  starting transfers between devices: 9.37 us -> 14.8 us
    all_gather x1 -> x0, blocking collectives: 13.6 us -> none  [body(): lax.all_gather(jnp.stack([router_high, router_low]), 'dp', axis=0, tiled=...]
    ppermute x0 -> x3, starting transfers between devices: none -> 5.4 us  [body(): lax.ppermute(router_pair, 'dp', [(i, (i + shift) % n_dp) for i in range(n...]
  transfers between devices with their start and end apart: 7 -> 10, of which waited for: 2 -> 2; matrix products, arithmetic and copies ran while one was open for 37% -> 39% of each run, Pallas kernels for 0% -> 0%
where the time goes in v6:
time: 167 us; the launch traced here: 165 us
  matrix products  50.6 us (30%)
  blocking collectives  27.8 us (17%)
  waiting for transfers between devices  25.2 us (15%)
  local copies, waits for them, and re-layouts  21.9 us (13%)
  between operations  14.9 us (9%)
  starting transfers between devices  14.8 us (9%)
  other arithmetic  9.4 us (6%)
    all_gather x1, waiting for transfers between devices, body(): lax.all_gather(jnp.concatenate([normed, delta, flag_cols], axis=1), 'ctx'...  21.7 us
    all_to_all x1, blocking collectives, body(): lax.all_to_all(jnp.concatenate([normed, delta], axis=0), 'dp', 1, 0, tile...  18.6 us
    dot_general x3, matrix products, project(): lax.dot_general(chunk_normed, weight, (((2,), (0,)), ((), ())), preferred...  14.8 us
    all_gather x1, blocking collectives, body(): lax.all_gather(router_split, 'ctx', axis=0, tiled=False).astype(jnp.float32)  9.27 us
    dot_general x3, matrix products, contract(): lax.dot_general(left, right, (((0,), (0,)), ((), ())), preferred_element_...  7.73 us
    dot_general x1, matrix products, body(): lax.dot_general(chunk_delta, w_out, (((2,), (1,)), ((), ())), preferred_e...  6.34 us
    dot_general x1, matrix products, body(): lax.dot_general(mixed_late.reshape(n_ctx, capacity, inner), w_out, (((2,)...  5.71 us
    ppermute x3, starting transfers between devices, body(): lax.ppermute(router_pair, 'dp', [(i, (i + shift) % n_dp) for i in range(n...  5.4 us
  transfers between devices with their start and end apart: 10, of which 2 were waited for; matrix products, arithmetic and copies ran while one was open for 39% of the time, Pallas kernels for 0%

profile of v6, /device:TPU:2, one launch (start us, length us, event | category | flops | bytes accessed | tf_op | source)
XLA Modules:
  0.0 164.6 jit_solution(12185821407023662923)
XLA Ops:
  7.2 0.6 compare_reduce_fusion.1
  8.5 0.7 compare_and_fusion
  9.2 1.9 %multiply_reduce_fusion.2 = (f32[20]{0:T(128)S(1)}, f32[20,6144]{1,0:T(8,128)S(1)}) fusion(bf16[1,128,6144]{2,1,0:T(8,128)(2,1)} %param.11, s32[20]{0:T(128)S(1)} %bitcast.159, pred[20]{0:T(512)(128)(4,1)S(1)} %get-tuple-element.28), kind=kOutput, calls=%fused_computation.63 | convolution fusion | flops 31708140 | bytes 2064564 | tf_op jit(solution)/shard_map/dot_general | solution.py:41
  11.1 1.4 fusion.44
  12.7 0.1 copy.156
  12.8 0.1 copy.157
  12.9 1.2 multiply_convert_fusion
  14.1 0.7 fusion.92
  14.8 0.9 fusion.50
  15.8 18.6 %all_to_all.21 = bf16[40,4,1536]{2,0,1:T(8,128)(2,1)} all-to-all(bf16[40,4,1536]{2,0,1:T(8,128)(2,1)S(1)} %bitcast.143), channel_id=1, replica_groups=mesh['dp'=4,'ctx'=8] {'dp'}, dimensions={1} | all-to-all | bytes 983040 | tf_op jit(solution)/shard_map/all_to_all | solution.py:60
  34.5 21.7 %all-gather.13.cloned.1.call-done = bf16[8,20,12416]{2,1,0:T(8,128)(2,1)} async-done(((bf16[1,20,12416]{2,1,0:T(8,128)(2,1)}), bf16[8,20,12416]{2,1,0:T(8,128)(2,1)}) %all-gather.13.cloned.1.call-update) | async-done | bytes 3973136 | tf_op jit(solution)/shard_map/all_gather | solution.py:52
  56.2 4.9 %fusion.8 = f32[8,20,512]{2,1,0:T(8,128)S(1)} fusion(bf16[6144,512]{1,0:T(8,128)(2,1)} %param.14, bf16[8,20,12416]{2,1,0:T(8,128)(2,1)} %all-gather.13.cloned.1.call-done), kind=kOutput, calls=%fused_computation.10 | convolution fusion | flops 1006632960 | bytes 8978432 | tf_op jit(solution)/shard_map/dot_general | solution.py:69
  61.1 0.1 reshape_reshape.10
  61.2 0.2 multiply_reduce_fusion.6
  61.5 4.9 %fusion.6 = f32[8,20,512]{2,1,0:T(8,128)S(1)} fusion(bf16[6144,512]{1,0:T(8,128)(2,1)} %param.15, bf16[8,20,12416]{2,1,0:T(8,128)(2,1)} %all-gather.13.cloned.1.call-done), kind=kOutput, calls=%fused_computation.8 | convolution fusion | flops 1006632960 | bytes 8978432 | tf_op jit(solution)/shard_map/dot_general | solution.py:69
  66.4 0.1 reshape_reshape.11
  66.6 0.2 multiply_reduce_fusion.5
  66.9 1.0 compare_reduce_fusion
  68.0 4.9 %fusion.29 = bf16[8,20,512]{2,1,0:T(8,128)(2,1)S(1)} fusion(bf16[6144,512]{1,0:T(8,128)(2,1)} %param.16, bf16[8,20,12416]{2,1,0:T(8,128)(2,1)} %all-gather.13.cloned.1.call-done), kind=kOutput, calls=%fused_computation.43 | convolution fusion | flops 1006714880 | bytes 8814592 | tf_op jit(solution)/shard_map/dot_general | solution.py:69
  73.1 0.4 fusion.63
  73.6 0.3 fusion.39
  73.9 1.5 collective-permute-start
  75.5 2.3 %collective-permute-start.2 = (bf16[160,512]{1,0:T(8,128)(2,1)S(1)}, bf16[160,512]{1,0:T(8,128)(2,1)}, u32[]{:S(2)}, u32[]{:S(2)}) collective-permute-start(bf16[160,512]{1,0:T(8,128)(2,1)S(1)} %bitcast.145), channel_id=1, source_target_pairs={{0,24},{8,0},{16,8},{24,16},{1,25},{9,1},{17,9},{25,17},{2,26},{10... | collective-permute-start | bytes 491528 | tf_op jit(solution)/shard_map/ppermute | solution.py:175
  77.8 0.6 collective-permute-start.1
  78.4 6.3 %fusion.34 = bf16[8,20,512]{2,1,0:T(8,128)(2,1)S(1)} fusion(bf16[512,6144]{1,0:T(8,128)(2,1)} %param.17, bf16[8,20,12416]{2,1,0:T(8,128)(2,1)} %all-gather.13.cloned.1.call-done), kind=kOutput, calls=%fused_computation.44 | convolution fusion | flops 1006714880 | bytes 8814592 | tf_op jit(solution)/shard_map/dot_general | solution.py:91
  84.8 0.2 fusion.40
  85.1 0.3 fusion.76
  85.3 0.5 multiply_reduce_fusion.3
  85.9 0.7 multiply_reduce_fusion.4
  86.6 0.2 copy_bitcast_fusion.2
  86.8 0.2 copy_bitcast_fusion.3
  87.1 5.7 %convolution_convert_fusion = bf16[8,20,6144]{2,1,0:T(8,128)(2,1)} fusion(bf16[8,20,512]{2,1,0:T(8,128)(2,1)S(1)} %reshape.220, bf16[512,6144]{1,0:T(8,128)(2,1)} %param.17), kind=kOutput, calls=%fused_computation.1 | convolution fusion | flops 1007616000 | bytes 8421376 | tf_op jit(solution)/shard_map/dot_general | solution.py:113
  92.8 4.8 %all-to-all-start = ((bf16[8,20,6144]{2,1,0:T(8,128)(2,1)}), bf16[8,20,6144]{2,1,0:T(8,128)(2,1)}, u32[]{:S(2)}, u32[]{:S(2)}) async-start(bf16[8,20,6144]{2,1,0:T(8,128)(2,1)} %convolution_convert_fusion), calls=%async_computation | async-start | bytes 4718592 | tf_op jit(solution)/shard_map/all_to_all | solution.py:119
  97.6 0.8 pad_maximum_fusion.1
  98.5 4.3 %copy.173 = bf16[8,160,1536]{2,0,1:T(8,128)(2,1)S(1)} copy(bf16[8,160,1536]{2,1,0:T(8,128)(2,1)} %all-gather.9.cloned.1.call-done) | data formatting | bytes 7864320 | tf_op jit(solution)/shard_map/all_gather | solution.py:63
  102.8 0.3 slice_bitcast_fusion
  103.0 1.5 copy.175
  104.6 5.0 %constant_dynamic-slice_fusion.1 = (bf16[1,160,1536]{2,0,1:T(2,128)(2,1)}, bf16[1,160,1536]{2,0,1:T(2,128)(2,1)}, bf16[1,160,1536]{2,0,1:T(2,128)(2,1)S(1)}, bf16[1,160,1536]{2,0,1:T(2,128)(2,1)S(1)}) fusion(bf16[4,160,1536]{2,0,1:T(4,128)(2,1)S(1)} %bitcast.138, s32[]{:T(128)S(6)} %select_n.48, s32[]{:T(128)S(6)} %select_n.50, s32[]{:T(128)S(6)} %select_n.46, ...), kind=kLoop, calls=%fused_computation.139 | loop fusion | bytes 3932176 | tf_op jit(solution)/shard_map/jit(dynamic_index_in_dim)/dynamic_slice | solution.py:179
  109.6 0.6 fusion.59
  110.2 0.7 copy-done.8
  110.9 1.5 convolution_add_fusion.2
  112.4 2.0 %copy.174 = bf16[4,8,20,1536]{3,2,1,0:T(8,128)(2,1)} copy(bf16[4,8,20,1536]{3,1,2,0:T(8,128)(2,1)S(1)} %get-tuple-element.31) | data formatting | bytes 3932160 | tf_op jit(solution)/shard_map/transpose | solution.py:66
  114.4 4.0 %reshape.222 = bf16[640,1536]{1,0:T(8,128)(2,1)} reshape(bf16[4,8,20,1536]{3,2,1,0:T(8,128)(2,1)} %copy.174) | data formatting | bytes 3932160 | tf_op jit(solution)/shard_map/reshape | solution.py:66
  118.4 2.0 %fusion.52 = f32[512,1536]{1,0:T(8,128)S(1)} fusion(bf16[160,512]{1,0:T(8,128)(2,1)} %collective-permute-done.2, bf16[1,160,1536]{2,0,1:T(2,128)(2,1)} %get-tuple-element.33), kind=kOutput, calls=%fused_computation.67 | convolution fusion | flops 251658240 | bytes 3801088 | tf_op jit(solution)/shard_map/dot_general | solution.py:177
  120.4 1.8 %fusion.13 = bf16[512,1536]{1,0:T(8,128)(2,1)} fusion(f32[512,1536]{1,0:T(8,128)S(1)} %fusion.52, f32[512,1536]{1,0:T(8,128)S(1)} %convolution_add_fusion.2, bf16[160,512]{1,0:T(8,128)(2,1)S(1)} %collective-permute-done.1, bf16[1,160,1536]{2,0,1:T(2,128)(2,1)S(1)} %copy-done.6), kind=kOutput, calls=%fused_computation.18 | convolution fusion | flops 254017536 | bytes 8519680 | tf_op jit(solution)/shard_map/dot_general | solution.py:177
  122.3 3.4 %all-to-all-done = bf16[8,20,6144]{2,1,0:T(8,128)(2,1)} async-done(((bf16[8,20,6144]{2,1,0:T(8,128)(2,1)}), bf16[8,20,6144]{2,1,0:T(8,128)(2,1)}, u32[]{:S(2)}, u32[]{:S(2)}) %all-to-all-start) | async-done | bytes 1966112 | tf_op jit(solution)/shard_map/all_to_all | solution.py:119
  125.7 2.1 %convert_reduce_fusion = f32[20,6144]{1,0:T(8,128)S(1)} fusion(bf16[8,20,6144]{2,1,0:T(8,128)(2,1)} %all-to-all-done), kind=kLoop, calls=%fused_computation.14 | loop fusion | flops 1843200 | bytes 2457600 | tf_op jit(solution)/shard_map/reduce_sum | solution.py:122
  127.8 0.2 multiply_reduce_fusion.1
  128.0 0.4 fusion.99
  128.6 9.3 %all-gather.4 = bf16[8,2,6144]{2,1,0:T(2,128)(2,1)S(1)} all-gather(bf16[1,2,6144]{2,1,0:T(2,128)(2,1)S(1)} %maximum_bitcast_fusion), channel_id=4, replica_groups=mesh['dp'=4,'ctx'=8] {'ctx'}, dimensions={0}, use_global_device_ids=true | all-gather | bytes 221184 | tf_op jit(solution)/shard_map/all_gather | solution.py:137
  137.8 0.2 convert_reduce_fusion.1
  138.1 1.6 collective-permute-start.3
  139.7 1.0 collective-permute-start.4
  140.7 2.8 %collective-permute-start.5 = (bf16[2,6144]{1,0:T(2,128)(2,1)S(1)}, bf16[2,6144]{1,0:T(2,128)(2,1)S(1)}, u32[]{:S(2)}, u32[]{:S(2)}) collective-permute-start(bf16[2,6144]{1,0:T(2,128)(2,1)S(1)} %pad_maximum_fusion.2), channel_id=1, source_target_pairs={{0,24},{8,0},{16,8},{24,16},{1,25},{9,1},{17,9},{25,17},{2,26},{10... | collective-permute-start | bytes 73736 | tf_op jit(solution)/shard_map/ppermute | solution.py:189
  143.6 2.8 %fusion.2 = bf16[1,128,6144]{2,1,0:T(8,128)(2,1)} fusion(bf16[1,128,6144]{2,1,0:T(8,128)(2,1)S(1)} %copy-done.4, f32[20,6144]{1,0:T(8,128)S(1)} %convert_reduce_fusion, f32[20]{0:T(128)S(1)} %fusion.44, s32[20]{0:T(128)S(1)} %bitcast.161, pred[20]{0:T(512)(128)(4,1)S(1)} %get-tuple-element.28), kind=kOutput, calls=%fused_computation.4 | convolution fusion | flops 191230976 | bytes 3637428 | tf_op jit(solution)/shard_map/dot_general | solution.py:124
  146.5 0.3 dynamic_update_slice.13
  147.0 0.3 dynamic_update_slice.14
  147.3 0.3 dynamic_update_slice.15
  147.7 0.3 dynamic_update_slice.16
  148.1 0.7 fusion.80
  148.7 1.6 fusion.110
  150.4 2.6 %convolution_convert_fusion.1 = bf16[1536,512]{1,0:T(8,128)(2,1)} fusion(bf16[640,1536]{1,0:T(8,128)(2,1)S(1)} %copy-done.7, bf16[640,512]{1,0:T(8,128)(2,1)S(1)} %bitcast.151), kind=kOutput, calls=%fused_computation.19 | convolution fusion | flops 1007419392 | bytes 4194304 | tf_op jit(solution)/shard_map/dot_general | solution.py:159
  152.9 2.6 %convolution_convert_fusion.2 = bf16[1536,512]{1,0:T(8,128)(2,1)} fusion(bf16[640,1536]{1,0:T(8,128)(2,1)S(1)} %copy-done.7, bf16[640,512]{1,0:T(8,128)(2,1)S(1)} %bitcast.150), kind=kOutput, calls=%fused_computation.20 | convolution fusion | flops 1007419392 | bytes 4194304 | tf_op jit(solution)/shard_map/dot_general | solution.py:159
  155.5 2.6 %convolution_convert_fusion.3 = bf16[1536,512]{1,0:T(8,128)(2,1)} fusion(bf16[640,1536]{1,0:T(8,128)(2,1)S(1)} %copy-done.7, bf16[640,512]{1,0:T(8,128)(2,1)S(1)} %bitcast.149), kind=kOutput, calls=%fused_computation.21 | convolution fusion | flops 1007419392 | bytes 4194304 | tf_op jit(solution)/shard_map/dot_general | solution.py:159
  (62 shorter events, 1.5 us)
Async XLA Ops:
  7.2 5.8 %copy-start = (bf16[1,128,6144]{2,1,0:T(8,128)(2,1)S(1)}, bf16[1,128,6144]{2,1,0:T(8,128)(2,1)}, u32[]{:S(2)}) copy-start(bf16[1,128,6144]{2,1,0:T(8,128)(2,1)} %param.12) | copy-start | bytes 4718596
  7.2 49.0 %all-gather.13.cloned.1.call-start = ((), (), s32[]{:S(2)}) async-start(), calls=%async_computation.4 | async-start | bytes 5363712 | tf_op jit(solution)/shard_map/all_gather | solution.py:52
  11.1 1.5 copy-start.2
  15.7 82.8 %all-gather.9.cloned.1.call-start = ((), (), s32[]{:S(2)}) async-start(), calls=%async_computation.2 | async-start | bytes 4423680 | tf_op jit(solution)/shard_map/all_gather | solution.py:63
  73.9 36.3 %collective-permute-start = (bf16[160,512]{1,0:T(8,128)(2,1)S(1)}, bf16[160,512]{1,0:T(8,128)(2,1)S(1)}, u32[]{:S(2)}, u32[]{:S(2)}) collective-permute-start(bf16[160,512]{1,0:T(8,128)(2,1)S(1)} %bitcast.144), channel_id=1, source_target_pairs={{0,8},{8,16},{16,24},{24,0},{1,9},{9,17},{17,25},{25,1},{2,10},{10... | collective-permute-start | bytes 491528 | tf_op jit(solution)/shard_map/ppermute | solution.py:175
  75.5 43.0 %collective-permute-start.2 = (bf16[160,512]{1,0:T(8,128)(2,1)S(1)}, bf16[160,512]{1,0:T(8,128)(2,1)}, u32[]{:S(2)}, u32[]{:S(2)}) collective-permute-start(bf16[160,512]{1,0:T(8,128)(2,1)S(1)} %bitcast.145), channel_id=1, source_target_pairs={{0,24},{8,0},{16,8},{24,16},{1,25},{9,1},{17,9},{25,17},{2,26},{10... | collective-permute-start | bytes 491528 | tf_op jit(solution)/shard_map/ppermute | solution.py:175
  77.8 42.6 %collective-permute-start.1 = (bf16[160,512]{1,0:T(8,128)(2,1)S(1)}, bf16[160,512]{1,0:T(8,128)(2,1)S(1)}, u32[]{:S(2)}, u32[]{:S(2)}) collective-permute-start(bf16[160,512]{1,0:T(8,128)(2,1)S(1)} %bitcast.146), channel_id=1, source_target_pairs={{0,16},{8,24},{16,0},{24,8},{1,17},{9,25},{17,1},{25,9},{2,18},{10... | collective-permute-start | bytes 491528 | tf_op jit(solution)/shard_map/ppermute | solution.py:175
  92.8 32.9 %all-to-all-start = ((bf16[8,20,6144]{2,1,0:T(8,128)(2,1)}), bf16[8,20,6144]{2,1,0:T(8,128)(2,1)}, u32[]{:S(2)}, u32[]{:S(2)}) async-start(bf16[8,20,6144]{2,1,0:T(8,128)(2,1)} %convolution_convert_fusion), calls=%async_computation | async-start | bytes 4718592 | tf_op jit(solution)/shard_map/all_to_all | solution.py:119
  97.6 51.1 %all-gather.11.cloned.1.call-start = ((), (), s32[]{:S(2)}) async-start(), calls=%async_computation.3 | async-start | bytes 2457600 | tf_op jit(solution)/shard_map/all_gather | solution.py:141
  110.2 0.7 copy-start.8
  118.4 2.0 %copy-start.6 = (bf16[1,160,1536]{2,0,1:T(2,128)(2,1)S(1)}, bf16[1,160,1536]{2,0,1:T(2,128)(2,1)}, u32[]{:S(2)}) copy-start(bf16[1,160,1536]{2,0,1:T(2,128)(2,1)} %get-tuple-element.32) | copy-start | bytes 1474564
  122.3 5.5 %copy-start.5 = (f32[20,6144]{1,0:T(8,128)S(1)}, f32[20,6144]{1,0:T(8,128)}, u32[]{:S(2)}) copy-start(f32[20,6144]{1,0:T(8,128)} %get-tuple-element.42) | copy-start | bytes 1474564
  122.3 5.7 %copy-start.3 = (f32[20,6144]{1,0:T(8,128)S(1)}, f32[20,6144]{1,0:T(8,128)}, u32[]{:S(2)}) copy-start(f32[20,6144]{1,0:T(8,128)} %copy-done.2) | copy-start | bytes 1474564
  122.3 21.3 %copy-start.4 = (bf16[1,128,6144]{2,1,0:T(8,128)(2,1)S(1)}, bf16[1,128,6144]{2,1,0:T(8,128)(2,1)}, u32[]{:S(2)}) copy-start(bf16[1,128,6144]{2,1,0:T(8,128)(2,1)} %param.11) | copy-start | bytes 4718596
  138.1 8.7 %collective-permute-start.3 = (bf16[2,6144]{1,0:T(2,128)(2,1)S(1)}, bf16[2,6144]{1,0:T(2,128)(2,1)S(1)}, u32[]{:S(2)}, u32[]{:S(2)}) collective-permute-start(bf16[2,6144]{1,0:T(2,128)(2,1)S(1)} %pad_maximum_fusion.2), channel_id=1, source_target_pairs={{0,8},{8,16},{16,24},{24,0},{1,9},{9,17},{17,25},{25,1},{2,10},{10... | collective-permute-start | bytes 73736 | tf_op jit(solution)/shard_map/ppermute | solution.py:189
  139.7 7.2 %collective-permute-start.4 = (bf16[2,6144]{1,0:T(2,128)(2,1)S(1)}, bf16[2,6144]{1,0:T(2,128)(2,1)S(1)}, u32[]{:S(2)}, u32[]{:S(2)}) collective-permute-start(bf16[2,6144]{1,0:T(2,128)(2,1)S(1)} %pad_maximum_fusion.2), channel_id=1, source_target_pairs={{0,16},{8,24},{16,0},{24,8},{1,17},{9,25},{17,1},{25,9},{2,18},{10... | collective-permute-start | bytes 73736 | tf_op jit(solution)/shard_map/ppermute | solution.py:189
  140.7 6.2 %collective-permute-start.5 = (bf16[2,6144]{1,0:T(2,128)(2,1)S(1)}, bf16[2,6144]{1,0:T(2,128)(2,1)S(1)}, u32[]{:S(2)}, u32[]{:S(2)}) collective-permute-start(bf16[2,6144]{1,0:T(2,128)(2,1)S(1)} %pad_maximum_fusion.2), channel_id=1, source_target_pairs={{0,24},{8,0},{16,8},{24,16},{1,25},{9,1},{17,9},{25,17},{2,26},{10... | collective-permute-start | bytes 73736 | tf_op jit(solution)/shard_map/ppermute | solution.py:189
  147.0 3.4 %copy-start.7 = (bf16[640,1536]{1,0:T(8,128)(2,1)S(1)}, bf16[640,1536]{1,0:T(8,128)(2,1)}, u32[]{:S(2)}) copy-start(bf16[640,1536]{1,0:T(8,128)(2,1)} %reshape.222) | copy-start | bytes 5898244
  155.5 2.6 %copy-start.1 = (bf16[1,128,6144]{2,1,0:T(8,128)(2,1)S(1)}, bf16[1,128,6144]{2,1,0:T(8,128)(2,1)}, u32[]{:S(2)}) copy-start(bf16[1,128,6144]{2,1,0:T(8,128)(2,1)} %param.12) | copy-start | bytes 4718596
Sparse Core Ops, SparseCore 0:
  15.8 40.3 all-gather.12
  58.0 35.6 all-gather.8
  100.0 43.8 all-gather.10

commit v7 on v6

--- a/solution.py
+++ b/solution.py
@@ -164,23 +164,15 @@
     grad_key = contract(normed_blocks, gathered(1))
     grad_value = contract(normed_blocks, gathered(2))
     dp_index = lax.axis_index("dp")
-    delta_by_seq = delta_blocks.reshape(n_dp, slots, block)
-    out_total = lax.dot_general(
-        mixed,
-        lax.dynamic_index_in_dim(delta_by_seq, dp_index, 0, keepdims=False),
-        (((0,), (0,)), ((), ())),
-        preferred_element_type=jnp.float32,
+    mixed_by_source = lax.dynamic_update_index_in_dim(
+        jnp.zeros((n_dp, slots, inner), jnp.bfloat16), mixed, dp_index, 0
     )
     for shift in range(1, n_dp):
         arrived = lax.ppermute(mixed, "dp", [(i, (i + shift) % n_dp) for i in range(n_dp)])
-        source = (dp_index + n_dp - shift) % n_dp
-        out_total = out_total + lax.dot_general(
-            arrived,
-            lax.dynamic_index_in_dim(delta_by_seq, source, 0, keepdims=False),
-            (((0,), (0,)), ((), ())),
-            preferred_element_type=jnp.float32,
+        mixed_by_source = lax.dynamic_update_index_in_dim(
+            mixed_by_source, arrived, (dp_index + n_dp - shift) % n_dp, 0
         )
-    grad_out = out_total.astype(jnp.bfloat16)
+    grad_out = contract(mixed_by_source.reshape(n_dp * slots, inner), delta_blocks)
     router_pair = jnp.stack([router_high, router_low])
     router_pieces = lax.dynamic_update_index_in_dim(
         jnp.zeros((n_dp,) + router_pair.shape, jnp.bfloat16), router_pair, dp_index, 0

time: 167 us -> 179 us (1.072)
  local copies, waits for them, and re-layouts: 21.9 us -> 36.7 us
  waiting for transfers between devices: 25.2 us -> 21.7 us
    dynamic_update_slice x0 -> x4, local copies, waits for them, and re-layouts: none -> 6.38 us  [the longest x3 4.79 us: body(): lax.dynamic_update_index_in_dim(mixed_by_source, arrived, (dp_index + n_d...]
    dot_general x4 -> x0, matrix products: 5.93 us -> none  [the longest x3 5.32 us: body(): lax.dot_general(arrived, lax.dynamic_index_in_dim(delta_by_seq, source, 0...]
    dynamic_slice x1 -> x0, local copies, waits for them, and re-layouts: 5.04 us -> none  [body(): lax.dynamic_index_in_dim(delta_by_seq, source, 0, keepdims=False)]
    dot_general x3 -> x4, matrix products: 7.73 us -> 12.1 us  [contract(): lax.dot_general(left, right, (((0,), (0,)), ((), ())), preferred_element_...]
    reshape x0 -> x1, local copies, waits for them, and re-layouts: none -> 3.98 us  [body(): pieces[:, :, 1].transpose(1, 0, 2, 3).reshape(n_dp * slots, block)]
    all_to_all x1, waiting for transfers between devices: 3.41 us -> 0.01 us  [body(): received = lax.all_to_all(contributions, 'ctx', 0, 0, tiled=True)]
    broadcast_in_dim x0 -> x2, local copies, waits for them, and re-layouts: none -> 2.54 us  [the longest x1 1.65 us: body(): lax.dynamic_update_index_in_dim(jnp.zeros((n_dp, slots, inner), jnp.bfloa...]
  transfers between devices with their start and end apart: 10 -> 10, of which waited for: 2 -> 1; matrix products, arithmetic and copies ran while one was open for 39% -> 46% of each run, Pallas kernels for 0% -> 0%
where the time goes in v7:
time: 179 us; the launch traced here: 176 us
  matrix products  51.3 us (29%)
  local copies, waits for them, and re-layouts  36.7 us (21%)
  blocking collectives  27.8 us (16%)
  waiting for transfers between devices  21.7 us (12%)
  between operations  14.8 us (8%)
  starting transfers between devices  13.8 us (8%)
  other arithmetic  10.1 us (6%)
    all_gather x1, waiting for transfers between devices, body(): lax.all_gather(jnp.concatenate([normed, delta, flag_cols], axis=1), 'ctx'...  21.7 us
    all_to_all x1, blocking collectives, body(): lax.all_to_all(jnp.concatenate([normed, delta], axis=0), 'dp', 1, 0, tile...  18.6 us
    dot_general x3, matrix products, project(): lax.dot_general(chunk_normed, weight, (((2,), (0,)), ((), ())), preferred...  14.8 us
    dot_general x4, matrix products, contract(): lax.dot_general(left, right, (((0,), (0,)), ((), ())), preferred_element_...  12.1 us
    all_gather x1, blocking collectives, body(): lax.all_gather(router_split, 'ctx', axis=0, tiled=False).astype(jnp.float32)  9.24 us
    dot_general x1, matrix products, body(): lax.dot_general(chunk_delta, w_out, (((2,), (1,)), ((), ())), preferred_e...  5.69 us
    dot_general x1, matrix products, body(): lax.dot_general(mixed_late.reshape(n_ctx, capacity, inner), w_out, (((2,)...  5.6 us
    ppermute x3, starting transfers between devices, body(): lax.ppermute(mixed, 'dp', [(i, (i + shift) % n_dp) for i in range(n_dp)])  5.33 us
  transfers between devices with their start and end apart: 10, of which 1 were waited for; matrix products, arithmetic and copies ran while one was open for 46% of the time, Pallas kernels for 0%

profile of v7, /device:TPU:2, one launch (start us, length us, event | category | flops | bytes accessed | tf_op | source)
XLA Modules:
  0.0 176.3 jit_solution(5929856860194669169)
XLA Ops:
  7.2 0.6 compare_reduce_fusion.1
  8.5 0.7 compare_and_fusion
  9.2 1.9 %multiply_reduce_fusion.2 = (f32[20]{0:T(128)S(1)}, f32[20,6144]{1,0:T(8,128)S(1)}) fusion(bf16[1,128,6144]{2,1,0:T(8,128)(2,1)} %param.11, s32[20]{0:T(128)S(1)} %bitcast.147, pred[20]{0:T(512)(128)(4,1)S(1)} %get-tuple-element.28), kind=kOutput, calls=%fused_computation.59 | convolution fusion | flops 31708140 | bytes 2064564 | tf_op jit(solution)/shard_map/dot_general | solution.py:41
  11.1 1.4 fusion.41
  12.9 0.4 multiply_convert_fusion
  13.2 0.7 fusion.79
  13.9 0.9 fusion.47
  15.0 18.6 %all_to_all.21 = bf16[40,4,1536]{2,0,1:T(8,128)(2,1)} all-to-all(bf16[40,4,1536]{2,0,1:T(8,128)(2,1)S(1)} %bitcast.134), channel_id=1, replica_groups=mesh['dp'=4,'ctx'=8] {'dp'}, dimensions={1} | all-to-all | bytes 983040 | tf_op jit(solution)/shard_map/all_to_all | solution.py:60
  33.6 21.7 %all-gather.13.cloned.1.call-done = bf16[8,20,12416]{2,1,0:T(8,128)(2,1)} async-done(((bf16[1,20,12416]{2,1,0:T(8,128)(2,1)}), bf16[8,20,12416]{2,1,0:T(8,128)(2,1)}) %all-gather.13.cloned.1.call-update) | async-done | bytes 3973136 | tf_op jit(solution)/shard_map/all_gather | solution.py:52
  55.3 4.9 %fusion.8 = f32[8,20,512]{2,1,0:T(8,128)S(1)} fusion(bf16[6144,512]{1,0:T(8,128)(2,1)} %param.14, bf16[8,20,12416]{2,1,0:T(8,128)(2,1)} %all-gather.13.cloned.1.call-done), kind=kOutput, calls=%fused_computation.10 | convolution fusion | flops 1006632960 | bytes 8978432 | tf_op jit(solution)/shard_map/dot_general | solution.py:69
  60.3 0.2 multiply_reduce_fusion.6
  60.6 4.9 %fusion.6 = f32[8,20,512]{2,1,0:T(8,128)S(1)} fusion(bf16[6144,512]{1,0:T(8,128)(2,1)} %param.15, bf16[8,20,12416]{2,1,0:T(8,128)(2,1)} %all-gather.13.cloned.1.call-done), kind=kOutput, calls=%fused_computation.8 | convolution fusion | flops 1006632960 | bytes 8978432 | tf_op jit(solution)/shard_map/dot_general | solution.py:69
  65.7 0.2 multiply_reduce_fusion.5
  66.0 1.0 compare_reduce_fusion
  67.1 4.9 %fusion.27 = bf16[8,20,512]{2,1,0:T(8,128)(2,1)S(1)} fusion(bf16[6144,512]{1,0:T(8,128)(2,1)} %param.16, bf16[8,20,12416]{2,1,0:T(8,128)(2,1)} %all-gather.13.cloned.1.call-done), kind=kOutput, calls=%fused_computation.40 | convolution fusion | flops 1006714880 | bytes 8814592 | tf_op jit(solution)/shard_map/dot_general | solution.py:69
  72.2 0.4 fusion.50
  72.7 0.3 convolution_convert_fusion.6
  73.0 0.7 copy_bitcast_fusion.4
  73.7 1.5 collective-permute-start
  75.2 2.4 %collective-permute-start.1 = (bf16[160,512]{1,0:T(8,128)(2,1)}, bf16[160,512]{1,0:T(8,128)(2,1)}, u32[]{:S(2)}, u32[]{:S(2)}) collective-permute-start(bf16[160,512]{1,0:T(8,128)(2,1)} %copy_bitcast_fusion.4), channel_id=1, source_target_pairs={{0,16},{8,24},{16,0},{24,8},{1,17},{9,25},{17,1},{25,9},{2,18},{10... | collective-permute-start | bytes 491528 | tf_op jit(solution)/shard_map/ppermute | solution.py:171
  77.6 1.4 collective-permute-start.2
  79.1 5.7 %fusion.32 = bf16[8,20,512]{2,1,0:T(8,128)(2,1)S(1)} fusion(bf16[512,6144]{1,0:T(8,128)(2,1)} %param.17, bf16[8,20,12416]{2,1,0:T(8,128)(2,1)} %all-gather.13.cloned.1.call-done), kind=kOutput, calls=%fused_computation.41 | convolution fusion | flops 1006714880 | bytes 8814592 | tf_op jit(solution)/shard_map/dot_general | solution.py:91
  84.8 0.2 fusion.37
  85.1 0.7 copy.221
  85.8 1.1 fusion.63
  86.9 2.0 %multiply_reduce_fusion.3 = (f32[160,4]{0,1:T(4,128)S(1)}, f32[160,4,128]{2,0,1:T(8,128)S(1)}) fusion(f32[160,4,128]{2,1,0:T(4,128)S(1)} %reshape_reshape.8, f32[160,4]{0,1:T(4,128)S(1)} %get-tuple-element.45, f32[160,4,128]{2,1,0:T(4,128)S(1)} %reshape_reshape.7, f32[160,4]{0,1:T(4,128)S(1)} %get-tuple-element.46, f32[4,160,160]{1,2,0:T(8,128)S(1)} %fusion.50, ...), kind=kOutput, calls=%fused_computation.67 | convolution fusion | flops 27136160 | bytes 1809920 | tf_op jit(solution)/shard_map/hij,ihd->jhd/dot_general | solution.py:105
  88.9 2.2 %multiply_reduce_fusion.4 = (f32[160,4]{0,1:T(4,128)S(1)}, f32[160,4,128]{2,0,1:T(8,128)S(1)}) fusion(f32[160,4,128]{2,1,0:T(4,128)S(1)} %reshape_reshape.7, f32[160,4]{0,1:T(4,128)S(1)} %get-tuple-element.46, f32[4,160,160]{1,2,0:T(8,128)S(1)} %fusion.50, f32[4,160,160]{1,2,0:T(8,128)} %fusion.63, f32[160,4,128]{2,1,0:T(4,128)S(1)} %reshape_reshape.8, ...), kind=kOutput, calls=%fused_computation.69 | convolution fusion | flops 27136160 | bytes 1809920 | tf_op jit(solution)/shard_map/hij,jhd->ihd/dot_general | solution.py:104
  91.1 0.9 copy_bitcast_fusion.2
  92.1 0.9 copy_bitcast_fusion.3
  93.0 1.0 reshape.227
  93.9 5.6 %convolution_convert_fusion = bf16[8,20,6144]{2,1,0:T(8,128)(2,1)} fusion(bf16[8,20,512]{2,1,0:T(8,128)(2,1)S(1)} %reshape.227, bf16[512,6144]{1,0:T(8,128)(2,1)} %param.17), kind=kOutput, calls=%fused_computation.1 | convolution fusion | flops 1007616000 | bytes 8421376 | tf_op jit(solution)/shard_map/dot_general | solution.py:113
  99.5 4.1 %all-to-all-start = ((bf16[8,20,6144]{2,1,0:T(8,128)(2,1)}), bf16[8,20,6144]{2,1,0:T(8,128)(2,1)S(1)}, u32[]{:S(2)}, u32[]{:S(2)}) async-start(bf16[8,20,6144]{2,1,0:T(8,128)(2,1)} %convolution_convert_fusion), calls=%async_computation | async-start | bytes 4718592 | tf_op jit(solution)/shard_map/all_to_all | solution.py:119
  103.6 1.9 %pad_maximum_fusion.1 = bf16[480,512]{1,0:T(8,128)(2,1)} fusion(bf16[160,512]{1,0:T(8,128)(2,1)} %bitcast.136, bf16[160,512]{1,0:T(8,128)(2,1)} %copy_bitcast_fusion.2, bf16[160,512]{1,0:T(8,128)(2,1)} %copy_bitcast_fusion.3), kind=kLoop, calls=%fused_computation.62 | loop fusion | flops 1474560 | bytes 983040 | tf_op jit(solution)/shard_map/concatenate | solution.py:142
  105.5 1.7 copy.151
  107.1 1.6 broadcast_in_dim.64
  108.8 0.9 broadcast_in_dim.63
  109.7 1.6 constant_dynamic-update-slice_fusion
  111.3 1.6 bitcast_dynamic-update-slice_fusion.2
  112.9 1.6 bitcast_dynamic-update-slice_fusion.1
  114.5 1.6 bitcast_dynamic-update-slice_fusion
  116.1 4.4 %copy.160 = bf16[8,160,1536]{2,0,1:T(8,128)(2,1)S(1)} copy(bf16[8,160,1536]{2,1,0:T(8,128)(2,1)} %all-gather.9.cloned.1.call-done) | data formatting | bytes 7864320 | tf_op jit(solution)/shard_map/all_gather | solution.py:63
  120.5 1.6 slice_bitcast_fusion
  122.1 2.0 %copy.163 = bf16[4,8,20,1536]{3,2,1,0:T(8,128)(2,1)} copy(bf16[4,8,20,1536]{3,1,2,0:T(8,128)(2,1)S(1)} %get-tuple-element.30) | data formatting | bytes 3932160 | tf_op jit(solution)/shard_map/transpose | solution.py:67
  124.1 4.0 %reshape.234 = bf16[640,1536]{1,0:T(8,128)(2,1)} reshape(bf16[4,8,20,1536]{3,2,1,0:T(8,128)(2,1)} %copy.163) | data formatting | bytes 3932160 | tf_op jit(solution)/shard_map/reshape | solution.py:67
  128.0 3.6 %copy.161 = bf16[4,8,20,1536]{3,2,1,0:T(8,128)(2,1)} copy(bf16[4,8,20,1536]{3,1,2,0:T(8,128)(2,1)} %get-tuple-element.31) | data formatting | bytes 3932160 | tf_op jit(solution)/shard_map/transpose | solution.py:66
  131.6 4.0 %reshape.229 = bf16[640,1536]{1,0:T(8,128)(2,1)} reshape(bf16[4,8,20,1536]{3,2,1,0:T(8,128)(2,1)} %copy.161) | data formatting | bytes 3932160 | tf_op jit(solution)/shard_map/reshape | solution.py:66
  135.6 4.3 %convolution_convert_fusion.1 = bf16[512,1536]{1,0:T(8,128)(2,1)} fusion(bf16[640,512]{1,0:T(8,128)(2,1)} %bitcast.30, bf16[640,1536]{1,0:T(8,128)(2,1)} %reshape.234), kind=kOutput, calls=%fused_computation.15 | convolution fusion | flops 1007419392 | bytes 4194304 | tf_op jit(solution)/shard_map/dot_general | solution.py:159
  139.9 0.4 convert_reduce_fusion
  140.3 0.2 multiply_reduce_fusion.1
  140.5 0.4 fusion.86
  141.1 9.2 %all-gather.4 = bf16[8,2,6144]{2,1,0:T(2,128)(2,1)S(1)} all-gather(bf16[1,2,6144]{2,1,0:T(2,128)(2,1)S(1)} %maximum_bitcast_fusion), channel_id=4, replica_groups=mesh['dp'=4,'ctx'=8] {'ctx'}, dimensions={0}, use_global_device_ids=true | all-gather | bytes 221184 | tf_op jit(solution)/shard_map/all_gather | solution.py:137
  150.6 1.2 collective-permute-start.3
  151.8 0.8 collective-permute-start.4
  152.6 2.4 %collective-permute-start.5 = (bf16[2,6144]{1,0:T(2,128)(2,1)S(1)}, bf16[2,6144]{1,0:T(2,128)(2,1)S(1)}, u32[]{:S(2)}, u32[]{:S(2)}) collective-permute-start(bf16[2,6144]{1,0:T(2,128)(2,1)S(1)} %pad_maximum_fusion.2), channel_id=1, source_target_pairs={{0,24},{8,0},{16,8},{24,16},{1,25},{9,1},{17,9},{25,17},{2,26},{10... | collective-permute-start | bytes 73736 | tf_op jit(solution)/shard_map/ppermute | solution.py:181
  155.0 2.8 %fusion.2 = bf16[1,128,6144]{2,1,0:T(8,128)(2,1)} fusion(bf16[1,128,6144]{2,1,0:T(8,128)(2,1)S(1)} %copy-done.2, f32[20,6144]{1,0:T(8,128)S(1)} %convert_reduce_fusion, f32[20]{0:T(128)S(1)} %fusion.41, s32[20]{0:T(128)S(1)} %bitcast.149, pred[20]{0:T(512)(128)(4,1)S(1)} %get-tuple-element.28), kind=kOutput, calls=%fused_computation.4 | convolution fusion | flops 191230976 | bytes 3637428 | tf_op jit(solution)/shard_map/dot_general | solution.py:124
  157.9 0.3 dynamic_update_slice.30
  158.5 0.3 dynamic_update_slice.31
  158.8 0.3 dynamic_update_slice.32
  159.2 0.6 dynamic_update_slice.33
  159.7 0.7 fusion.67
  160.4 1.6 fusion.97
  162.0 2.6 %convolution_convert_fusion.2 = bf16[1536,512]{1,0:T(8,128)(2,1)} fusion(bf16[640,1536]{1,0:T(8,128)(2,1)S(1)} %copy-done.3, bf16[640,512]{1,0:T(8,128)(2,1)S(1)} %bitcast.139), kind=kOutput, calls=%fused_computation.16 | convolution fusion | flops 1007419392 | bytes 4194304 | tf_op jit(solution)/shard_map/dot_general | solution.py:159
  164.6 2.6 %convolution_convert_fusion.3 = bf16[1536,512]{1,0:T(8,128)(2,1)} fusion(bf16[640,1536]{1,0:T(8,128)(2,1)S(1)} %copy-done.3, bf16[640,512]{1,0:T(8,128)(2,1)S(1)} %bitcast.138), kind=kOutput, calls=%fused_computation.17 | convolution fusion | flops 1007419392 | bytes 4194304 | tf_op jit(solution)/shard_map/dot_general | solution.py:159
  167.2 2.6 %convolution_convert_fusion.4 = bf16[1536,512]{1,0:T(8,128)(2,1)} fusion(bf16[640,1536]{1,0:T(8,128)(2,1)S(1)} %copy-done.3, bf16[640,512]{1,0:T(8,128)(2,1)S(1)} %bitcast.137), kind=kOutput, calls=%fused_computation.18 | convolution fusion | flops 1007419392 | bytes 4194304 | tf_op jit(solution)/shard_map/dot_general | solution.py:159
  (58 shorter events, 2.0 us)
Async XLA Ops:
  7.2 5.7 %copy-start = (bf16[1,128,6144]{2,1,0:T(8,128)(2,1)S(1)}, bf16[1,128,6144]{2,1,0:T(8,128)(2,1)}, u32[]{:S(2)}) copy-start(bf16[1,128,6144]{2,1,0:T(8,128)(2,1)} %param.12) | copy-start | bytes 4718596
  7.2 48.1 %all-gather.13.cloned.1.call-start = ((), (), s32[]{:S(2)}) async-start(), calls=%async_computation.4 | async-start | bytes 5363712 | tf_op jit(solution)/shard_map/all_gather | solution.py:52
  14.8 101.3 %all-gather.9.cloned.1.call-start = ((), (), s32[]{:S(2)}) async-start(), calls=%async_computation.2 | async-start | bytes 4423680 | tf_op jit(solution)/shard_map/all_gather | solution.py:63
  73.0 11.8 %copy-start.4 = (bf16[4,128,160]{1,2,0:T(8,128)(2,1)}, bf16[4,128,160]{1,2,0:T(8,128)(2,1)S(1)}, u32[]{:S(2)}) copy-start(bf16[4,128,160]{1,2,0:T(8,128)(2,1)S(1)} %convolution_convert_fusion.6) | copy-start | bytes 491524
  73.7 37.6 %collective-permute-start = (bf16[160,512]{1,0:T(8,128)(2,1)}, bf16[160,512]{1,0:T(8,128)(2,1)}, u32[]{:S(2)}, u32[]{:S(2)}) collective-permute-start(bf16[160,512]{1,0:T(8,128)(2,1)} %copy_bitcast_fusion.4), channel_id=1, source_target_pairs={{0,8},{8,16},{16,24},{24,0},{1,9},{9,17},{17,25},{25,1},{2,10},{10... | collective-permute-start | bytes 491528 | tf_op jit(solution)/shard_map/ppermute | solution.py:171
  75.2 37.7 %collective-permute-start.1 = (bf16[160,512]{1,0:T(8,128)(2,1)}, bf16[160,512]{1,0:T(8,128)(2,1)}, u32[]{:S(2)}, u32[]{:S(2)}) collective-permute-start(bf16[160,512]{1,0:T(8,128)(2,1)} %copy_bitcast_fusion.4), channel_id=1, source_target_pairs={{0,16},{8,24},{16,0},{24,8},{1,17},{9,25},{17,1},{25,9},{2,18},{10... | collective-permute-start | bytes 491528 | tf_op jit(solution)/shard_map/ppermute | solution.py:171
  77.6 36.9 %collective-permute-start.2 = (bf16[160,512]{1,0:T(8,128)(2,1)}, bf16[160,512]{1,0:T(8,128)(2,1)}, u32[]{:S(2)}, u32[]{:S(2)}) collective-permute-start(bf16[160,512]{1,0:T(8,128)(2,1)} %copy_bitcast_fusion.4), channel_id=1, source_target_pairs={{0,24},{8,0},{16,8},{24,16},{1,25},{9,1},{17,9},{25,17},{2,26},{10... | collective-permute-start | bytes 491528 | tf_op jit(solution)/shard_map/ppermute | solution.py:171
  99.5 40.4 %all-to-all-start = ((bf16[8,20,6144]{2,1,0:T(8,128)(2,1)}), bf16[8,20,6144]{2,1,0:T(8,128)(2,1)S(1)}, u32[]{:S(2)}, u32[]{:S(2)}) async-start(bf16[8,20,6144]{2,1,0:T(8,128)(2,1)} %convolution_convert_fusion), calls=%async_computation | async-start | bytes 4718592 | tf_op jit(solution)/shard_map/all_to_all | solution.py:119
  103.6 56.8 %all-gather.11.cloned.1.call-start = ((), (), s32[]{:S(2)}) async-start(), calls=%async_computation.3 | async-start | bytes 2457600 | tf_op jit(solution)/shard_map/all_gather | solution.py:141
  139.9 15.1 %copy-start.2 = (bf16[1,128,6144]{2,1,0:T(8,128)(2,1)S(1)}, bf16[1,128,6144]{2,1,0:T(8,128)(2,1)}, u32[]{:S(2)}) copy-start(bf16[1,128,6144]{2,1,0:T(8,128)(2,1)} %param.11) | copy-start | bytes 4718596
  150.6 7.6 %collective-permute-start.3 = (bf16[2,6144]{1,0:T(2,128)(2,1)S(1)}, bf16[2,6144]{1,0:T(2,128)(2,1)S(1)}, u32[]{:S(2)}, u32[]{:S(2)}) collective-permute-start(bf16[2,6144]{1,0:T(2,128)(2,1)S(1)} %pad_maximum_fusion.2), channel_id=1, source_target_pairs={{0,8},{8,16},{16,24},{24,0},{1,9},{9,17},{17,25},{25,1},{2,10},{10... | collective-permute-start | bytes 73736 | tf_op jit(solution)/shard_map/ppermute | solution.py:181
  151.8 6.5 %collective-permute-start.4 = (bf16[2,6144]{1,0:T(2,128)(2,1)S(1)}, bf16[2,6144]{1,0:T(2,128)(2,1)S(1)}, u32[]{:S(2)}, u32[]{:S(2)}) collective-permute-start(bf16[2,6144]{1,0:T(2,128)(2,1)S(1)} %pad_maximum_fusion.2), channel_id=1, source_target_pairs={{0,16},{8,24},{16,0},{24,8},{1,17},{9,25},{17,1},{25,9},{2,18},{10... | collective-permute-start | bytes 73736 | tf_op jit(solution)/shard_map/ppermute | solution.py:181
  152.6 5.8 %collective-permute-start.5 = (bf16[2,6144]{1,0:T(2,128)(2,1)S(1)}, bf16[2,6144]{1,0:T(2,128)(2,1)S(1)}, u32[]{:S(2)}, u32[]{:S(2)}) collective-permute-start(bf16[2,6144]{1,0:T(2,128)(2,1)S(1)} %pad_maximum_fusion.2), channel_id=1, source_target_pairs={{0,24},{8,0},{16,8},{24,16},{1,25},{9,1},{17,9},{25,17},{2,26},{10... | collective-permute-start | bytes 73736 | tf_op jit(solution)/shard_map/ppermute | solution.py:181
  158.5 3.6 %copy-start.3 = (bf16[640,1536]{1,0:T(8,128)(2,1)S(1)}, bf16[640,1536]{1,0:T(8,128)(2,1)}, u32[]{:S(2)}) copy-start(bf16[640,1536]{1,0:T(8,128)(2,1)} %reshape.229) | copy-start | bytes 5898244
  167.2 2.6 %copy-start.1 = (bf16[1,128,6144]{2,1,0:T(8,128)(2,1)S(1)}, bf16[1,128,6144]{2,1,0:T(8,128)(2,1)}, u32[]{:S(2)}) copy-start(bf16[1,128,6144]{2,1,0:T(8,128)(2,1)} %param.12) | copy-start | bytes 4718596
Sparse Core Ops, SparseCore 0:
  14.9 40.3 all-gather.12
  57.2 35.6 all-gather.8
  108.9 42.3 all-gather.10

commit v8 on v6

--- a/solution.py
+++ b/solution.py
@@ -143,7 +143,6 @@
             [
                 query_back,
                 key_back,
-                value_back,
             ],
             axis=0,
         ),
@@ -162,7 +161,6 @@
 
     grad_query = contract(normed_blocks, gathered(0))
     grad_key = contract(normed_blocks, gathered(1))
-    grad_value = contract(normed_blocks, gathered(2))
     dp_index = lax.axis_index("dp")
     delta_by_seq = delta_blocks.reshape(n_dp, slots, block)
     out_total = lax.dot_general(
@@ -181,6 +179,15 @@
             preferred_element_type=jnp.float32,
         )
     grad_out = out_total.astype(jnp.bfloat16)
+    value_by_source = lax.dynamic_update_index_in_dim(
+        jnp.zeros((n_dp, slots, inner), jnp.bfloat16), value_back, dp_index, 0
+    )
+    for shift in range(1, n_dp):
+        arrived = lax.ppermute(value_back, "dp", [(i, (i + shift) % n_dp) for i in range(n_dp)])
+        value_by_source = lax.dynamic_update_index_in_dim(
+            value_by_source, arrived, (dp_index + n_dp - shift) % n_dp, 0
+        )
+    grad_value = contract(normed_blocks, value_by_source.reshape(n_dp * slots, inner))
     router_pair = jnp.stack([router_high, router_low])
     router_pieces = lax.dynamic_update_index_in_dim(
         jnp.zeros((n_dp,) + router_pair.shape, jnp.bfloat16), router_pair, dp_index, 0

time: 167 us -> 181 us (1.084)
  local copies, waits for them, and re-layouts: 21.9 us -> 29.8 us
  starting transfers between devices: 14.8 us -> 18.9 us
  matrix products: 50.6 us -> 53.3 us
  waiting for transfers between devices: 25.2 us -> 23 us
    dynamic_update_slice x0 -> x4, local copies, waits for them, and re-layouts: none -> 5.46 us  [the longest x3 3.87 us: body(): lax.dynamic_update_index_in_dim(value_by_source, arrived, (dp_index + n_d...]
    ppermute x0 -> x3, starting transfers between devices: none -> 5.33 us  [body(): lax.ppermute(value_back, 'dp', [(i, (i + shift) % n_dp) for i in range(n_...]
    all_to_all x1, waiting for transfers between devices: 3.41 us -> 0.01 us  [body(): received = lax.all_to_all(contributions, 'ctx', 0, 0, tiled=True)]
  transfers between devices with their start and end apart: 10 -> 13, of which waited for: 2 -> 3; matrix products, arithmetic and copies ran while one was open for 39% -> 45% of each run, Pallas kernels for 0% -> 0%
where the time goes in v8:
time: 181 us; the launch traced here: 179 us
  matrix products  53.3 us (29%)
  local copies, waits for them, and re-layouts  29.8 us (16%)
  blocking collectives  28 us (15%)
  waiting for transfers between devices  23 us (13%)
  starting transfers between devices  18.9 us (10%)
  between operations  14.9 us (8%)
  other arithmetic  10.9 us (6%)
    all_gather x1, waiting for transfers between devices, body(): lax.all_gather(jnp.concatenate([normed, delta, flag_cols], axis=1), 'ctx'...  21.7 us
    all_to_all x1, blocking collectives, body(): lax.all_to_all(jnp.concatenate([normed, delta], axis=0), 'dp', 1, 0, tile...  18.6 us
    dot_general x3, matrix products, project(): lax.dot_general(chunk_normed, weight, (((2,), (0,)), ((), ())), preferred...  14.8 us
    all_gather x1, blocking collectives, body(): lax.all_gather(router_split, 'ctx', axis=0, tiled=False).astype(jnp.float32)  9.47 us
    dot_general x3, matrix products, contract(): lax.dot_general(left, right, (((0,), (0,)), ((), ())), preferred_element_...  8.9 us
    dot_general x1, matrix products, body(): lax.dot_general(chunk_delta, w_out, (((2,), (1,)), ((), ())), preferred_e...  6.22 us
    dot_general x3, matrix products, body(): lax.dot_general(arrived, lax.dynamic_index_in_dim(delta_by_seq, source, 0...  5.94 us
    dot_general x1, matrix products, body(): lax.dot_general(mixed_late.reshape(n_ctx, capacity, inner), w_out, (((2,)...  5.6 us
  transfers between devices with their start and end apart: 13, of which 3 were waited for; matrix products, arithmetic and copies ran while one was open for 45% of the time, Pallas kernels for 0%

profile of v8, /device:TPU:2, one launch (start us, length us, event | category | flops | bytes accessed | tf_op | source)
XLA Modules:
  0.0 178.9 jit_solution(12786931050730344731)
XLA Ops:
  7.2 0.6 compare_reduce_fusion.1
  8.5 0.7 compare_and_fusion
  9.2 1.9 %multiply_reduce_fusion.2 = (f32[20]{0:T(128)S(1)}, f32[20,6144]{1,0:T(8,128)S(1)}) fusion(bf16[1,128,6144]{2,1,0:T(8,128)(2,1)} %param.11, s32[20]{0:T(128)S(1)} %bitcast.161, pred[20]{0:T(512)(128)(4,1)S(1)} %get-tuple-element.28), kind=kOutput, calls=%fused_computation.63 | convolution fusion | flops 31708140 | bytes 2064564 | tf_op jit(solution)/shard_map/dot_general | solution.py:41
  11.1 1.4 fusion.44
  12.9 0.4 multiply_convert_fusion
  13.2 0.7 fusion.92
  13.9 0.9 fusion.50
  15.0 18.6 %all_to_all.21 = bf16[40,4,1536]{2,0,1:T(8,128)(2,1)} all-to-all(bf16[40,4,1536]{2,0,1:T(8,128)(2,1)S(1)} %bitcast.150), channel_id=1, replica_groups=mesh['dp'=4,'ctx'=8] {'dp'}, dimensions={1} | all-to-all | bytes 983040 | tf_op jit(solution)/shard_map/all_to_all | solution.py:60
  33.6 21.7 %all-gather.13.cloned.1.call-done = bf16[8,20,12416]{2,1,0:T(8,128)(2,1)} async-done(((bf16[1,20,12416]{2,1,0:T(8,128)(2,1)}), bf16[8,20,12416]{2,1,0:T(8,128)(2,1)}) %all-gather.13.cloned.1.call-update) | async-done | bytes 3973136 | tf_op jit(solution)/shard_map/all_gather | solution.py:52
  55.3 4.9 %fusion.8 = f32[8,20,512]{2,1,0:T(8,128)S(1)} fusion(bf16[6144,512]{1,0:T(8,128)(2,1)} %param.14, bf16[8,20,12416]{2,1,0:T(8,128)(2,1)} %all-gather.13.cloned.1.call-done), kind=kOutput, calls=%fused_computation.10 | convolution fusion | flops 1006632960 | bytes 8978432 | tf_op jit(solution)/shard_map/dot_general | solution.py:69
  60.6 4.9 %fusion.6 = f32[8,20,512]{2,1,0:T(8,128)S(1)} fusion(bf16[6144,512]{1,0:T(8,128)(2,1)} %param.15, bf16[8,20,12416]{2,1,0:T(8,128)(2,1)} %all-gather.13.cloned.1.call-done), kind=kOutput, calls=%fused_computation.8 | convolution fusion | flops 1006632960 | bytes 8978432 | tf_op jit(solution)/shard_map/dot_general | solution.py:69
  66.0 1.0 compare_reduce_fusion
  67.1 4.9 %fusion.29 = bf16[8,20,512]{2,1,0:T(8,128)(2,1)S(1)} fusion(bf16[6144,512]{1,0:T(8,128)(2,1)} %param.16, bf16[8,20,12416]{2,1,0:T(8,128)(2,1)} %all-gather.13.cloned.1.call-done), kind=kOutput, calls=%fused_computation.43 | convolution fusion | flops 1006714880 | bytes 8814592 | tf_op jit(solution)/shard_map/dot_general | solution.py:69
  72.2 0.4 fusion.63
  72.7 0.3 fusion.39
  73.0 0.7 copy.255
  73.8 1.5 collective-permute-start.3
  75.2 2.3 %collective-permute-start.5 = (bf16[160,512]{1,0:T(8,128)(2,1)}, bf16[160,512]{1,0:T(8,128)(2,1)}, u32[]{:S(2)}, u32[]{:S(2)}) collective-permute-start(bf16[160,512]{1,0:T(8,128)(2,1)} %bitcast.143), channel_id=1, source_target_pairs={{0,24},{8,0},{16,8},{24,16},{1,25},{9,1},{17,9},{25,17},{2,26},{10... | collective-permute-start | bytes 491528 | tf_op jit(solution)/shard_map/ppermute | solution.py:173
  77.6 0.6 collective-permute-start.4
  78.2 6.2 %fusion.34 = bf16[8,20,512]{2,1,0:T(8,128)(2,1)S(1)} fusion(bf16[512,6144]{1,0:T(8,128)(2,1)} %param.17, bf16[8,20,12416]{2,1,0:T(8,128)(2,1)} %all-gather.13.cloned.1.call-done), kind=kOutput, calls=%fused_computation.44 | convolution fusion | flops 1006714880 | bytes 8814592 | tf_op jit(solution)/shard_map/dot_general | solution.py:91
  84.7 0.7 copy.254
  85.7 1.1 multiply_reduce_fusion.3
  86.8 0.7 multiply_reduce_fusion.4
  87.5 1.9 %copy_bitcast_fusion.2 = bf16[160,512]{1,0:T(8,128)(2,1)} fusion(f32[160,4,128]{2,0,1:T(8,128)} %get-tuple-element.47, f32[160,4,128]{2,1,0:T(4,128)S(1)} %reshape_reshape.11, f32[160,4]{0,1:T(4,128)S(1)} %broadcast_multiply_fusion, f32[160,4]{0,1:T(4,128)S(1)} %get-tuple-element.48), kind=kLoop, calls=%fused_computation.96 | loop fusion | flops 409600 | bytes 824320 | tf_op jit(solution)/shard_map/reshape | solution.py:109
  89.4 0.9 copy_bitcast_fusion.3
  90.3 1.5 collective-permute-start
  91.7 0.9 collective-permute-start.1
  92.7 1.0 reshape.220
  93.6 5.6 %convolution_convert_fusion = bf16[8,20,6144]{2,1,0:T(8,128)(2,1)} fusion(bf16[8,20,512]{2,1,0:T(8,128)(2,1)S(1)} %reshape.220, bf16[512,6144]{1,0:T(8,128)(2,1)} %param.17), kind=kOutput, calls=%fused_computation.1 | convolution fusion | flops 1007616000 | bytes 8421376 | tf_op jit(solution)/shard_map/dot_general | solution.py:113
  99.2 4.3 %all-to-all-start = ((bf16[8,20,6144]{2,1,0:T(8,128)(2,1)}), bf16[8,20,6144]{2,1,0:T(8,128)(2,1)S(1)}, u32[]{:S(2)}, u32[]{:S(2)}) async-start(bf16[8,20,6144]{2,1,0:T(8,128)(2,1)} %convolution_convert_fusion), calls=%async_computation | async-start | bytes 4718592 | tf_op jit(solution)/shard_map/all_to_all | solution.py:119
  103.5 1.8 pad_maximum_fusion.1
  105.3 0.9 broadcast_in_dim.63
  106.2 1.6 bitcast_dynamic-update-slice_fusion.3
  107.8 2.9 %collective-permute-start.2 = (bf16[160,512]{1,0:T(8,128)(2,1)}, bf16[160,512]{1,0:T(8,128)(2,1)S(1)}, u32[]{:S(2)}, u32[]{:S(2)}) collective-permute-start(bf16[160,512]{1,0:T(8,128)(2,1)} %bitcast.142), channel_id=1, source_target_pairs={{0,24},{8,0},{16,8},{24,16},{1,25},{9,1},{17,9},{25,17},{2,26},{10... | collective-permute-start | bytes 491528 | tf_op jit(solution)/shard_map/ppermute | solution.py:186
  110.7 1.6 bitcast_dynamic-update-slice_fusion.2
  112.3 1.6 bitcast_dynamic-update-slice_fusion.1
  113.9 0.9 collective-permute-done.2
  114.8 0.7 bitcast_dynamic-update-slice_fusion
  115.4 4.3 %copy.173 = bf16[8,160,1536]{2,0,1:T(8,128)(2,1)S(1)} copy(bf16[8,160,1536]{2,1,0:T(8,128)(2,1)} %all-gather.9.cloned.1.call-done) | data formatting | bytes 7864320 | tf_op jit(solution)/shard_map/all_gather | solution.py:63
  119.7 0.3 slice_bitcast_fusion
  120.0 1.5 copy.175
  121.5 5.2 %constant_dynamic-slice_fusion.1 = (bf16[1,160,1536]{2,0,1:T(2,128)(2,1)}, bf16[1,160,1536]{2,0,1:T(2,128)(2,1)}, bf16[1,160,1536]{2,0,1:T(2,128)(2,1)}, bf16[1,160,1536]{2,0,1:T(2,128)(2,1)}) fusion(bf16[4,160,1536]{2,0,1:T(4,128)(2,1)S(1)} %bitcast.146, s32[]{:T(128)S(6)} %select_n.59, s32[]{:T(128)S(6)} %select_n.61, s32[]{:T(128)S(6)} %select_n.57, ...), kind=kLoop, calls=%fused_computation.139 | loop fusion | bytes 3932176 | tf_op jit(solution)/shard_map/jit(dynamic_index_in_dim)/dynamic_slice | solution.py:177
  126.7 2.0 %copy.174 = bf16[4,8,20,1536]{3,2,1,0:T(8,128)(2,1)} copy(bf16[4,8,20,1536]{3,1,2,0:T(8,128)(2,1)S(1)} %get-tuple-element.31) | data formatting | bytes 3932160 | tf_op jit(solution)/shard_map/transpose | solution.py:66
  128.7 4.0 %reshape.222 = bf16[640,1536]{1,0:T(8,128)(2,1)} reshape(bf16[4,8,20,1536]{3,2,1,0:T(8,128)(2,1)} %copy.174) | data formatting | bytes 3932160 | tf_op jit(solution)/shard_map/reshape | solution.py:66
  132.7 2.0 %fusion.59 = f32[512,1536]{1,0:T(8,128)S(1)} fusion(bf16[1,160,1536]{2,0,1:T(2,128)(2,1)} %get-tuple-element.35, bf16[4,20,8,128]{3,2,1,0:T(8,128)(2,1)} %copy-done.8), kind=kOutput, calls=%fused_computation.73 | convolution fusion | flops 251658240 | bytes 3801088 | tf_op jit(solution)/shard_map/dot_general | solution.py:166
  134.7 1.7 convolution_add_fusion.2
  136.4 3.7 %convolution_convert_fusion.1 = bf16[1536,512]{1,0:T(8,128)(2,1)} fusion(bf16[640,1536]{1,0:T(8,128)(2,1)S(1)} %copy-done.6, bf16[640,512]{1,0:T(8,128)(2,1)} %bitcast.30), kind=kOutput, calls=%fused_computation.19 | convolution fusion | flops 1007419392 | bytes 4194304 | tf_op jit(solution)/shard_map/dot_general | solution.py:158
  140.2 1.6 fusion.52
  141.8 2.7 %fusion.13 = bf16[512,1536]{1,0:T(8,128)(2,1)} fusion(f32[512,1536]{1,0:T(8,128)S(1)} %fusion.52, f32[512,1536]{1,0:T(8,128)S(1)} %convolution_add_fusion.2, bf16[160,512]{1,0:T(8,128)(2,1)} %collective-permute-done.4, bf16[1,160,1536]{2,0,1:T(2,128)(2,1)S(1)} %copy-done.3), kind=kOutput, calls=%fused_computation.18 | convolution fusion | flops 254017536 | bytes 8519680 | tf_op jit(solution)/shard_map/dot_general | solution.py:175
  144.5 0.4 convert_reduce_fusion
  145.1 0.4 fusion.99
  145.6 9.5 %all-gather.4 = bf16[8,2,6144]{2,1,0:T(2,128)(2,1)S(1)} all-gather(bf16[1,2,6144]{2,1,0:T(2,128)(2,1)S(1)} %maximum_bitcast_fusion), channel_id=4, replica_groups=mesh['dp'=4,'ctx'=8] {'ctx'}, dimensions={0}, use_global_device_ids=true | all-gather | bytes 221184 | tf_op jit(solution)/shard_map/all_gather | solution.py:137
  155.4 1.1 collective-permute-start.6
  156.5 3.7 %collective-permute-start.7 = (bf16[2,6144]{1,0:T(2,128)(2,1)S(1)}, bf16[2,6144]{1,0:T(2,128)(2,1)S(1)}, u32[]{:S(2)}, u32[]{:S(2)}) collective-permute-start(bf16[2,6144]{1,0:T(2,128)(2,1)S(1)} %pad_maximum_fusion.2), channel_id=1, source_target_pairs={{0,16},{8,24},{16,0},{24,8},{1,17},{9,25},{17,1},{25,9},{2,18},{10... | collective-permute-start | bytes 73736 | tf_op jit(solution)/shard_map/ppermute | solution.py:196
  160.3 2.8 %fusion.2 = bf16[1,128,6144]{2,1,0:T(8,128)(2,1)} fusion(bf16[1,128,6144]{2,1,0:T(8,128)(2,1)S(1)} %copy-done.2, f32[20,6144]{1,0:T(8,128)S(1)} %convert_reduce_fusion, f32[20]{0:T(128)S(1)} %fusion.44, s32[20]{0:T(128)S(1)} %bitcast.163, pred[20]{0:T(512)(128)(4,1)S(1)} %get-tuple-element.28), kind=kOutput, calls=%fused_computation.4 | convolution fusion | flops 191230976 | bytes 3637428 | tf_op jit(solution)/shard_map/dot_general | solution.py:124
  163.2 0.3 dynamic_update_slice.30
  163.6 0.4 collective-permute-done.8
  164.0 0.3 dynamic_update_slice.31
  164.4 0.3 dynamic_update_slice.32
  164.7 0.3 dynamic_update_slice.33
  165.1 0.7 fusion.80
  165.8 1.4 fusion.110
  167.2 2.6 %convolution_convert_fusion.2 = bf16[1536,512]{1,0:T(8,128)(2,1)} fusion(bf16[640,1536]{1,0:T(8,128)(2,1)S(1)} %copy-done.7, bf16[640,512]{1,0:T(8,128)(2,1)S(1)} %bitcast.153), kind=kOutput, calls=%fused_computation.20 | convolution fusion | flops 1007419392 | bytes 4194304 | tf_op jit(solution)/shard_map/dot_general | solution.py:158
  169.8 2.6 %convolution_convert_fusion.3 = bf16[1536,512]{1,0:T(8,128)(2,1)} fusion(bf16[640,1536]{1,0:T(8,128)(2,1)S(1)} %copy-done.7, bf16[640,512]{1,0:T(8,128)(2,1)S(1)} %bitcast.152), kind=kOutput, calls=%fused_computation.21 | convolution fusion | flops 1007419392 | bytes 4194304 | tf_op jit(solution)/shard_map/dot_general | solution.py:158
  (73 shorter events, 3.2 us)
Async XLA Ops:
  7.2 5.7 %copy-start = (bf16[1,128,6144]{2,1,0:T(8,128)(2,1)S(1)}, bf16[1,128,6144]{2,1,0:T(8,128)(2,1)}, u32[]{:S(2)}) copy-start(bf16[1,128,6144]{2,1,0:T(8,128)(2,1)} %param.12) | copy-start | bytes 4718596
  7.2 48.1 %all-gather.13.cloned.1.call-start = ((), (), s32[]{:S(2)}) async-start(), calls=%async_computation.4 | async-start | bytes 5363712 | tf_op jit(solution)/shard_map/all_gather | solution.py:52
  14.8 100.7 %all-gather.9.cloned.1.call-start = ((), (), s32[]{:S(2)}) async-start(), calls=%async_computation.2 | async-start | bytes 4423680 | tf_op jit(solution)/shard_map/all_gather | solution.py:63
  73.0 5.2 %copy-start.8 = (bf16[4,20,8,128]{3,2,1,0:T(8,128)(2,1)}, bf16[4,20,8,128]{3,2,1,0:T(8,128)(2,1)S(1)}, u32[]{:S(2)}) copy-start(bf16[4,20,8,128]{3,2,1,0:T(8,128)(2,1)S(1)} %fusion.39) | copy-start | bytes 491524
  73.8 60.9 %collective-permute-start.3 = (bf16[160,512]{1,0:T(8,128)(2,1)}, bf16[160,512]{1,0:T(8,128)(2,1)}, u32[]{:S(2)}, u32[]{:S(2)}) collective-permute-start(bf16[160,512]{1,0:T(8,128)(2,1)} %bitcast.143), channel_id=1, source_target_pairs={{0,8},{8,16},{16,24},{24,0},{1,9},{9,17},{17,25},{25,1},{2,10},{10... | collective-permute-start | bytes 491528 | tf_op jit(solution)/shard_map/ppermute | solution.py:173
  75.2 64.9 %collective-permute-start.5 = (bf16[160,512]{1,0:T(8,128)(2,1)}, bf16[160,512]{1,0:T(8,128)(2,1)}, u32[]{:S(2)}, u32[]{:S(2)}) collective-permute-start(bf16[160,512]{1,0:T(8,128)(2,1)} %bitcast.143), channel_id=1, source_target_pairs={{0,24},{8,0},{16,8},{24,16},{1,25},{9,1},{17,9},{25,17},{2,26},{10... | collective-permute-start | bytes 491528 | tf_op jit(solution)/shard_map/ppermute | solution.py:173
  77.6 64.2 %collective-permute-start.4 = (bf16[160,512]{1,0:T(8,128)(2,1)}, bf16[160,512]{1,0:T(8,128)(2,1)}, u32[]{:S(2)}, u32[]{:S(2)}) collective-permute-start(bf16[160,512]{1,0:T(8,128)(2,1)} %bitcast.143), channel_id=1, source_target_pairs={{0,16},{8,24},{16,0},{24,8},{1,17},{9,25},{17,1},{25,9},{2,18},{10... | collective-permute-start | bytes 491528 | tf_op jit(solution)/shard_map/ppermute | solution.py:173
  90.3 17.5 %collective-permute-start = (bf16[160,512]{1,0:T(8,128)(2,1)}, bf16[160,512]{1,0:T(8,128)(2,1)}, u32[]{:S(2)}, u32[]{:S(2)}) collective-permute-start(bf16[160,512]{1,0:T(8,128)(2,1)} %bitcast.142), channel_id=1, source_target_pairs={{0,8},{8,16},{16,24},{24,0},{1,9},{9,17},{17,25},{25,1},{2,10},{10... | collective-permute-start | bytes 491528 | tf_op jit(solution)/shard_map/ppermute | solution.py:186
  91.7 20.5 %collective-permute-start.1 = (bf16[160,512]{1,0:T(8,128)(2,1)}, bf16[160,512]{1,0:T(8,128)(2,1)}, u32[]{:S(2)}, u32[]{:S(2)}) collective-permute-start(bf16[160,512]{1,0:T(8,128)(2,1)} %bitcast.142), channel_id=1, source_target_pairs={{0,16},{8,24},{16,0},{24,8},{1,17},{9,25},{17,1},{25,9},{2,18},{10... | collective-permute-start | bytes 491528 | tf_op jit(solution)/shard_map/ppermute | solution.py:186
  99.2 45.3 %all-to-all-start = ((bf16[8,20,6144]{2,1,0:T(8,128)(2,1)}), bf16[8,20,6144]{2,1,0:T(8,128)(2,1)S(1)}, u32[]{:S(2)}, u32[]{:S(2)}) async-start(bf16[8,20,6144]{2,1,0:T(8,128)(2,1)} %convolution_convert_fusion), calls=%async_computation | async-start | bytes 4718592 | tf_op jit(solution)/shard_map/all_to_all | solution.py:119
  103.5 62.3 %all-gather.11.cloned.1.call-start = ((), (), s32[]{:S(2)}) async-start(), calls=%async_computation.3 | async-start | bytes 1638400 | tf_op jit(solution)/shard_map/all_gather | solution.py:141
  107.8 7.0 %collective-permute-start.2 = (bf16[160,512]{1,0:T(8,128)(2,1)}, bf16[160,512]{1,0:T(8,128)(2,1)S(1)}, u32[]{:S(2)}, u32[]{:S(2)}) collective-permute-start(bf16[160,512]{1,0:T(8,128)(2,1)} %bitcast.142), channel_id=1, source_target_pairs={{0,24},{8,0},{16,8},{24,16},{1,25},{9,1},{17,9},{25,17},{2,26},{10... | collective-permute-start | bytes 491528 | tf_op jit(solution)/shard_map/ppermute | solution.py:186
  132.7 2.0 %copy-start.5 = (bf16[1,160,1536]{2,0,1:T(2,128)(2,1)S(1)}, bf16[1,160,1536]{2,0,1:T(2,128)(2,1)}, u32[]{:S(2)}) copy-start(bf16[1,160,1536]{2,0,1:T(2,128)(2,1)} %get-tuple-element.34) | copy-start | bytes 1474564
  134.7 1.7 copy-start.6
  136.4 3.8 %copy-start.4 = (bf16[1,160,1536]{2,0,1:T(2,128)(2,1)S(1)}, bf16[1,160,1536]{2,0,1:T(2,128)(2,1)}, u32[]{:S(2)}) copy-start(bf16[1,160,1536]{2,0,1:T(2,128)(2,1)} %get-tuple-element.33) | copy-start | bytes 1474564
  140.2 1.6 copy-start.3
  144.5 15.8 %copy-start.2 = (bf16[1,128,6144]{2,1,0:T(8,128)(2,1)S(1)}, bf16[1,128,6144]{2,1,0:T(8,128)(2,1)}, u32[]{:S(2)}) copy-start(bf16[1,128,6144]{2,1,0:T(8,128)(2,1)} %param.11) | copy-start | bytes 4718596
  155.4 8.1 %collective-permute-start.6 = (bf16[2,6144]{1,0:T(2,128)(2,1)S(1)}, bf16[2,6144]{1,0:T(2,128)(2,1)S(1)}, u32[]{:S(2)}, u32[]{:S(2)}) collective-permute-start(bf16[2,6144]{1,0:T(2,128)(2,1)S(1)} %pad_maximum_fusion.2), channel_id=1, source_target_pairs={{0,8},{8,16},{16,24},{24,0},{1,9},{9,17},{17,25},{25,1},{2,10},{10... | collective-permute-start | bytes 73736 | tf_op jit(solution)/shard_map/ppermute | solution.py:196
  156.5 7.1 %collective-permute-start.7 = (bf16[2,6144]{1,0:T(2,128)(2,1)S(1)}, bf16[2,6144]{1,0:T(2,128)(2,1)S(1)}, u32[]{:S(2)}, u32[]{:S(2)}) collective-permute-start(bf16[2,6144]{1,0:T(2,128)(2,1)S(1)} %pad_maximum_fusion.2), channel_id=1, source_target_pairs={{0,16},{8,24},{16,0},{24,8},{1,17},{9,25},{17,1},{25,9},{2,18},{10... | collective-permute-start | bytes 73736 | tf_op jit(solution)/shard_map/ppermute | solution.py:196
  160.2 3.8 %collective-permute-start.8 = (bf16[2,6144]{1,0:T(2,128)(2,1)S(1)}, bf16[2,6144]{1,0:T(2,128)(2,1)S(1)}, u32[]{:S(2)}, u32[]{:S(2)}) collective-permute-start(bf16[2,6144]{1,0:T(2,128)(2,1)S(1)} %pad_maximum_fusion.2), channel_id=1, source_target_pairs={{0,24},{8,0},{16,8},{24,16},{1,25},{9,1},{17,9},{25,17},{2,26},{10... | collective-permute-start | bytes 73736 | tf_op jit(solution)/shard_map/ppermute | solution.py:196
  163.1 4.1 %copy-start.7 = (bf16[640,1536]{1,0:T(8,128)(2,1)S(1)}, bf16[640,1536]{1,0:T(8,128)(2,1)}, u32[]{:S(2)}) copy-start(bf16[640,1536]{1,0:T(8,128)(2,1)} %reshape.222) | copy-start | bytes 5898244
  169.8 2.6 %copy-start.1 = (bf16[1,128,6144]{2,1,0:T(8,128)(2,1)S(1)}, bf16[1,128,6144]{2,1,0:T(8,128)(2,1)}, u32[]{:S(2)}) copy-start(bf16[1,128,6144]{2,1,0:T(8,128)(2,1)} %param.12) | copy-start | bytes 4718596
Sparse Core Ops, SparseCore 0:
  14.9 40.3 all-gather.12
  57.2 35.6 all-gather.8
  105.9 33.2 all-gather.10

commit v9 on v5

--- a/solution.py
+++ b/solution.py
@@ -136,8 +136,6 @@
     router_group = jnp.sum(
         lax.all_gather(router_split, "ctx", axis=0, tiled=False).astype(jnp.float32), axis=(0, 1)
     )
-    router_high = router_group.astype(jnp.bfloat16)
-    router_low = (router_group - router_high.astype(jnp.float32)).astype(jnp.bfloat16)
     factors = lax.all_gather(
         jnp.concatenate(
             [
@@ -181,10 +179,13 @@
             preferred_element_type=jnp.float32,
         )
     grad_out = out_total.astype(jnp.bfloat16)
-    router_pieces = lax.all_gather(
-        jnp.stack([router_high, router_low]), "dp", axis=0, tiled=False
-    ).astype(jnp.float32)
-    grad_router = jnp.sum(router_pieces[:, 0] + router_pieces[:, 1], axis=0)
+    grad_router = router_group
+    bit = 1
+    while bit < n_dp:
+        grad_router = grad_router + lax.ppermute(
+            grad_router, "dp", [(i, i ^ bit) for i in range(n_dp)]
+        )
+        bit *= 2
     return (layer_out, grad_query, grad_key, grad_value, grad_out, grad_router)
 
 

time: 174 us -> 170 us (0.977)
  blocking collectives: 41.4 us -> 28 us
  waiting for transfers between devices: 25.2 us -> 30.7 us
  local copies, waits for them, and re-layouts: 20.9 us -> 18.1 us
  matrix products: 50.6 us -> 53.3 us
  starting transfers between devices: 9.37 us -> 12 us
    all_gather x1 -> x0, blocking collectives: 13.6 us -> none  [body(): lax.all_gather(jnp.stack([router_high, router_low]), 'dp', axis=0, tiled=...]
    all_to_all x1, waiting for transfers between devices: 3.41 us -> 8.95 us  [body(): received = lax.all_to_all(contributions, 'ctx', 0, 0, tiled=True)]
    ppermute x0 -> x2, starting transfers between devices: none -> 2.59 us  [body(): lax.ppermute(grad_router, 'dp', [(i, i ^ bit) for i in range(n_dp)])]
    reshape x1, local copies, waits for them, and re-layouts: 3.99 us -> 1.98 us  [body(): pieces[:, :, 0].transpose(1, 0, 2, 3).reshape(n_dp * slots, block)]
  transfers between devices with their start and end apart: 7 -> 9, of which waited for: 2 -> 2; matrix products, arithmetic and copies ran while one was open for 37% -> 38% of each run, Pallas kernels for 0% -> 0%
where the time goes in v9:
time: 170 us; the launch traced here: 168 us
  matrix products  53.3 us (31%)
  waiting for transfers between devices  30.7 us (18%)
  blocking collectives  28 us (16%)
  local copies, waits for them, and re-layouts  18.1 us (11%)
  between operations  14.8 us (9%)
  starting transfers between devices  12 us (7%)
  other arithmetic  10.6 us (6%)
    all_gather x1, waiting for transfers between devices, body(): lax.all_gather(jnp.concatenate([normed, delta, flag_cols], axis=1), 'ctx'...  21.7 us
    all_to_all x1, blocking collectives, body(): lax.all_to_all(jnp.concatenate([normed, delta], axis=0), 'dp', 1, 0, tile...  18.6 us
    dot_general x3, matrix products, project(): lax.dot_general(chunk_normed, weight, (((2,), (0,)), ((), ())), preferred...  14.8 us
    all_gather x1, blocking collectives, body(): lax.all_gather(router_split, 'ctx', axis=0, tiled=False).astype(jnp.float32)  9.48 us
    all_to_all x1, waiting for transfers between devices, body(): received = lax.all_to_all(contributions, 'ctx', 0, 0, tiled=True)  8.95 us
    dot_general x3, matrix products, contract(): lax.dot_general(left, right, (((0,), (0,)), ((), ())), preferred_element_...  7.74 us
    dot_general x3, matrix products, body(): lax.dot_general(arrived, lax.dynamic_index_in_dim(delta_by_seq, source, 0...  6.54 us
    dot_general x1, matrix products, body(): lax.dot_general(chunk_delta, w_out, (((2,), (1,)), ((), ())), preferred_e...  6.34 us
  transfers between devices with their start and end apart: 9, of which 2 were waited for; matrix products, arithmetic and copies ran while one was open for 38% of the time, Pallas kernels for 0%

profile of v9, /device:TPU:2, one launch (start us, length us, event | category | flops | bytes accessed | tf_op | source)
XLA Modules:
  0.0 167.6 jit_solution(15437864639726890491)
XLA Ops:
  7.2 0.6 compare_reduce_fusion.1
  8.5 0.7 compare_and_fusion
  9.2 1.9 %multiply_reduce_fusion.2 = (f32[20]{0:T(128)S(1)}, f32[20,6144]{1,0:T(8,128)S(1)}) fusion(bf16[1,128,6144]{2,1,0:T(8,128)(2,1)} %param.11, s32[20]{0:T(128)S(1)} %bitcast.148, pred[20]{0:T(512)(128)(4,1)S(1)} %get-tuple-element.28), kind=kOutput, calls=%fused_computation.63 | convolution fusion | flops 31708140 | bytes 2064564 | tf_op jit(solution)/shard_map/dot_general | solution.py:41
  11.1 1.4 fusion.44
  12.6 0.1 multiply_convert_fusion.1
  12.7 0.1 copy.105
  12.8 0.1 copy.106
  12.9 1.2 multiply_convert_fusion
  14.1 0.7 fusion.91
  14.8 0.9 fusion.50
  15.7 0.1 pad_maximum_fusion
  15.8 18.6 %all_to_all.21 = bf16[40,4,1536]{2,0,1:T(8,128)(2,1)} all-to-all(bf16[40,4,1536]{2,0,1:T(8,128)(2,1)S(1)} %bitcast.137), channel_id=1, replica_groups=mesh['dp'=4,'ctx'=8] {'dp'}, dimensions={1} | all-to-all | bytes 983040 | tf_op jit(solution)/shard_map/all_to_all | solution.py:60
  34.5 21.7 %all-gather.13.cloned.1.call-done = bf16[8,20,12416]{2,1,0:T(8,128)(2,1)} async-done(((bf16[1,20,12416]{2,1,0:T(8,128)(2,1)}), bf16[8,20,12416]{2,1,0:T(8,128)(2,1)}) %all-gather.13.cloned.1.call-update) | async-done | bytes 3973136 | tf_op jit(solution)/shard_map/all_gather | solution.py:52
  56.2 4.9 %fusion.8 = f32[8,20,512]{2,1,0:T(8,128)S(1)} fusion(bf16[6144,512]{1,0:T(8,128)(2,1)} %param.14, bf16[8,20,12416]{2,1,0:T(8,128)(2,1)} %all-gather.13.cloned.1.call-done), kind=kOutput, calls=%fused_computation.10 | convolution fusion | flops 1006632960 | bytes 8978432 | tf_op jit(solution)/shard_map/dot_general | solution.py:69
  61.1 0.1 reshape_reshape.10
  61.2 0.2 multiply_reduce_fusion.6
  61.4 0.1 copy.107
  61.5 4.9 %fusion.6 = f32[8,20,512]{2,1,0:T(8,128)S(1)} fusion(bf16[6144,512]{1,0:T(8,128)(2,1)} %param.15, bf16[8,20,12416]{2,1,0:T(8,128)(2,1)} %all-gather.13.cloned.1.call-done), kind=kOutput, calls=%fused_computation.8 | convolution fusion | flops 1006632960 | bytes 8978432 | tf_op jit(solution)/shard_map/dot_general | solution.py:69
  66.4 0.1 reshape_reshape.11
  66.6 0.2 multiply_reduce_fusion.5
  66.9 1.0 compare_reduce_fusion
  67.9 0.1 gt.16
  68.0 4.9 %fusion.29 = bf16[8,20,512]{2,1,0:T(8,128)(2,1)S(1)} fusion(bf16[6144,512]{1,0:T(8,128)(2,1)} %param.16, bf16[8,20,12416]{2,1,0:T(8,128)(2,1)} %all-gather.13.cloned.1.call-done), kind=kOutput, calls=%fused_computation.43 | convolution fusion | flops 1006714880 | bytes 8814592 | tf_op jit(solution)/shard_map/dot_general | solution.py:69
  73.0 0.1 fusion.73
  73.1 0.4 fusion.63
  73.5 0.3 fusion.39
  73.9 1.5 collective-permute-start
  75.5 2.3 %collective-permute-start.2 = (bf16[160,512]{1,0:T(8,128)(2,1)S(1)}, bf16[160,512]{1,0:T(8,128)(2,1)}, u32[]{:S(2)}, u32[]{:S(2)}) collective-permute-start(bf16[160,512]{1,0:T(8,128)(2,1)S(1)} %bitcast.139), channel_id=1, source_target_pairs={{0,24},{8,0},{16,8},{24,16},{1,25},{9,1},{17,9},{25,17},{2,26},{10... | collective-permute-start | bytes 491528 | tf_op jit(solution)/shard_map/ppermute | solution.py:173
  77.8 0.6 collective-permute-start.1
  78.4 6.3 %fusion.34 = bf16[8,20,512]{2,1,0:T(8,128)(2,1)S(1)} fusion(bf16[512,6144]{1,0:T(8,128)(2,1)} %param.17, bf16[8,20,12416]{2,1,0:T(8,128)(2,1)} %all-gather.13.cloned.1.call-done), kind=kOutput, calls=%fused_computation.44 | convolution fusion | flops 1006714880 | bytes 8814592 | tf_op jit(solution)/shard_map/dot_general | solution.py:91
  84.8 0.2 fusion.40
  85.1 0.3 fusion.76
  85.3 0.5 multiply_reduce_fusion.3
  85.9 0.7 multiply_reduce_fusion.4
  86.6 0.2 copy_bitcast_fusion.2
  86.8 0.2 copy_bitcast_fusion.3
  87.1 5.8 %convolution_convert_fusion = bf16[8,20,6144]{2,1,0:T(8,128)(2,1)} fusion(bf16[8,20,512]{2,1,0:T(8,128)(2,1)S(1)} %reshape.199, bf16[512,6144]{1,0:T(8,128)(2,1)} %param.17), kind=kOutput, calls=%fused_computation.1 | convolution fusion | flops 1007616000 | bytes 8421376 | tf_op jit(solution)/shard_map/dot_general | solution.py:113
  92.9 4.8 %all-to-all-start = ((bf16[8,20,6144]{2,1,0:T(8,128)(2,1)}), bf16[8,20,6144]{2,1,0:T(8,128)(2,1)}, u32[]{:S(2)}, u32[]{:S(2)}) async-start(bf16[8,20,6144]{2,1,0:T(8,128)(2,1)} %convolution_convert_fusion), calls=%async_computation | async-start | bytes 4718592 | tf_op jit(solution)/shard_map/all_to_all | solution.py:119
  97.7 0.8 pad_maximum_fusion.1
  98.6 4.3 %copy.122 = bf16[8,160,1536]{2,0,1:T(8,128)(2,1)S(1)} copy(bf16[8,160,1536]{2,1,0:T(8,128)(2,1)} %all-gather.9.cloned.1.call-done) | data formatting | bytes 7864320 | tf_op jit(solution)/shard_map/all_gather | solution.py:63
  102.9 1.6 slice_bitcast_fusion
  104.4 1.5 copy.124
  105.9 4.9 %constant_dynamic-slice_fusion.1 = (bf16[1,160,1536]{2,0,1:T(2,128)(2,1)}, bf16[1,160,1536]{2,0,1:T(2,128)(2,1)S(1)}, bf16[1,160,1536]{2,0,1:T(2,128)(2,1)S(1)}, bf16[1,160,1536]{2,0,1:T(2,128)(2,1)S(1)}) fusion(bf16[4,160,1536]{2,0,1:T(4,128)(2,1)S(1)} %bitcast.132, s32[]{:T(128)S(6)} %select_n.37, s32[]{:T(128)S(6)} %select_n.39, s32[]{:T(128)S(6)} %select_n.35, ...), kind=kLoop, calls=%fused_computation.135 | loop fusion | bytes 3932176 | tf_op jit(solution)/shard_map/jit(dynamic_index_in_dim)/dynamic_slice | solution.py:177
  110.8 0.6 fusion.59
  111.4 3.2 %fusion.52 = f32[512,1536]{1,0:T(8,128)} fusion(bf16[160,512]{1,0:T(8,128)(2,1)} %collective-permute-done.2, bf16[1,160,1536]{2,0,1:T(2,128)(2,1)S(1)} %get-tuple-element.33), kind=kOutput, calls=%fused_computation.67 | convolution fusion | flops 251658240 | bytes 3801088 | tf_op jit(solution)/shard_map/dot_general | solution.py:175
  114.6 0.7 copy-done.10
  115.3 1.5 convolution_add_fusion.2
  116.8 9.0 %all-to-all-done = bf16[8,20,6144]{2,1,0:T(8,128)(2,1)} async-done(((bf16[8,20,6144]{2,1,0:T(8,128)(2,1)}), bf16[8,20,6144]{2,1,0:T(8,128)(2,1)}, u32[]{:S(2)}, u32[]{:S(2)}) %all-to-all-start) | async-done | bytes 1966112 | tf_op jit(solution)/shard_map/all_to_all | solution.py:119
  125.8 2.3 %convert_reduce_fusion = f32[20,6144]{1,0:T(8,128)S(1)} fusion(bf16[8,20,6144]{2,1,0:T(8,128)(2,1)} %all-to-all-done), kind=kLoop, calls=%fused_computation.14 | loop fusion | flops 1843200 | bytes 2457600 | tf_op jit(solution)/shard_map/reduce_sum | solution.py:122
  128.1 1.5 multiply_reduce_fusion.1
  129.6 0.4 fusion.98
  130.1 9.5 %all-gather.4 = bf16[8,2,6144]{2,1,0:T(2,128)(2,1)S(1)} all-gather(bf16[1,2,6144]{2,1,0:T(2,128)(2,1)S(1)} %maximum_bitcast_fusion), channel_id=4, replica_groups=mesh['dp'=4,'ctx'=8] {'ctx'}, dimensions={0}, use_global_device_ids=true | all-gather | bytes 221184 | tf_op jit(solution)/shard_map/all_gather | solution.py:137
  139.6 0.2 convert_reduce_fusion.1
  139.8 1.6 collective-permute-start.3
  141.4 1.8 %fusion.13 = bf16[512,1536]{1,0:T(8,128)(2,1)} fusion(f32[512,1536]{1,0:T(8,128)S(1)} %copy-done.2, f32[512,1536]{1,0:T(8,128)S(1)} %convolution_add_fusion.2, bf16[160,512]{1,0:T(8,128)(2,1)S(1)} %collective-permute-done.1, bf16[1,160,1536]{2,0,1:T(2,128)(2,1)S(1)} %copy-done.8), kind=kOutput, calls=%fused_computation.18 | convolution fusion | flops 254017536 | bytes 8519680 | tf_op jit(solution)/shard_map/dot_general | solution.py:175
  143.2 0.6 copy.123
  143.9 2.0 %reshape.201 = bf16[640,1536]{1,0:T(8,128)(2,1)} reshape(bf16[4,8,20,1536]{3,2,1,0:T(8,128)(2,1)S(1)} %copy.123) | data formatting | bytes 3932160 | tf_op jit(solution)/shard_map/reshape | solution.py:66
  145.8 1.0 collective-permute-start.4
  146.9 4.2 %fusion.2 = bf16[1,128,6144]{2,1,0:T(8,128)(2,1)} fusion(bf16[1,128,6144]{2,1,0:T(8,128)(2,1)} %param.11, f32[20,6144]{1,0:T(8,128)S(1)} %copy-done.7, f32[20]{0:T(128)S(1)} %fusion.44, s32[20]{0:T(128)S(1)} %bitcast.150, pred[20]{0:T(512)(128)(4,1)S(1)} %get-tuple-element.28), kind=kOutput, calls=%fused_computation.4 | convolution fusion | flops 191230976 | bytes 3637428 | tf_op jit(solution)/shard_map/dot_general | solution.py:124
  151.0 0.6 add.100
  151.6 1.6 fusion.109
  153.3 2.6 %convolution_convert_fusion.1 = bf16[1536,512]{1,0:T(8,128)(2,1)} fusion(bf16[640,1536]{1,0:T(8,128)(2,1)S(1)} %copy-done.9, bf16[640,512]{1,0:T(8,128)(2,1)S(1)} %bitcast.145), kind=kOutput, calls=%fused_computation.19 | convolution fusion | flops 1007419392 | bytes 4194304 | tf_op jit(solution)/shard_map/dot_general | solution.py:157
  155.9 2.6 %convolution_convert_fusion.2 = bf16[1536,512]{1,0:T(8,128)(2,1)} fusion(bf16[640,1536]{1,0:T(8,128)(2,1)S(1)} %copy-done.9, bf16[640,512]{1,0:T(8,128)(2,1)S(1)} %bitcast.144), kind=kOutput, calls=%fused_computation.20 | convolution fusion | flops 1007419392 | bytes 4194304 | tf_op jit(solution)/shard_map/dot_general | solution.py:157
  158.4 2.6 %convolution_convert_fusion.3 = bf16[1536,512]{1,0:T(8,128)(2,1)} fusion(bf16[640,1536]{1,0:T(8,128)(2,1)S(1)} %copy-done.9, bf16[640,512]{1,0:T(8,128)(2,1)S(1)} %bitcast.143), kind=kOutput, calls=%fused_computation.21 | convolution fusion | flops 1007419392 | bytes 4194304 | tf_op jit(solution)/shard_map/dot_general | solution.py:157
  (51 shorter events, 0.7 us)
Async XLA Ops:
  7.2 5.8 %copy-start = (bf16[1,128,6144]{2,1,0:T(8,128)(2,1)S(1)}, bf16[1,128,6144]{2,1,0:T(8,128)(2,1)}, u32[]{:S(2)}) copy-start(bf16[1,128,6144]{2,1,0:T(8,128)(2,1)} %param.12) | copy-start | bytes 4718596
  7.2 49.0 %all-gather.13.cloned.1.call-start = ((), (), s32[]{:S(2)}) async-start(), calls=%async_computation.4 | async-start | bytes 5363712 | tf_op jit(solution)/shard_map/all_gather | solution.py:52
  11.1 1.5 copy-start.3
  15.7 82.9 %all-gather.9.cloned.1.call-start = ((), (), s32[]{:S(2)}) async-start(), calls=%async_computation.2 | async-start | bytes 4423680 | tf_op jit(solution)/shard_map/all_gather | solution.py:63
  73.9 40.7 %collective-permute-start = (bf16[160,512]{1,0:T(8,128)(2,1)S(1)}, bf16[160,512]{1,0:T(8,128)(2,1)S(1)}, u32[]{:S(2)}, u32[]{:S(2)}) collective-permute-start(bf16[160,512]{1,0:T(8,128)(2,1)S(1)} %bitcast.138), channel_id=1, source_target_pairs={{0,8},{8,16},{16,24},{24,0},{1,9},{9,17},{17,25},{25,1},{2,10},{10... | collective-permute-start | bytes 491528 | tf_op jit(solution)/shard_map/ppermute | solution.py:173
  75.5 36.0 %collective-permute-start.2 = (bf16[160,512]{1,0:T(8,128)(2,1)S(1)}, bf16[160,512]{1,0:T(8,128)(2,1)}, u32[]{:S(2)}, u32[]{:S(2)}) collective-permute-start(bf16[160,512]{1,0:T(8,128)(2,1)S(1)} %bitcast.139), channel_id=1, source_target_pairs={{0,24},{8,0},{16,8},{24,16},{1,25},{9,1},{17,9},{25,17},{2,26},{10... | collective-permute-start | bytes 491528 | tf_op jit(solution)/shard_map/ppermute | solution.py:173
  77.8 63.6 %collective-permute-start.1 = (bf16[160,512]{1,0:T(8,128)(2,1)S(1)}, bf16[160,512]{1,0:T(8,128)(2,1)S(1)}, u32[]{:S(2)}, u32[]{:S(2)}) collective-permute-start(bf16[160,512]{1,0:T(8,128)(2,1)S(1)} %bitcast.140), channel_id=1, source_target_pairs={{0,16},{8,24},{16,0},{24,8},{1,17},{9,25},{17,1},{25,9},{2,18},{10... | collective-permute-start | bytes 491528 | tf_op jit(solution)/shard_map/ppermute | solution.py:173
  92.9 32.9 %all-to-all-start = ((bf16[8,20,6144]{2,1,0:T(8,128)(2,1)}), bf16[8,20,6144]{2,1,0:T(8,128)(2,1)}, u32[]{:S(2)}, u32[]{:S(2)}) async-start(bf16[8,20,6144]{2,1,0:T(8,128)(2,1)} %convolution_convert_fusion), calls=%async_computation | async-start | bytes 4718592 | tf_op jit(solution)/shard_map/all_to_all | solution.py:119
  97.7 53.9 %all-gather.11.cloned.1.call-start = ((), (), s32[]{:S(2)}) async-start(), calls=%async_computation.3 | async-start | bytes 2457600 | tf_op jit(solution)/shard_map/all_gather | solution.py:139
  114.6 0.7 copy-start.10
  125.8 3.8 %copy-start.4 = (f32[20,6144]{1,0:T(8,128)S(1)}, f32[20,6144]{1,0:T(8,128)}, u32[]{:S(2)}) copy-start(f32[20,6144]{1,0:T(8,128)} %copy-done.3) | copy-start | bytes 1474564
  125.8 15.6 %copy-start.2 = (f32[512,1536]{1,0:T(8,128)S(1)}, f32[512,1536]{1,0:T(8,128)}, u32[]{:S(2)}) copy-start(f32[512,1536]{1,0:T(8,128)} %fusion.52) | copy-start | bytes 9437188
  125.8 15.6 %copy-start.8 = (bf16[1,160,1536]{2,0,1:T(2,128)(2,1)S(1)}, bf16[1,160,1536]{2,0,1:T(2,128)(2,1)}, u32[]{:S(2)}) copy-start(bf16[1,160,1536]{2,0,1:T(2,128)(2,1)} %get-tuple-element.32) | copy-start | bytes 1474564
  128.1 13.3 %copy-start.6 = (f32[20,6144]{1,0:T(8,128)}, f32[20,6144]{1,0:T(8,128)S(1)}, u32[]{:S(2)}) copy-start(f32[20,6144]{1,0:T(8,128)S(1)} %convert_reduce_fusion) | copy-start | bytes 1474564
  139.8 6.0 %collective-permute-start.3 = (f32[6144]{0:T(1024)S(1)}, f32[6144]{0:T(1024)S(1)}, u32[]{:S(2)}, u32[]{:S(2)}) collective-permute-start(f32[6144]{0:T(1024)S(1)} %convert_reduce_fusion.1), channel_id=1, source_target_pairs={{0,8},{8,0},{16,24},{24,16},{1,9},{9,1},{17,25},{25,17},{2,10},{10... | collective-permute-start | bytes 73736 | tf_op jit(solution)/shard_map/ppermute | solution.py:185
  141.4 1.8 %copy-start.5 = (bf16[4,8,20,1536]{3,1,2,0:T(8,128)(2,1)S(1)}, bf16[4,8,20,1536]{3,1,2,0:T(8,128)(2,1)}, u32[]{:S(2)}) copy-start(bf16[4,8,20,1536]{3,1,2,0:T(8,128)(2,1)} %get-tuple-element.31) | copy-start | bytes 5898244
  143.8 3.0 %copy-start.7 = (f32[20,6144]{1,0:T(8,128)S(1)}, f32[20,6144]{1,0:T(8,128)}, u32[]{:S(2)}) copy-start(f32[20,6144]{1,0:T(8,128)} %copy-done.6) | copy-start | bytes 1474564
  145.8 5.2 %collective-permute-start.4 = (f32[6144]{0:T(1024)S(1)}, f32[6144]{0:T(1024)S(1)}, u32[]{:S(2)}, u32[]{:S(2)}) collective-permute-start(f32[6144]{0:T(1024)S(1)} %add.99), channel_id=1, source_target_pairs={{0,16},{8,24},{16,0},{24,8},{1,17},{9,25},{17,1},{25,9},{2,18},{10... | collective-permute-start | bytes 73736 | tf_op jit(solution)/shard_map/ppermute | solution.py:185
  151.0 2.2 %copy-start.9 = (bf16[640,1536]{1,0:T(8,128)(2,1)S(1)}, bf16[640,1536]{1,0:T(8,128)(2,1)}, u32[]{:S(2)}) copy-start(bf16[640,1536]{1,0:T(8,128)(2,1)} %reshape.201) | copy-start | bytes 5898244
  158.4 2.6 %copy-start.1 = (bf16[1,128,6144]{2,1,0:T(8,128)(2,1)S(1)}, bf16[1,128,6144]{2,1,0:T(8,128)(2,1)}, u32[]{:S(2)}) copy-start(bf16[1,128,6144]{2,1,0:T(8,128)(2,1)} %param.12) | copy-start | bytes 4718596
Sparse Core Ops, SparseCore 0:
  15.8 40.3 all-gather.12
  58.0 35.6 all-gather.8
  100.1 43.6 all-gather.10

commit v10 on v6

--- a/solution.py
+++ b/solution.py
@@ -139,30 +139,18 @@
     router_high = router_group.astype(jnp.bfloat16)
     router_low = (router_group - router_high.astype(jnp.float32)).astype(jnp.bfloat16)
     factors = lax.all_gather(
-        jnp.concatenate(
-            [
-                query_back,
-                key_back,
-                value_back,
-            ],
-            axis=0,
-        ),
-        "dp",
-        axis=0,
-        tiled=False,
-    )
-
-    def gathered(index):
-        return factors[:, index * slots : (index + 1) * slots].reshape(n_dp * slots, inner)
+        jnp.concatenate([query_back, key_back, value_back], axis=1), "dp", axis=0, tiled=False
+    ).reshape(n_dp * slots, 3 * inner)
 
     def contract(left, right):
         return lax.dot_general(
             left, right, (((0,), (0,)), ((), ())), preferred_element_type=jnp.float32
         ).astype(jnp.bfloat16)
 
-    grad_query = contract(normed_blocks, gathered(0))
-    grad_key = contract(normed_blocks, gathered(1))
-    grad_value = contract(normed_blocks, gathered(2))
+    grads = contract(normed_blocks, factors)
+    grad_query = grads[:, :inner]
+    grad_key = grads[:, inner : 2 * inner]
+    grad_value = grads[:, 2 * inner :]
     dp_index = lax.axis_index("dp")
     delta_by_seq = delta_blocks.reshape(n_dp, slots, block)
     out_total = lax.dot_general(

time: 167 us -> 166 us (level)
    dot_general x3 -> x1, matrix products: 7.73 us -> 6.13 us  [contract(): lax.dot_general(left, right, (((0,), (0,)), ((), ())), preferred_element_...]
where the time goes in v10:
time: 166 us; the launch traced here: 164 us
  matrix products  49 us (30%)
  blocking collectives  27.8 us (17%)
  waiting for transfers between devices  25.2 us (15%)
  local copies, waits for them, and re-layouts  22.6 us (14%)
  between operations  14.9 us (9%)
  starting transfers between devices  14.8 us (9%)
  other arithmetic  9.4 us (6%)
    all_gather x1, waiting for transfers between devices, body(): lax.all_gather(jnp.concatenate([normed, delta, flag_cols], axis=1), 'ctx'...  21.7 us
    all_to_all x1, blocking collectives, body(): lax.all_to_all(jnp.concatenate([normed, delta], axis=0), 'dp', 1, 0, tile...  18.6 us
    dot_general x3, matrix products, project(): lax.dot_general(chunk_normed, weight, (((2,), (0,)), ((), ())), preferred...  14.8 us
    all_gather x1, blocking collectives, body(): lax.all_gather(router_split, 'ctx', axis=0, tiled=False).astype(jnp.float32)  9.27 us
    dot_general x1, matrix products, body(): lax.dot_general(chunk_delta, w_out, (((2,), (1,)), ((), ())), preferred_e...  6.34 us
    dot_general x1, matrix products, contract(): lax.dot_general(left, right, (((0,), (0,)), ((), ())), preferred_element_...  6.13 us
    dot_general x1, matrix products, body(): lax.dot_general(mixed_late.reshape(n_ctx, capacity, inner), w_out, (((2,)...  5.71 us
    ppermute x3, starting transfers between devices, body(): lax.ppermute(router_pair, 'dp', [(i, (i + shift) % n_dp) for i in range(n...  5.39 us
  transfers between devices with their start and end apart: 10, of which 2 were waited for; matrix products, arithmetic and copies ran while one was open for 39% of the time, Pallas kernels for 0%

profile of v10, /device:TPU:2, one launch (start us, length us, event | category | flops | bytes accessed | tf_op | source)
XLA Modules:
  0.0 163.7 jit_solution(5084498948195645536)
XLA Ops:
  7.2 0.6 compare_reduce_fusion.1
  8.5 0.7 compare_and_fusion
  9.2 1.9 %multiply_reduce_fusion.2 = (f32[20]{0:T(128)S(1)}, f32[20,6144]{1,0:T(8,128)S(1)}) fusion(bf16[1,128,6144]{2,1,0:T(8,128)(2,1)} %param.11, s32[20]{0:T(128)S(1)} %bitcast.147, pred[20]{0:T(512)(128)(4,1)S(1)} %get-tuple-element.28), kind=kOutput, calls=%fused_computation.61 | convolution fusion | flops 31708140 | bytes 2064564 | tf_op jit(solution)/shard_map/dot_general | solution.py:41
  11.1 1.4 fusion.44
  12.6 0.1 multiply_convert_fusion.1
  12.7 0.1 copy.156
  12.8 0.1 copy.157
  12.9 1.2 multiply_convert_fusion
  14.1 0.7 fusion.92
  14.8 0.9 fusion.50
  15.7 0.1 pad_maximum_fusion
  15.8 18.6 %all_to_all.21 = bf16[40,4,1536]{2,0,1:T(8,128)(2,1)} all-to-all(bf16[40,4,1536]{2,0,1:T(8,128)(2,1)S(1)} %bitcast.134), channel_id=1, replica_groups=mesh['dp'=4,'ctx'=8] {'dp'}, dimensions={1} | all-to-all | bytes 983040 | tf_op jit(solution)/shard_map/all_to_all | solution.py:60
  34.5 21.7 %all-gather.13.cloned.1.call-done = bf16[8,20,12416]{2,1,0:T(8,128)(2,1)} async-done(((bf16[1,20,12416]{2,1,0:T(8,128)(2,1)}), bf16[8,20,12416]{2,1,0:T(8,128)(2,1)}) %all-gather.13.cloned.1.call-update) | async-done | bytes 3973136 | tf_op jit(solution)/shard_map/all_gather | solution.py:52
  56.2 4.9 %fusion.8 = f32[8,20,512]{2,1,0:T(8,128)S(1)} fusion(bf16[6144,512]{1,0:T(8,128)(2,1)} %param.14, bf16[8,20,12416]{2,1,0:T(8,128)(2,1)} %all-gather.13.cloned.1.call-done), kind=kOutput, calls=%fused_computation.11 | convolution fusion | flops 1006632960 | bytes 8978432 | tf_op jit(solution)/shard_map/dot_general | solution.py:69
  61.1 0.1 reshape_reshape.10
  61.2 0.2 multiply_reduce_fusion.6
  61.5 4.9 %fusion.6 = f32[8,20,512]{2,1,0:T(8,128)S(1)} fusion(bf16[6144,512]{1,0:T(8,128)(2,1)} %param.15, bf16[8,20,12416]{2,1,0:T(8,128)(2,1)} %all-gather.13.cloned.1.call-done), kind=kOutput, calls=%fused_computation.9 | convolution fusion | flops 1006632960 | bytes 8978432 | tf_op jit(solution)/shard_map/dot_general | solution.py:69
  66.4 0.1 reshape_reshape.11
  66.6 0.2 multiply_reduce_fusion.5
  66.9 1.0 compare_reduce_fusion
  68.0 4.9 %fusion.29 = bf16[8,20,512]{2,1,0:T(8,128)(2,1)S(1)} fusion(bf16[6144,512]{1,0:T(8,128)(2,1)} %param.16, bf16[8,20,12416]{2,1,0:T(8,128)(2,1)} %all-gather.13.cloned.1.call-done), kind=kOutput, calls=%fused_computation.41 | convolution fusion | flops 1006714880 | bytes 8814592 | tf_op jit(solution)/shard_map/dot_general | solution.py:69
  73.1 0.4 fusion.63
  73.6 0.3 fusion.39
  73.9 1.5 collective-permute-start
  75.5 2.3 %collective-permute-start.2 = (bf16[160,512]{1,0:T(8,128)(2,1)S(1)}, bf16[160,512]{1,0:T(8,128)(2,1)}, u32[]{:S(2)}, u32[]{:S(2)}) collective-permute-start(bf16[160,512]{1,0:T(8,128)(2,1)S(1)} %bitcast.136), channel_id=1, source_target_pairs={{0,24},{8,0},{16,8},{24,16},{1,25},{9,1},{17,9},{25,17},{2,26},{10... | collective-permute-start | bytes 491528 | tf_op jit(solution)/shard_map/ppermute | solution.py:163
  77.8 0.6 collective-permute-start.1
  78.4 6.3 %fusion.34 = bf16[8,20,512]{2,1,0:T(8,128)(2,1)S(1)} fusion(bf16[512,6144]{1,0:T(8,128)(2,1)} %param.17, bf16[8,20,12416]{2,1,0:T(8,128)(2,1)} %all-gather.13.cloned.1.call-done), kind=kOutput, calls=%fused_computation.42 | convolution fusion | flops 1006714880 | bytes 8814592 | tf_op jit(solution)/shard_map/dot_general | solution.py:91
  84.8 0.2 fusion.40
  85.1 0.3 fusion.76
  85.3 0.5 multiply_reduce_fusion.3
  85.9 0.7 multiply_reduce_fusion.4
  86.6 0.2 copy_bitcast_fusion.2
  86.8 0.2 copy_bitcast_fusion.3
  87.1 5.7 %convolution_convert_fusion.1 = bf16[8,20,6144]{2,1,0:T(8,128)(2,1)} fusion(bf16[8,20,512]{2,1,0:T(8,128)(2,1)S(1)} %reshape.214, bf16[512,6144]{1,0:T(8,128)(2,1)} %param.17), kind=kOutput, calls=%fused_computation.2 | convolution fusion | flops 1007616000 | bytes 8421376 | tf_op jit(solution)/shard_map/dot_general | solution.py:113
  92.8 4.8 %all-to-all-start = ((bf16[8,20,6144]{2,1,0:T(8,128)(2,1)}), bf16[8,20,6144]{2,1,0:T(8,128)(2,1)}, u32[]{:S(2)}, u32[]{:S(2)}) async-start(bf16[8,20,6144]{2,1,0:T(8,128)(2,1)} %convolution_convert_fusion.1), calls=%async_computation | async-start | bytes 4718592 | tf_op jit(solution)/shard_map/all_to_all | solution.py:119
  97.6 0.8 pad_maximum_fusion.1
  98.5 4.3 %copy.173 = bf16[8,160,1536]{2,0,1:T(8,128)(2,1)S(1)} copy(bf16[8,160,1536]{2,1,0:T(8,128)(2,1)} %all-gather.9.cloned.1.call-done) | data formatting | bytes 7864320 | tf_op jit(solution)/shard_map/all_gather | solution.py:63
  102.8 0.3 slice_bitcast_fusion
  103.0 1.5 copy.175
  104.6 5.0 %constant_dynamic-slice_fusion.1 = (bf16[1,160,1536]{2,0,1:T(2,128)(2,1)}, bf16[1,160,1536]{2,0,1:T(2,128)(2,1)}, bf16[1,160,1536]{2,0,1:T(2,128)(2,1)S(1)}, bf16[1,160,1536]{2,0,1:T(2,128)(2,1)S(1)}) fusion(bf16[4,160,1536]{2,0,1:T(4,128)(2,1)S(1)} %bitcast.130, s32[]{:T(128)S(6)} %select_n.48, s32[]{:T(128)S(6)} %select_n.50, s32[]{:T(128)S(6)} %select_n.46, ...), kind=kLoop, calls=%fused_computation.137 | loop fusion | bytes 3932176 | tf_op jit(solution)/shard_map/jit(dynamic_index_in_dim)/dynamic_slice | solution.py:167
  109.6 0.6 fusion.59
  110.2 0.7 copy-done.7
  110.9 1.5 convolution_add_fusion.2
  112.4 2.0 %copy.174 = bf16[4,8,20,1536]{3,2,1,0:T(8,128)(2,1)} copy(bf16[4,8,20,1536]{3,1,2,0:T(8,128)(2,1)S(1)} %get-tuple-element.34) | data formatting | bytes 3932160 | tf_op jit(solution)/shard_map/transpose | solution.py:66
  114.4 4.0 %reshape.216 = bf16[640,1536]{1,0:T(8,128)(2,1)} reshape(bf16[4,8,20,1536]{3,2,1,0:T(8,128)(2,1)} %copy.174) | data formatting | bytes 3932160 | tf_op jit(solution)/shard_map/reshape | solution.py:66
  118.4 2.0 %fusion.52 = f32[512,1536]{1,0:T(8,128)S(1)} fusion(bf16[160,512]{1,0:T(8,128)(2,1)} %collective-permute-done.2, bf16[1,160,1536]{2,0,1:T(2,128)(2,1)} %get-tuple-element.36), kind=kOutput, calls=%fused_computation.65 | convolution fusion | flops 251658240 | bytes 3801088 | tf_op jit(solution)/shard_map/dot_general | solution.py:165
  120.4 1.8 %fusion.13 = bf16[512,1536]{1,0:T(8,128)(2,1)} fusion(f32[512,1536]{1,0:T(8,128)S(1)} %fusion.52, f32[512,1536]{1,0:T(8,128)S(1)} %convolution_add_fusion.2, bf16[160,512]{1,0:T(8,128)(2,1)S(1)} %collective-permute-done.1, bf16[1,160,1536]{2,0,1:T(2,128)(2,1)S(1)} %copy-done.6), kind=kOutput, calls=%fused_computation.19 | convolution fusion | flops 254017536 | bytes 8519680 | tf_op jit(solution)/shard_map/dot_general | solution.py:165
  122.3 3.4 %all-to-all-done = bf16[8,20,6144]{2,1,0:T(8,128)(2,1)} async-done(((bf16[8,20,6144]{2,1,0:T(8,128)(2,1)}), bf16[8,20,6144]{2,1,0:T(8,128)(2,1)}, u32[]{:S(2)}, u32[]{:S(2)}) %all-to-all-start) | async-done | bytes 1966112 | tf_op jit(solution)/shard_map/all_to_all | solution.py:119
  125.7 2.1 %convert_reduce_fusion = f32[20,6144]{1,0:T(8,128)S(1)} fusion(bf16[8,20,6144]{2,1,0:T(8,128)(2,1)} %all-to-all-done), kind=kLoop, calls=%fused_computation.15 | loop fusion | flops 1843200 | bytes 2457600 | tf_op jit(solution)/shard_map/reduce_sum | solution.py:122
  127.8 0.2 multiply_reduce_fusion.1
  128.0 0.4 fusion.99
  128.6 9.3 %all-gather.4 = bf16[8,2,6144]{2,1,0:T(2,128)(2,1)S(1)} all-gather(bf16[1,2,6144]{2,1,0:T(2,128)(2,1)S(1)} %maximum_bitcast_fusion), channel_id=4, replica_groups=mesh['dp'=4,'ctx'=8] {'ctx'}, dimensions={0}, use_global_device_ids=true | all-gather | bytes 221184 | tf_op jit(solution)/shard_map/all_gather | solution.py:137
  137.8 0.2 convert_reduce_fusion.1
  138.1 1.6 collective-permute-start.3
  139.7 1.0 collective-permute-start.4
  140.7 2.8 %collective-permute-start.5 = (bf16[2,6144]{1,0:T(2,128)(2,1)S(1)}, bf16[2,6144]{1,0:T(2,128)(2,1)S(1)}, u32[]{:S(2)}, u32[]{:S(2)}) collective-permute-start(bf16[2,6144]{1,0:T(2,128)(2,1)S(1)} %pad_maximum_fusion.2), channel_id=1, source_target_pairs={{0,24},{8,0},{16,8},{24,16},{1,25},{9,1},{17,9},{25,17},{2,26},{10... | collective-permute-start | bytes 73736 | tf_op jit(solution)/shard_map/ppermute | solution.py:177
  143.6 2.8 %fusion.2 = bf16[1,128,6144]{2,1,0:T(8,128)(2,1)} fusion(bf16[1,128,6144]{2,1,0:T(8,128)(2,1)S(1)} %copy-done.4, f32[20,6144]{1,0:T(8,128)S(1)} %convert_reduce_fusion, f32[20]{0:T(128)S(1)} %fusion.44, s32[20]{0:T(128)S(1)} %bitcast.149, pred[20]{0:T(512)(128)(4,1)S(1)} %get-tuple-element.28), kind=kOutput, calls=%fused_computation.5 | convolution fusion | flops 191230976 | bytes 3637428 | tf_op jit(solution)/shard_map/dot_general | solution.py:124
  146.4 0.3 dynamic_update_slice.13
  147.0 0.3 dynamic_update_slice.14
  147.3 0.3 dynamic_update_slice.15
  147.7 0.3 dynamic_update_slice.16
  148.0 0.7 fusion.80
  148.7 6.1 %convolution_convert_fusion = bf16[1536,1536]{1,0:T(8,128)(2,1)S(1)} fusion(bf16[640,1536]{1,0:T(8,128)(2,1)} %reshape.216, bf16[640,1536]{1,0:T(8,128)(2,1)} %all-gather.11.cloned.1.call-done), kind=kOutput, calls=%fused_computation.1 | convolution fusion | flops 3022258176 | bytes 8650752 | tf_op jit(solution)/shard_map/dot_general | solution.py:146
  154.8 2.3 %fusion.110 = (bf16[1536,512]{1,0:T(8,128)(2,1)}, bf16[1536,512]{1,0:T(8,128)(2,1)}, bf16[1536,512]{1,0:T(8,128)(2,1)}) fusion(bf16[1536,1536]{1,0:T(8,128)(2,1)S(1)} %convolution_convert_fusion), kind=kLoop, calls=%fused_computation.153 | loop fusion | bytes 9437184 | tf_op jit(solution)/shard_map/slice | solution.py:153
  (58 shorter events, 1.3 us)
Async XLA Ops:
  7.2 5.8 %copy-start = (bf16[1,128,6144]{2,1,0:T(8,128)(2,1)S(1)}, bf16[1,128,6144]{2,1,0:T(8,128)(2,1)}, u32[]{:S(2)}) copy-start(bf16[1,128,6144]{2,1,0:T(8,128)(2,1)} %param.12) | copy-start | bytes 4718596
  7.2 49.0 %all-gather.13.cloned.1.call-start = ((), (), s32[]{:S(2)}) async-start(), calls=%async_computation.4 | async-start | bytes 5363712 | tf_op jit(solution)/shard_map/all_gather | solution.py:52
  11.1 1.5 copy-start.2
  15.7 82.8 %all-gather.9.cloned.1.call-start = ((), (), s32[]{:S(2)}) async-start(), calls=%async_computation.2 | async-start | bytes 4423680 | tf_op jit(solution)/shard_map/all_gather | solution.py:63
  73.9 36.3 %collective-permute-start = (bf16[160,512]{1,0:T(8,128)(2,1)S(1)}, bf16[160,512]{1,0:T(8,128)(2,1)S(1)}, u32[]{:S(2)}, u32[]{:S(2)}) collective-permute-start(bf16[160,512]{1,0:T(8,128)(2,1)S(1)} %bitcast.135), channel_id=1, source_target_pairs={{0,8},{8,16},{16,24},{24,0},{1,9},{9,17},{17,25},{25,1},{2,10},{10... | collective-permute-start | bytes 491528 | tf_op jit(solution)/shard_map/ppermute | solution.py:163
  75.5 43.0 %collective-permute-start.2 = (bf16[160,512]{1,0:T(8,128)(2,1)S(1)}, bf16[160,512]{1,0:T(8,128)(2,1)}, u32[]{:S(2)}, u32[]{:S(2)}) collective-permute-start(bf16[160,512]{1,0:T(8,128)(2,1)S(1)} %bitcast.136), channel_id=1, source_target_pairs={{0,24},{8,0},{16,8},{24,16},{1,25},{9,1},{17,9},{25,17},{2,26},{10... | collective-permute-start | bytes 491528 | tf_op jit(solution)/shard_map/ppermute | solution.py:163
  77.8 42.6 %collective-permute-start.1 = (bf16[160,512]{1,0:T(8,128)(2,1)S(1)}, bf16[160,512]{1,0:T(8,128)(2,1)S(1)}, u32[]{:S(2)}, u32[]{:S(2)}) collective-permute-start(bf16[160,512]{1,0:T(8,128)(2,1)S(1)} %bitcast.137), channel_id=1, source_target_pairs={{0,16},{8,24},{16,0},{24,8},{1,17},{9,25},{17,1},{25,9},{2,18},{10... | collective-permute-start | bytes 491528 | tf_op jit(solution)/shard_map/ppermute | solution.py:163
  92.8 32.9 %all-to-all-start = ((bf16[8,20,6144]{2,1,0:T(8,128)(2,1)}), bf16[8,20,6144]{2,1,0:T(8,128)(2,1)}, u32[]{:S(2)}, u32[]{:S(2)}) async-start(bf16[8,20,6144]{2,1,0:T(8,128)(2,1)} %convolution_convert_fusion.1), calls=%async_computation | async-start | bytes 4718592 | tf_op jit(solution)/shard_map/all_to_all | solution.py:119
  97.6 51.1 %all-gather.11.cloned.1.call-start = ((), (), s32[]{:S(2)}) async-start(), calls=%async_computation.3 | async-start | bytes 2457600 | tf_op jit(solution)/shard_map/all_gather | solution.py:141
  110.2 0.7 copy-start.7
  118.4 2.0 %copy-start.6 = (bf16[1,160,1536]{2,0,1:T(2,128)(2,1)S(1)}, bf16[1,160,1536]{2,0,1:T(2,128)(2,1)}, u32[]{:S(2)}) copy-start(bf16[1,160,1536]{2,0,1:T(2,128)(2,1)} %get-tuple-element.35) | copy-start | bytes 1474564
  122.3 5.5 %copy-start.5 = (f32[20,6144]{1,0:T(8,128)S(1)}, f32[20,6144]{1,0:T(8,128)}, u32[]{:S(2)}) copy-start(f32[20,6144]{1,0:T(8,128)} %get-tuple-element.42) | copy-start | bytes 1474564
  122.3 5.7 %copy-start.3 = (f32[20,6144]{1,0:T(8,128)S(1)}, f32[20,6144]{1,0:T(8,128)}, u32[]{:S(2)}) copy-start(f32[20,6144]{1,0:T(8,128)} %copy-done.2) | copy-start | bytes 1474564
  122.3 21.3 %copy-start.4 = (bf16[1,128,6144]{2,1,0:T(8,128)(2,1)S(1)}, bf16[1,128,6144]{2,1,0:T(8,128)(2,1)}, u32[]{:S(2)}) copy-start(bf16[1,128,6144]{2,1,0:T(8,128)(2,1)} %param.11) | copy-start | bytes 4718596
  138.1 8.7 %collective-permute-start.3 = (bf16[2,6144]{1,0:T(2,128)(2,1)S(1)}, bf16[2,6144]{1,0:T(2,128)(2,1)S(1)}, u32[]{:S(2)}, u32[]{:S(2)}) collective-permute-start(bf16[2,6144]{1,0:T(2,128)(2,1)S(1)} %pad_maximum_fusion.2), channel_id=1, source_target_pairs={{0,8},{8,16},{16,24},{24,0},{1,9},{9,17},{17,25},{25,1},{2,10},{10... | collective-permute-start | bytes 73736 | tf_op jit(solution)/shard_map/ppermute | solution.py:177
  139.7 7.1 %collective-permute-start.4 = (bf16[2,6144]{1,0:T(2,128)(2,1)S(1)}, bf16[2,6144]{1,0:T(2,128)(2,1)S(1)}, u32[]{:S(2)}, u32[]{:S(2)}) collective-permute-start(bf16[2,6144]{1,0:T(2,128)(2,1)S(1)} %pad_maximum_fusion.2), channel_id=1, source_target_pairs={{0,16},{8,24},{16,0},{24,8},{1,17},{9,25},{17,1},{25,9},{2,18},{10... | collective-permute-start | bytes 73736 | tf_op jit(solution)/shard_map/ppermute | solution.py:177
  140.7 6.2 %collective-permute-start.5 = (bf16[2,6144]{1,0:T(2,128)(2,1)S(1)}, bf16[2,6144]{1,0:T(2,128)(2,1)S(1)}, u32[]{:S(2)}, u32[]{:S(2)}) collective-permute-start(bf16[2,6144]{1,0:T(2,128)(2,1)S(1)} %pad_maximum_fusion.2), channel_id=1, source_target_pairs={{0,24},{8,0},{16,8},{24,16},{1,25},{9,1},{17,9},{25,17},{2,26},{10... | collective-permute-start | bytes 73736 | tf_op jit(solution)/shard_map/ppermute | solution.py:177
  148.7 8.4 %copy-start.1 = (bf16[1,128,6144]{2,1,0:T(8,128)(2,1)S(1)}, bf16[1,128,6144]{2,1,0:T(8,128)(2,1)}, u32[]{:S(2)}) copy-start(bf16[1,128,6144]{2,1,0:T(8,128)(2,1)} %param.12) | copy-start | bytes 4718596
Sparse Core Ops, SparseCore 0:
  15.8 40.3 all-gather.12
  58.0 35.6 all-gather.8
  100.0 43.8 all-gather.10

commit v11 on v10

--- a/solution.py
+++ b/solution.py
@@ -19,6 +19,14 @@
 
 def norm_back(grad_hat, normal, inverse):
     return inverse * (grad_hat - normal * jnp.mean(grad_hat * normal, axis=-1, keepdims=True))
+
+
+def bf16_pieces(values):
+    high = values.astype(jnp.bfloat16)
+    rest = values - high.astype(jnp.float32)
+    middle = rest.astype(jnp.bfloat16)
+    low = (rest - middle.astype(jnp.float32)).astype(jnp.bfloat16)
+    return jnp.stack([high, middle, low])
 
 
 def rounded_term(part):
@@ -121,10 +129,16 @@
     )
     update = jnp.sum(received.astype(jnp.float32), axis=0)
     scaled = weights[:, None] * update
-    spread = jnp.dot(onehot.astype(jnp.float32).T, scaled, precision=HIGHEST_PRECISION)
+    spread = jnp.sum(
+        jnp.einsum("jt,kjd->ktd", onehot, bf16_pieces(scaled), preferred_element_type=jnp.float32),
+        axis=0,
+    )
     layer_out = (tokens[0].astype(jnp.float32) + spread).astype(jnp.bfloat16)[None]
     gate_back = jnp.sum(rows_back * update, axis=-1) * weights * (1.0 - weights)
-    router_part = jnp.dot(gate_back, rows, precision=HIGHEST_PRECISION)
+    router_part = jnp.sum(
+        jnp.dot(bf16_pieces(gate_back), rows.astype(jnp.bfloat16), preferred_element_type=jnp.float32),
+        axis=0,
+    )
     router_split = jnp.stack(
         [
             router_part.astype(jnp.bfloat16),

time: 166 us -> 171 us (1.030)
  local copies, waits for them, and re-layouts: 22.6 us -> 29.3 us
    unnamed x16 -> x22, local copies, waits for them, and re-layouts: 0.7 us -> 3.84 us
    broadcast_in_dim x3, local copies, waits for them, and re-layouts: 0.12 us -> 2.33 us  [body(): lax.dynamic_update_index_in_dim(router_pieces, arrived, (dp_index + n_dp...]
  transfers between devices with their start and end apart: 10 -> 10, of which waited for: 2 -> 2; matrix products, arithmetic and copies ran while one was open for 39% -> 42% of each run, Pallas kernels for 0% -> 0%
where the time goes in v11:
time: 171 us; the launch traced here: 169 us
  matrix products  47.6 us (28%)
  local copies, waits for them, and re-layouts  29.3 us (17%)
  blocking collectives  27.8 us (16%)
  waiting for transfers between devices  23.6 us (14%)
  between operations  15 us (9%)
  starting transfers between devices  14.7 us (9%)
  other arithmetic  10.7 us (6%)
    all_gather x1, waiting for transfers between devices, body(): lax.all_gather(jnp.concatenate([normed, delta, flag_cols], axis=1), 'ctx'...  20.1 us
    all_to_all x1, blocking collectives, body(): lax.all_to_all(jnp.concatenate([normed, delta], axis=0), 'dp', 1, 0, tile...  18.6 us
    dot_general x3, matrix products, project(): lax.dot_general(chunk_normed, weight, (((2,), (0,)), ((), ())), preferred...  14.8 us
    all_gather x1, blocking collectives, body(): lax.all_gather(router_split, 'ctx', axis=0, tiled=False).astype(jnp.float32)  9.27 us
    dot_general x1, matrix products, body(): lax.dot_general(chunk_delta, w_out, (((2,), (1,)), ((), ())), preferred_e...  6.34 us
    dot_general x1, matrix products, contract(): lax.dot_general(left, right, (((0,), (0,)), ((), ())), preferred_element_...  5.76 us
    dot_general x1, matrix products, body(): lax.dot_general(mixed_late.reshape(n_ctx, capacity, inner), w_out, (((2,)...  5.68 us
    ppermute x3, starting transfers between devices, body(): lax.ppermute(router_pair, 'dp', [(i, (i + shift) % n_dp) for i in range(n...  5.35 us
  transfers between devices with their start and end apart: 10, of which 2 were waited for; matrix products, arithmetic and copies ran while one was open for 42% of the time, Pallas kernels for 0%

profile of v11, /device:TPU:2, one launch (start us, length us, event | category | flops | bytes accessed | tf_op | source)
XLA Modules:
  0.0 168.6 jit_solution(1569957198804962139)
XLA Ops:
  7.2 0.6 compare_reduce_fusion.1
  8.5 0.7 compare_and_fusion
  9.2 1.9 %multiply_reduce_fusion.2 = (f32[20]{0:T(128)S(1)}, f32[20,6144]{1,0:T(8,128)S(1)}) fusion(bf16[1,128,6144]{2,1,0:T(8,128)(2,1)} %param.11, s32[20]{0:T(128)S(1)} %bitcast.173, pred[20]{0:T(512)(128)(4,1)S(1)} %get-tuple-element.58), kind=kOutput, calls=%fused_computation.70 | convolution fusion | flops 31708140 | bytes 2064564 | tf_op jit(solution)/shard_map/dot_general | solution.py:49
  11.1 1.4 fusion.44
  12.9 1.2 multiply_convert_fusion
  14.1 0.8 fusion.99
  14.9 0.9 fusion.55
  16.0 18.6 %all_to_all.21 = bf16[40,4,1536]{2,0,1:T(8,128)(2,1)} all-to-all(bf16[40,4,1536]{2,0,1:T(8,128)(2,1)S(1)} %bitcast.162), channel_id=1, replica_groups=mesh['dp'=4,'ctx'=8] {'dp'}, dimensions={1} | all-to-all | bytes 983040 | tf_op jit(solution)/shard_map/all_to_all | solution.py:68
  34.6 1.6 copy.164
  36.2 20.1 %all-gather.13.cloned.1.call-done = bf16[8,20,12416]{2,1,0:T(8,128)(2,1)} async-done(((bf16[1,20,12416]{2,1,0:T(8,128)(2,1)}), bf16[8,20,12416]{2,1,0:T(8,128)(2,1)}) %all-gather.13.cloned.1.call-update) | async-done | bytes 3973136 | tf_op jit(solution)/shard_map/all_gather | solution.py:60
  56.3 4.9 %fusion.6 = f32[8,20,512]{2,1,0:T(8,128)S(1)} fusion(bf16[6144,512]{1,0:T(8,128)(2,1)} %param.14, bf16[8,20,12416]{2,1,0:T(8,128)(2,1)} %all-gather.13.cloned.1.call-done), kind=kOutput, calls=%fused_computation.8 | convolution fusion | flops 1006632960 | bytes 8978432 | tf_op jit(solution)/shard_map/dot_general | solution.py:77
  61.3 0.2 multiply_reduce_fusion.6
  61.6 4.9 %fusion.4 = f32[8,20,512]{2,1,0:T(8,128)S(1)} fusion(bf16[6144,512]{1,0:T(8,128)(2,1)} %param.15, bf16[8,20,12416]{2,1,0:T(8,128)(2,1)} %all-gather.13.cloned.1.call-done), kind=kOutput, calls=%fused_computation.6 | convolution fusion | flops 1006632960 | bytes 8978432 | tf_op jit(solution)/shard_map/dot_general | solution.py:77
  66.7 0.2 multiply_reduce_fusion.5
  67.0 1.0 compare_reduce_fusion
  68.1 4.9 %fusion.29 = bf16[8,20,512]{2,1,0:T(8,128)(2,1)S(1)} fusion(bf16[6144,512]{1,0:T(8,128)(2,1)} %param.16, bf16[8,20,12416]{2,1,0:T(8,128)(2,1)} %all-gather.13.cloned.1.call-done), kind=kOutput, calls=%fused_computation.42 | convolution fusion | flops 1006714880 | bytes 8814592 | tf_op jit(solution)/shard_map/dot_general | solution.py:77
  73.2 0.4 fusion.69
  73.7 0.3 fusion.39
  74.0 1.5 collective-permute-start
  75.6 2.3 %collective-permute-start.2 = (bf16[160,512]{1,0:T(8,128)(2,1)S(1)}, bf16[160,512]{1,0:T(8,128)(2,1)}, u32[]{:S(2)}, u32[]{:S(2)}) collective-permute-start(bf16[160,512]{1,0:T(8,128)(2,1)S(1)} %bitcast.164), channel_id=1, source_target_pairs={{0,24},{8,0},{16,8},{24,16},{1,25},{9,1},{17,9},{25,17},{2,26},{10... | collective-permute-start | bytes 491528 | tf_op jit(solution)/shard_map/ppermute | solution.py:177
  77.9 0.6 collective-permute-start.1
  78.5 6.3 %fusion.34 = bf16[8,20,512]{2,1,0:T(8,128)(2,1)S(1)} fusion(bf16[512,6144]{1,0:T(8,128)(2,1)} %param.17, bf16[8,20,12416]{2,1,0:T(8,128)(2,1)} %all-gather.13.cloned.1.call-done), kind=kOutput, calls=%fused_computation.43 | convolution fusion | flops 1006714880 | bytes 8814592 | tf_op jit(solution)/shard_map/dot_general | solution.py:99
  84.9 0.2 fusion.40
  85.2 0.3 fusion.82
  85.5 0.5 multiply_reduce_fusion.3
  86.0 0.7 multiply_reduce_fusion.4
  86.7 0.2 copy_bitcast_fusion.2
  86.9 0.2 copy_bitcast_fusion.3
  87.2 5.7 %convolution_convert_fusion.1 = bf16[8,20,6144]{2,1,0:T(8,128)(2,1)} fusion(bf16[8,20,512]{2,1,0:T(8,128)(2,1)S(1)} %reshape.319, bf16[512,6144]{1,0:T(8,128)(2,1)} %param.17), kind=kOutput, calls=%fused_computation.2 | convolution fusion | flops 1007616000 | bytes 8421376 | tf_op jit(solution)/shard_map/dot_general | solution.py:121
  92.9 4.8 %all-to-all-start = ((bf16[8,20,6144]{2,1,0:T(8,128)(2,1)}), bf16[8,20,6144]{2,1,0:T(8,128)(2,1)}, u32[]{:S(2)}, u32[]{:S(2)}) async-start(bf16[8,20,6144]{2,1,0:T(8,128)(2,1)} %convolution_convert_fusion.1), calls=%async_computation | async-start | bytes 4718592 | tf_op jit(solution)/shard_map/all_to_all | solution.py:127
  97.7 0.8 pad_maximum_fusion.1
  98.6 4.3 %copy.182 = bf16[8,160,1536]{2,0,1:T(8,128)(2,1)S(1)} copy(bf16[8,160,1536]{2,1,0:T(8,128)(2,1)} %all-gather.9.cloned.1.call-done) | data formatting | bytes 7864320 | tf_op jit(solution)/shard_map/all_gather | solution.py:71
  102.9 0.3 slice_bitcast_fusion
  103.1 1.5 copy.184
  104.7 5.0 %constant_dynamic-slice_fusion.1 = (bf16[1,160,1536]{2,0,1:T(2,128)(2,1)}, bf16[1,160,1536]{2,0,1:T(2,128)(2,1)}, bf16[1,160,1536]{2,0,1:T(2,128)(2,1)S(1)}, bf16[1,160,1536]{2,0,1:T(2,128)(2,1)S(1)}) fusion(bf16[4,160,1536]{2,0,1:T(4,128)(2,1)S(1)} %bitcast.158, s32[]{:T(128)S(6)} %select_n.48, s32[]{:T(128)S(6)} %select_n.50, s32[]{:T(128)S(6)} %select_n.46, ...), kind=kLoop, calls=%fused_computation.154 | loop fusion | bytes 3932176 | tf_op jit(solution)/shard_map/jit(dynamic_index_in_dim)/dynamic_slice | solution.py:181
  109.7 0.6 fusion.64
  110.3 0.7 copy-done.9
  111.0 1.5 convolution_add_fusion.1
  112.5 2.1 %copy.183 = bf16[4,8,20,1536]{3,2,1,0:T(8,128)(2,1)} copy(bf16[4,8,20,1536]{3,1,2,0:T(8,128)(2,1)S(1)} %get-tuple-element.64) | data formatting | bytes 3932160 | tf_op jit(solution)/shard_map/transpose | solution.py:74
  114.6 4.0 %reshape.321 = bf16[640,1536]{1,0:T(8,128)(2,1)} reshape(bf16[4,8,20,1536]{3,2,1,0:T(8,128)(2,1)} %copy.183) | data formatting | bytes 3932160 | tf_op jit(solution)/shard_map/reshape | solution.py:74
  118.6 2.0 %fusion.57 = f32[512,1536]{1,0:T(8,128)S(1)} fusion(bf16[160,512]{1,0:T(8,128)(2,1)} %collective-permute-done.2, bf16[1,160,1536]{2,0,1:T(2,128)(2,1)} %get-tuple-element.66), kind=kOutput, calls=%fused_computation.75 | convolution fusion | flops 251658240 | bytes 3801088 | tf_op jit(solution)/shard_map/dot_general | solution.py:179
  120.6 1.8 %fusion.12 = bf16[512,1536]{1,0:T(8,128)(2,1)} fusion(f32[512,1536]{1,0:T(8,128)S(1)} %fusion.57, f32[512,1536]{1,0:T(8,128)S(1)} %convolution_add_fusion.1, bf16[160,512]{1,0:T(8,128)(2,1)S(1)} %collective-permute-done.1, bf16[1,160,1536]{2,0,1:T(2,128)(2,1)S(1)} %copy-done.7), kind=kOutput, calls=%fused_computation.18 | convolution fusion | flops 254017536 | bytes 8519680 | tf_op jit(solution)/shard_map/dot_general | solution.py:179
  122.4 3.4 %all-to-all-done = bf16[8,20,6144]{2,1,0:T(8,128)(2,1)} async-done(((bf16[8,20,6144]{2,1,0:T(8,128)(2,1)}), bf16[8,20,6144]{2,1,0:T(8,128)(2,1)}, u32[]{:S(2)}, u32[]{:S(2)}) %all-to-all-start) | async-done | bytes 1966112 | tf_op jit(solution)/shard_map/all_to_all | solution.py:127
  125.8 2.1 %convert_reduce_fusion = f32[20,6144]{1,0:T(8,128)S(1)} fusion(bf16[8,20,6144]{2,1,0:T(8,128)(2,1)} %all-to-all-done), kind=kLoop, calls=%fused_computation.12 | loop fusion | flops 1843200 | bytes 2457600 | tf_op jit(solution)/shard_map/reduce_sum | solution.py:130
  127.9 0.2 multiply_reduce_fusion.1
  128.4 9.3 %all-gather.4 = bf16[8,2,6144]{2,1,0:T(2,128)(2,1)S(1)} all-gather(bf16[1,2,6144]{2,1,0:T(2,128)(2,1)S(1)} %maximum_bitcast_fusion), channel_id=4, replica_groups=mesh['dp'=4,'ctx'=8] {'ctx'}, dimensions={0}, use_global_device_ids=true | all-gather | bytes 221184 | tf_op jit(solution)/shard_map/all_gather | solution.py:151
  138.0 0.7 pad_maximum_fusion.2
  138.7 1.5 collective-permute-start.3
  140.2 0.9 collective-permute-start.4
  141.1 2.9 %collective-permute-start.5 = (bf16[2,6144]{1,0:T(2,128)(2,1)}, bf16[2,6144]{1,0:T(2,128)(2,1)}, u32[]{:S(2)}, u32[]{:S(2)}) collective-permute-start(bf16[2,6144]{1,0:T(2,128)(2,1)} %pad_maximum_fusion.2), channel_id=1, source_target_pairs={{0,24},{8,0},{16,8},{24,16},{1,25},{9,1},{17,9},{25,17},{2,26},{10... | collective-permute-start | bytes 73736 | tf_op jit(solution)/shard_map/ppermute | solution.py:191
  144.2 1.9 %convolution_reduce_fusion = f32[6144,128]{1,0:T(8,128)S(1)} fusion(bf16[1,20,6144]{2,1,0:T(8,128)(2,1)S(1)} %get-tuple-element.70, bf16[1,20,6144]{2,1,0:T(8,128)(2,1)S(1)} %get-tuple-element.71, bf16[1,20,6144]{2,1,0:T(8,128)(2,1)S(1)} %get-tuple-element.69, s32[20]{0:T(128)S(1)} %bitcast.175, pred[20]{0:T(512)(128)(4,1)S(1)} %get-tuple-element.58), kind=kOutput, calls=%fused_computation.19 | convolution fusion | flops 96687104 | bytes 3883108 | tf_op jit(solution)/shard_map/jt,kjd->ktd/dot_general | solution.py:133
  146.1 0.3 fusion.17
  146.5 0.7 copy.185
  147.2 1.6 copy.189
  148.8 1.1 dynamic_update_slice.13
  149.9 0.8 copy.186
  150.7 0.8 copy.187
  151.5 0.8 copy.188
  152.3 0.3 dynamic_update_slice.14
  152.7 0.3 dynamic_update_slice.15
  153.0 0.3 dynamic_update_slice.16
  153.4 0.7 fusion.86
  154.0 5.8 %convolution_convert_fusion = bf16[1536,1536]{1,0:T(8,128)(2,1)S(1)} fusion(bf16[640,1536]{1,0:T(8,128)(2,1)S(1)} %copy-done.8, bf16[640,1536]{1,0:T(8,128)(2,1)} %all-gather.11.cloned.1.call-done), kind=kOutput, calls=%fused_computation.1 | convolution fusion | flops 3022258176 | bytes 8650752 | tf_op jit(solution)/shard_map/dot_general | solution.py:160
  159.8 2.3 %fusion.117 = (bf16[1536,512]{1,0:T(8,128)(2,1)}, bf16[1536,512]{1,0:T(8,128)(2,1)}, bf16[1536,512]{1,0:T(8,128)(2,1)}) fusion(bf16[1536,1536]{1,0:T(8,128)(2,1)S(1)} %convolution_convert_fusion), kind=kLoop, calls=%fused_computation.170 | loop fusion | bytes 9437184 | tf_op jit(solution)/shard_map/slice | solution.py:167
  (67 shorter events, 2.3 us)
Async XLA Ops:
  7.2 5.8 %copy-start = (bf16[1,128,6144]{2,1,0:T(8,128)(2,1)S(1)}, bf16[1,128,6144]{2,1,0:T(8,128)(2,1)}, u32[]{:S(2)}) copy-start(bf16[1,128,6144]{2,1,0:T(8,128)(2,1)} %param.12) | copy-start | bytes 4718596
  7.2 49.1 %all-gather.13.cloned.1.call-start = ((), (), s32[]{:S(2)}) async-start(), calls=%async_computation.4 | async-start | bytes 5363712 | tf_op jit(solution)/shard_map/all_gather | solution.py:60
  11.1 1.5 copy-start.2
  14.1 20.5 %copy-start.4 = (bf16[1,128,6144]{2,1,0:T(8,128)(2,1)S(1)}, bf16[1,128,6144]{2,1,0:T(8,128)(2,1)}, u32[]{:S(2)}) copy-start(bf16[1,128,6144]{2,1,0:T(8,128)(2,1)} %param.11) | copy-start | bytes 4718596
  15.8 82.8 %all-gather.9.cloned.1.call-start = ((), (), s32[]{:S(2)}) async-start(), calls=%async_computation.2 | async-start | bytes 4423680 | tf_op jit(solution)/shard_map/all_gather | solution.py:71
  74.0 36.3 %collective-permute-start = (bf16[160,512]{1,0:T(8,128)(2,1)S(1)}, bf16[160,512]{1,0:T(8,128)(2,1)S(1)}, u32[]{:S(2)}, u32[]{:S(2)}) collective-permute-start(bf16[160,512]{1,0:T(8,128)(2,1)S(1)} %bitcast.163), channel_id=1, source_target_pairs={{0,8},{8,16},{16,24},{24,0},{1,9},{9,17},{17,25},{25,1},{2,10},{10... | collective-permute-start | bytes 491528 | tf_op jit(solution)/shard_map/ppermute | solution.py:177
  75.6 43.0 %collective-permute-start.2 = (bf16[160,512]{1,0:T(8,128)(2,1)S(1)}, bf16[160,512]{1,0:T(8,128)(2,1)}, u32[]{:S(2)}, u32[]{:S(2)}) collective-permute-start(bf16[160,512]{1,0:T(8,128)(2,1)S(1)} %bitcast.164), channel_id=1, source_target_pairs={{0,24},{8,0},{16,8},{24,16},{1,25},{9,1},{17,9},{25,17},{2,26},{10... | collective-permute-start | bytes 491528 | tf_op jit(solution)/shard_map/ppermute | solution.py:177
  77.9 42.6 %collective-permute-start.1 = (bf16[160,512]{1,0:T(8,128)(2,1)S(1)}, bf16[160,512]{1,0:T(8,128)(2,1)S(1)}, u32[]{:S(2)}, u32[]{:S(2)}) collective-permute-start(bf16[160,512]{1,0:T(8,128)(2,1)S(1)} %bitcast.165), channel_id=1, source_target_pairs={{0,16},{8,24},{16,0},{24,8},{1,17},{9,25},{17,1},{25,9},{2,18},{10... | collective-permute-start | bytes 491528 | tf_op jit(solution)/shard_map/ppermute | solution.py:177
  92.9 32.9 %all-to-all-start = ((bf16[8,20,6144]{2,1,0:T(8,128)(2,1)}), bf16[8,20,6144]{2,1,0:T(8,128)(2,1)}, u32[]{:S(2)}, u32[]{:S(2)}) async-start(bf16[8,20,6144]{2,1,0:T(8,128)(2,1)} %convolution_convert_fusion.1), calls=%async_computation | async-start | bytes 4718592 | tf_op jit(solution)/shard_map/all_to_all | solution.py:127
  97.7 56.3 %all-gather.11.cloned.1.call-start = ((), (), s32[]{:S(2)}) async-start(), calls=%async_computation.3 | async-start | bytes 2457600 | tf_op jit(solution)/shard_map/all_gather | solution.py:155
  110.3 0.7 copy-start.9
  118.6 2.0 %copy-start.7 = (bf16[1,160,1536]{2,0,1:T(2,128)(2,1)S(1)}, bf16[1,160,1536]{2,0,1:T(2,128)(2,1)}, u32[]{:S(2)}) copy-start(bf16[1,160,1536]{2,0,1:T(2,128)(2,1)} %get-tuple-element.65) | copy-start | bytes 1474564
  122.4 5.5 %copy-start.6 = (f32[20,6144]{1,0:T(8,128)S(1)}, f32[20,6144]{1,0:T(8,128)}, u32[]{:S(2)}) copy-start(f32[20,6144]{1,0:T(8,128)} %get-tuple-element.77) | copy-start | bytes 1474564
  122.4 5.7 %copy-start.3 = (f32[20,6144]{1,0:T(8,128)S(1)}, f32[20,6144]{1,0:T(8,128)}, u32[]{:S(2)}) copy-start(f32[20,6144]{1,0:T(8,128)} %copy-done.2) | copy-start | bytes 1474564
  137.9 8.2 %copy-start.5 = (bf16[1,128,6144]{1,2,0:T(8,128)(2,1)S(1)}, bf16[1,128,6144]{1,2,0:T(8,128)(2,1)}, u32[]{:S(2)}) copy-start(bf16[1,128,6144]{1,2,0:T(8,128)(2,1)} %copy.164) | copy-start | bytes 4718596
  138.7 11.3 %collective-permute-start.3 = (bf16[2,6144]{1,0:T(2,128)(2,1)}, bf16[2,6144]{1,0:T(2,128)(2,1)}, u32[]{:S(2)}, u32[]{:S(2)}) collective-permute-start(bf16[2,6144]{1,0:T(2,128)(2,1)} %pad_maximum_fusion.2), channel_id=1, source_target_pairs={{0,8},{8,16},{16,24},{24,0},{1,9},{9,17},{17,25},{25,1},{2,10},{10... | collective-permute-start | bytes 73736 | tf_op jit(solution)/shard_map/ppermute | solution.py:191
  140.2 10.6 %collective-permute-start.4 = (bf16[2,6144]{1,0:T(2,128)(2,1)}, bf16[2,6144]{1,0:T(2,128)(2,1)}, u32[]{:S(2)}, u32[]{:S(2)}) collective-permute-start(bf16[2,6144]{1,0:T(2,128)(2,1)} %pad_maximum_fusion.2), channel_id=1, source_target_pairs={{0,16},{8,24},{16,0},{24,8},{1,17},{9,25},{17,1},{25,9},{2,18},{10... | collective-permute-start | bytes 73736 | tf_op jit(solution)/shard_map/ppermute | solution.py:191
  141.1 10.4 %collective-permute-start.5 = (bf16[2,6144]{1,0:T(2,128)(2,1)}, bf16[2,6144]{1,0:T(2,128)(2,1)}, u32[]{:S(2)}, u32[]{:S(2)}) collective-permute-start(bf16[2,6144]{1,0:T(2,128)(2,1)} %pad_maximum_fusion.2), channel_id=1, source_target_pairs={{0,24},{8,0},{16,8},{24,16},{1,25},{9,1},{17,9},{25,17},{2,26},{10... | collective-permute-start | bytes 73736 | tf_op jit(solution)/shard_map/ppermute | solution.py:191
  146.5 7.6 %copy-start.8 = (bf16[640,1536]{1,0:T(8,128)(2,1)S(1)}, bf16[640,1536]{1,0:T(8,128)(2,1)}, u32[]{:S(2)}) copy-start(bf16[640,1536]{1,0:T(8,128)(2,1)} %reshape.321) | copy-start | bytes 5898244
  154.0 8.1 %copy-start.1 = (bf16[1,128,6144]{2,1,0:T(8,128)(2,1)S(1)}, bf16[1,128,6144]{2,1,0:T(8,128)(2,1)}, u32[]{:S(2)}) copy-start(bf16[1,128,6144]{2,1,0:T(8,128)(2,1)} %param.12) | copy-start | bytes 4718596
Sparse Core Ops, SparseCore 0:
  15.9 40.3 all-gather.12
  58.2 35.6 all-gather.8
  100.1 43.5 all-gather.10

commit v12 on v10

--- a/solution.py
+++ b/solution.py
@@ -125,17 +125,7 @@
     layer_out = (tokens[0].astype(jnp.float32) + spread).astype(jnp.bfloat16)[None]
     gate_back = jnp.sum(rows_back * update, axis=-1) * weights * (1.0 - weights)
     router_part = jnp.dot(gate_back, rows, precision=HIGHEST_PRECISION)
-    router_split = jnp.stack(
-        [
-            router_part.astype(jnp.bfloat16),
-            (router_part - router_part.astype(jnp.bfloat16).astype(jnp.float32)).astype(
-                jnp.bfloat16
-            ),
-        ]
-    )
-    router_group = jnp.sum(
-        lax.all_gather(router_split, "ctx", axis=0, tiled=False).astype(jnp.float32), axis=(0, 1)
-    )
+    router_group = jnp.sum(lax.all_gather(router_part, "ctx", axis=0, tiled=False), axis=0)
     router_high = router_group.astype(jnp.bfloat16)
     router_low = (router_group - router_high.astype(jnp.float32)).astype(jnp.bfloat16)
     factors = lax.all_gather(

time: 166 us -> 166 us (level)
  no operation moved by 1% of the time
where the time goes in v12:
time: 166 us; the launch traced here: 163 us
  matrix products  49 us (30%)
  blocking collectives  27.8 us (17%)
  waiting for transfers between devices  25.2 us (15%)
  local copies, waits for them, and re-layouts  22.6 us (14%)
  between operations  14.9 us (9%)
  starting transfers between devices  14.8 us (9%)
  other arithmetic  9.17 us (6%)
    all_gather x1, waiting for transfers between devices, body(): lax.all_gather(jnp.concatenate([normed, delta, flag_cols], axis=1), 'ctx'...  21.7 us
    all_to_all x1, blocking collectives, body(): lax.all_to_all(jnp.concatenate([normed, delta], axis=0), 'dp', 1, 0, tile...  18.6 us
    dot_general x3, matrix products, project(): lax.dot_general(chunk_normed, weight, (((2,), (0,)), ((), ())), preferred...  14.8 us
    all_gather x1, blocking collectives, body(): lax.all_gather(router_part, 'ctx', axis=0, tiled=False)  9.27 us
    dot_general x1, matrix products, body(): lax.dot_general(chunk_delta, w_out, (((2,), (1,)), ((), ())), preferred_e...  6.34 us
    dot_general x1, matrix products, contract(): lax.dot_general(left, right, (((0,), (0,)), ((), ())), preferred_element_...  6.13 us
    dot_general x1, matrix products, body(): lax.dot_general(mixed_late.reshape(n_ctx, capacity, inner), w_out, (((2,)...  5.71 us
    ppermute x3, starting transfers between devices, body(): lax.ppermute(router_pair, 'dp', [(i, (i + shift) % n_dp) for i in range(n...  5.39 us
  transfers between devices with their start and end apart: 10, of which 2 were waited for; matrix products, arithmetic and copies ran while one was open for 39% of the time, Pallas kernels for 0%

profile of v12, /device:TPU:2, one launch (start us, length us, event | category | flops | bytes accessed | tf_op | source)
XLA Modules:
  0.0 163.4 jit_solution(13383185385864482506)
XLA Ops:
  7.2 0.6 compare_reduce_fusion.1
  8.5 0.7 compare_and_fusion
  9.2 1.9 %multiply_reduce_fusion.2 = (f32[20]{0:T(128)S(1)}, f32[20,6144]{1,0:T(8,128)S(1)}) fusion(bf16[1,128,6144]{2,1,0:T(8,128)(2,1)} %param.11, s32[20]{0:T(128)S(1)} %bitcast.145, pred[20]{0:T(512)(128)(4,1)S(1)} %get-tuple-element.26), kind=kOutput, calls=%fused_computation.61 | convolution fusion | flops 31708140 | bytes 2064564 | tf_op jit(solution)/shard_map/dot_general | solution.py:41
  11.1 1.4 fusion.44
  12.6 0.1 multiply_convert_fusion.1
  12.7 0.1 copy.156
  12.8 0.1 copy.157
  12.9 1.2 multiply_convert_fusion
  14.1 0.7 fusion.92
  14.8 0.9 fusion.50
  15.7 0.1 pad_maximum_fusion
  15.8 18.6 %all_to_all.21 = bf16[40,4,1536]{2,0,1:T(8,128)(2,1)} all-to-all(bf16[40,4,1536]{2,0,1:T(8,128)(2,1)S(1)} %bitcast.132), channel_id=1, replica_groups=mesh['dp'=4,'ctx'=8] {'dp'}, dimensions={1} | all-to-all | bytes 983040 | tf_op jit(solution)/shard_map/all_to_all | solution.py:60
  34.5 21.7 %all-gather.12.cloned.1.call-done = bf16[8,20,12416]{2,1,0:T(8,128)(2,1)} async-done(((bf16[1,20,12416]{2,1,0:T(8,128)(2,1)}), bf16[8,20,12416]{2,1,0:T(8,128)(2,1)}) %all-gather.12.cloned.1.call-update) | async-done | bytes 3973136 | tf_op jit(solution)/shard_map/all_gather | solution.py:52
  56.2 4.9 %fusion.8 = f32[8,20,512]{2,1,0:T(8,128)S(1)} fusion(bf16[6144,512]{1,0:T(8,128)(2,1)} %param.14, bf16[8,20,12416]{2,1,0:T(8,128)(2,1)} %all-gather.12.cloned.1.call-done), kind=kOutput, calls=%fused_computation.11 | convolution fusion | flops 1006632960 | bytes 8978432 | tf_op jit(solution)/shard_map/dot_general | solution.py:69
  61.1 0.1 reshape_reshape.10
  61.2 0.2 multiply_reduce_fusion.6
  61.5 4.9 %fusion.6 = f32[8,20,512]{2,1,0:T(8,128)S(1)} fusion(bf16[6144,512]{1,0:T(8,128)(2,1)} %param.15, bf16[8,20,12416]{2,1,0:T(8,128)(2,1)} %all-gather.12.cloned.1.call-done), kind=kOutput, calls=%fused_computation.9 | convolution fusion | flops 1006632960 | bytes 8978432 | tf_op jit(solution)/shard_map/dot_general | solution.py:69
  66.4 0.1 reshape_reshape.11
  66.6 0.2 multiply_reduce_fusion.5
  66.9 1.0 compare_reduce_fusion
  68.0 4.9 %fusion.29 = bf16[8,20,512]{2,1,0:T(8,128)(2,1)S(1)} fusion(bf16[6144,512]{1,0:T(8,128)(2,1)} %param.16, bf16[8,20,12416]{2,1,0:T(8,128)(2,1)} %all-gather.12.cloned.1.call-done), kind=kOutput, calls=%fused_computation.41 | convolution fusion | flops 1006714880 | bytes 8814592 | tf_op jit(solution)/shard_map/dot_general | solution.py:69
  73.0 0.1 fusion.73
  73.1 0.4 fusion.63
  73.6 0.3 fusion.39
  73.9 1.5 collective-permute-start
  75.5 2.3 %collective-permute-start.2 = (bf16[160,512]{1,0:T(8,128)(2,1)S(1)}, bf16[160,512]{1,0:T(8,128)(2,1)}, u32[]{:S(2)}, u32[]{:S(2)}) collective-permute-start(bf16[160,512]{1,0:T(8,128)(2,1)S(1)} %bitcast.134), channel_id=1, source_target_pairs={{0,24},{8,0},{16,8},{24,16},{1,25},{9,1},{17,9},{25,17},{2,26},{10... | collective-permute-start | bytes 491528 | tf_op jit(solution)/shard_map/ppermute | solution.py:153
  77.8 0.6 collective-permute-start.1
  78.4 6.3 %fusion.34 = bf16[8,20,512]{2,1,0:T(8,128)(2,1)S(1)} fusion(bf16[512,6144]{1,0:T(8,128)(2,1)} %param.17, bf16[8,20,12416]{2,1,0:T(8,128)(2,1)} %all-gather.12.cloned.1.call-done), kind=kOutput, calls=%fused_computation.42 | convolution fusion | flops 1006714880 | bytes 8814592 | tf_op jit(solution)/shard_map/dot_general | solution.py:91
  84.8 0.2 fusion.40
  85.1 0.3 fusion.76
  85.3 0.5 multiply_reduce_fusion.3
  85.9 0.7 multiply_reduce_fusion.4
  86.6 0.2 copy_bitcast_fusion.2
  86.8 0.2 copy_bitcast_fusion.3
  87.1 5.7 %convolution_convert_fusion.1 = bf16[8,20,6144]{2,1,0:T(8,128)(2,1)} fusion(bf16[8,20,512]{2,1,0:T(8,128)(2,1)S(1)} %reshape.214, bf16[512,6144]{1,0:T(8,128)(2,1)} %param.17), kind=kOutput, calls=%fused_computation.2 | convolution fusion | flops 1007616000 | bytes 8421376 | tf_op jit(solution)/shard_map/dot_general | solution.py:113
  92.8 4.8 %all-to-all-start = ((bf16[8,20,6144]{2,1,0:T(8,128)(2,1)}), bf16[8,20,6144]{2,1,0:T(8,128)(2,1)}, u32[]{:S(2)}, u32[]{:S(2)}) async-start(bf16[8,20,6144]{2,1,0:T(8,128)(2,1)} %convolution_convert_fusion.1), calls=%async_computation | async-start | bytes 4718592 | tf_op jit(solution)/shard_map/all_to_all | solution.py:119
  97.6 0.8 pad_maximum_fusion.1
  98.5 4.3 %copy.173 = bf16[8,160,1536]{2,0,1:T(8,128)(2,1)S(1)} copy(bf16[8,160,1536]{2,1,0:T(8,128)(2,1)} %all-gather.8.cloned.1.call-done) | data formatting | bytes 7864320 | tf_op jit(solution)/shard_map/all_gather | solution.py:63
  102.8 0.3 slice_bitcast_fusion
  103.0 1.5 copy.175
  104.6 5.0 %constant_dynamic-slice_fusion.1 = (bf16[1,160,1536]{2,0,1:T(2,128)(2,1)}, bf16[1,160,1536]{2,0,1:T(2,128)(2,1)}, bf16[1,160,1536]{2,0,1:T(2,128)(2,1)S(1)}, bf16[1,160,1536]{2,0,1:T(2,128)(2,1)S(1)}) fusion(bf16[4,160,1536]{2,0,1:T(4,128)(2,1)S(1)} %bitcast.128, s32[]{:T(128)S(6)} %select_n.48, s32[]{:T(128)S(6)} %select_n.50, s32[]{:T(128)S(6)} %select_n.46, ...), kind=kLoop, calls=%fused_computation.134 | loop fusion | bytes 3932176 | tf_op jit(solution)/shard_map/jit(dynamic_index_in_dim)/dynamic_slice | solution.py:157
  109.6 0.6 fusion.59
  110.2 0.7 copy-done.7
  110.9 1.5 convolution_add_fusion.2
  112.4 2.0 %copy.174 = bf16[4,8,20,1536]{3,2,1,0:T(8,128)(2,1)} copy(bf16[4,8,20,1536]{3,1,2,0:T(8,128)(2,1)S(1)} %get-tuple-element.32) | data formatting | bytes 3932160 | tf_op jit(solution)/shard_map/transpose | solution.py:66
  114.4 4.0 %reshape.216 = bf16[640,1536]{1,0:T(8,128)(2,1)} reshape(bf16[4,8,20,1536]{3,2,1,0:T(8,128)(2,1)} %copy.174) | data formatting | bytes 3932160 | tf_op jit(solution)/shard_map/reshape | solution.py:66
  118.4 2.0 %fusion.52 = f32[512,1536]{1,0:T(8,128)S(1)} fusion(bf16[160,512]{1,0:T(8,128)(2,1)} %collective-permute-done.2, bf16[1,160,1536]{2,0,1:T(2,128)(2,1)} %get-tuple-element.34), kind=kOutput, calls=%fused_computation.65 | convolution fusion | flops 251658240 | bytes 3801088 | tf_op jit(solution)/shard_map/dot_general | solution.py:155
  120.4 1.8 %fusion.13 = bf16[512,1536]{1,0:T(8,128)(2,1)} fusion(f32[512,1536]{1,0:T(8,128)S(1)} %fusion.52, f32[512,1536]{1,0:T(8,128)S(1)} %convolution_add_fusion.2, bf16[160,512]{1,0:T(8,128)(2,1)S(1)} %collective-permute-done.1, bf16[1,160,1536]{2,0,1:T(2,128)(2,1)S(1)} %copy-done.6), kind=kOutput, calls=%fused_computation.19 | convolution fusion | flops 254017536 | bytes 8519680 | tf_op jit(solution)/shard_map/dot_general | solution.py:155
  122.3 3.4 %all-to-all-done = bf16[8,20,6144]{2,1,0:T(8,128)(2,1)} async-done(((bf16[8,20,6144]{2,1,0:T(8,128)(2,1)}), bf16[8,20,6144]{2,1,0:T(8,128)(2,1)}, u32[]{:S(2)}, u32[]{:S(2)}) %all-to-all-start) | async-done | bytes 1966112 | tf_op jit(solution)/shard_map/all_to_all | solution.py:119
  125.7 2.1 %convert_reduce_fusion = f32[20,6144]{1,0:T(8,128)S(1)} fusion(bf16[8,20,6144]{2,1,0:T(8,128)(2,1)} %all-to-all-done), kind=kLoop, calls=%fused_computation.15 | loop fusion | flops 1843200 | bytes 2457600 | tf_op jit(solution)/shard_map/reduce_sum | solution.py:122
  127.8 0.2 multiply_reduce_fusion.1
  128.0 0.4 fusion.99
  128.4 9.3 %all-gather.2 = f32[49152]{0:T(1024)S(1)} all-gather(f32[6144]{0:T(1024)S(1)} %bitcast.140), channel_id=4, replica_groups=mesh['dp'=4,'ctx'=8] {'ctx'}, dimensions={0}, use_global_device_ids=true | all-gather | bytes 221184 | tf_op jit(solution)/shard_map/all_gather | solution.py:128
  137.9 1.6 collective-permute-start.3
  139.5 1.0 collective-permute-start.4
  140.4 2.8 %collective-permute-start.5 = (bf16[2,6144]{1,0:T(2,128)(2,1)S(1)}, bf16[2,6144]{1,0:T(2,128)(2,1)S(1)}, u32[]{:S(2)}, u32[]{:S(2)}) collective-permute-start(bf16[2,6144]{1,0:T(2,128)(2,1)S(1)} %pad_maximum_fusion.2), channel_id=1, source_target_pairs={{0,24},{8,0},{16,8},{24,16},{1,25},{9,1},{17,9},{25,17},{2,26},{10... | collective-permute-start | bytes 73736 | tf_op jit(solution)/shard_map/ppermute | solution.py:167
  143.4 2.8 %fusion.2 = bf16[1,128,6144]{2,1,0:T(8,128)(2,1)} fusion(bf16[1,128,6144]{2,1,0:T(8,128)(2,1)S(1)} %copy-done.4, f32[20,6144]{1,0:T(8,128)S(1)} %convert_reduce_fusion, f32[20]{0:T(128)S(1)} %fusion.44, s32[20]{0:T(128)S(1)} %bitcast.147, pred[20]{0:T(512)(128)(4,1)S(1)} %get-tuple-element.26), kind=kOutput, calls=%fused_computation.5 | convolution fusion | flops 191230976 | bytes 3637428 | tf_op jit(solution)/shard_map/dot_general | solution.py:124
  146.2 0.3 dynamic_update_slice.13
  146.7 0.3 dynamic_update_slice.14
  147.1 0.3 dynamic_update_slice.15
  147.4 0.3 dynamic_update_slice.16
  147.8 0.7 fusion.80
  148.5 6.1 %convolution_convert_fusion = bf16[1536,1536]{1,0:T(8,128)(2,1)S(1)} fusion(bf16[640,1536]{1,0:T(8,128)(2,1)} %reshape.216, bf16[640,1536]{1,0:T(8,128)(2,1)} %all-gather.10.cloned.1.call-done), kind=kOutput, calls=%fused_computation.1 | convolution fusion | flops 3022258176 | bytes 8650752 | tf_op jit(solution)/shard_map/dot_general | solution.py:136
  154.6 2.3 %fusion.110 = (bf16[1536,512]{1,0:T(8,128)(2,1)}, bf16[1536,512]{1,0:T(8,128)(2,1)}, bf16[1536,512]{1,0:T(8,128)(2,1)}) fusion(bf16[1536,1536]{1,0:T(8,128)(2,1)S(1)} %convolution_convert_fusion), kind=kLoop, calls=%fused_computation.150 | loop fusion | bytes 9437184 | tf_op jit(solution)/shard_map/slice | solution.py:143
  (55 shorter events, 1.2 us)
Async XLA Ops:
  7.2 5.8 %copy-start = (bf16[1,128,6144]{2,1,0:T(8,128)(2,1)S(1)}, bf16[1,128,6144]{2,1,0:T(8,128)(2,1)}, u32[]{:S(2)}) copy-start(bf16[1,128,6144]{2,1,0:T(8,128)(2,1)} %param.12) | copy-start | bytes 4718596
  7.2 49.0 %all-gather.12.cloned.1.call-start = ((), (), s32[]{:S(2)}) async-start(), calls=%async_computation.4 | async-start | bytes 5363712 | tf_op jit(solution)/shard_map/all_gather | solution.py:52
  11.1 1.5 copy-start.2
  15.7 82.8 %all-gather.8.cloned.1.call-start = ((), (), s32[]{:S(2)}) async-start(), calls=%async_computation.2 | async-start | bytes 4423680 | tf_op jit(solution)/shard_map/all_gather | solution.py:63
  73.9 36.3 %collective-permute-start = (bf16[160,512]{1,0:T(8,128)(2,1)S(1)}, bf16[160,512]{1,0:T(8,128)(2,1)S(1)}, u32[]{:S(2)}, u32[]{:S(2)}) collective-permute-start(bf16[160,512]{1,0:T(8,128)(2,1)S(1)} %bitcast.133), channel_id=1, source_target_pairs={{0,8},{8,16},{16,24},{24,0},{1,9},{9,17},{17,25},{25,1},{2,10},{10... | collective-permute-start | bytes 491528 | tf_op jit(solution)/shard_map/ppermute | solution.py:153
  75.5 43.0 %collective-permute-start.2 = (bf16[160,512]{1,0:T(8,128)(2,1)S(1)}, bf16[160,512]{1,0:T(8,128)(2,1)}, u32[]{:S(2)}, u32[]{:S(2)}) collective-permute-start(bf16[160,512]{1,0:T(8,128)(2,1)S(1)} %bitcast.134), channel_id=1, source_target_pairs={{0,24},{8,0},{16,8},{24,16},{1,25},{9,1},{17,9},{25,17},{2,26},{10... | collective-permute-start | bytes 491528 | tf_op jit(solution)/shard_map/ppermute | solution.py:153
  77.8 42.6 %collective-permute-start.1 = (bf16[160,512]{1,0:T(8,128)(2,1)S(1)}, bf16[160,512]{1,0:T(8,128)(2,1)S(1)}, u32[]{:S(2)}, u32[]{:S(2)}) collective-permute-start(bf16[160,512]{1,0:T(8,128)(2,1)S(1)} %bitcast.135), channel_id=1, source_target_pairs={{0,16},{8,24},{16,0},{24,8},{1,17},{9,25},{17,1},{25,9},{2,18},{10... | collective-permute-start | bytes 491528 | tf_op jit(solution)/shard_map/ppermute | solution.py:153
  92.8 32.9 %all-to-all-start = ((bf16[8,20,6144]{2,1,0:T(8,128)(2,1)}), bf16[8,20,6144]{2,1,0:T(8,128)(2,1)}, u32[]{:S(2)}, u32[]{:S(2)}) async-start(bf16[8,20,6144]{2,1,0:T(8,128)(2,1)} %convolution_convert_fusion.1), calls=%async_computation | async-start | bytes 4718592 | tf_op jit(solution)/shard_map/all_to_all | solution.py:119
  97.6 50.8 %all-gather.10.cloned.1.call-start = ((), (), s32[]{:S(2)}) async-start(), calls=%async_computation.3 | async-start | bytes 2457600 | tf_op jit(solution)/shard_map/all_gather | solution.py:131
  110.2 0.7 copy-start.7
  118.4 2.0 %copy-start.6 = (bf16[1,160,1536]{2,0,1:T(2,128)(2,1)S(1)}, bf16[1,160,1536]{2,0,1:T(2,128)(2,1)}, u32[]{:S(2)}) copy-start(bf16[1,160,1536]{2,0,1:T(2,128)(2,1)} %get-tuple-element.33) | copy-start | bytes 1474564
  122.3 5.5 %copy-start.5 = (f32[20,6144]{1,0:T(8,128)S(1)}, f32[20,6144]{1,0:T(8,128)}, u32[]{:S(2)}) copy-start(f32[20,6144]{1,0:T(8,128)} %get-tuple-element.40) | copy-start | bytes 1474564
  122.3 5.7 %copy-start.3 = (f32[20,6144]{1,0:T(8,128)S(1)}, f32[20,6144]{1,0:T(8,128)}, u32[]{:S(2)}) copy-start(f32[20,6144]{1,0:T(8,128)} %copy-done.2) | copy-start | bytes 1474564
  122.3 21.1 %copy-start.4 = (bf16[1,128,6144]{2,1,0:T(8,128)(2,1)S(1)}, bf16[1,128,6144]{2,1,0:T(8,128)(2,1)}, u32[]{:S(2)}) copy-start(bf16[1,128,6144]{2,1,0:T(8,128)(2,1)} %param.11) | copy-start | bytes 4718596
  137.9 8.7 %collective-permute-start.3 = (bf16[2,6144]{1,0:T(2,128)(2,1)S(1)}, bf16[2,6144]{1,0:T(2,128)(2,1)S(1)}, u32[]{:S(2)}, u32[]{:S(2)}) collective-permute-start(bf16[2,6144]{1,0:T(2,128)(2,1)S(1)} %pad_maximum_fusion.2), channel_id=1, source_target_pairs={{0,8},{8,16},{16,24},{24,0},{1,9},{9,17},{17,25},{25,1},{2,10},{10... | collective-permute-start | bytes 73736 | tf_op jit(solution)/shard_map/ppermute | solution.py:167
  139.5 7.1 %collective-permute-start.4 = (bf16[2,6144]{1,0:T(2,128)(2,1)S(1)}, bf16[2,6144]{1,0:T(2,128)(2,1)S(1)}, u32[]{:S(2)}, u32[]{:S(2)}) collective-permute-start(bf16[2,6144]{1,0:T(2,128)(2,1)S(1)} %pad_maximum_fusion.2), channel_id=1, source_target_pairs={{0,16},{8,24},{16,0},{24,8},{1,17},{9,25},{17,1},{25,9},{2,18},{10... | collective-permute-start | bytes 73736 | tf_op jit(solution)/shard_map/ppermute | solution.py:167
  140.4 6.2 %collective-permute-start.5 = (bf16[2,6144]{1,0:T(2,128)(2,1)S(1)}, bf16[2,6144]{1,0:T(2,128)(2,1)S(1)}, u32[]{:S(2)}, u32[]{:S(2)}) collective-permute-start(bf16[2,6144]{1,0:T(2,128)(2,1)S(1)} %pad_maximum_fusion.2), channel_id=1, source_target_pairs={{0,24},{8,0},{16,8},{24,16},{1,25},{9,1},{17,9},{25,17},{2,26},{10... | collective-permute-start | bytes 73736 | tf_op jit(solution)/shard_map/ppermute | solution.py:167
  148.5 8.4 %copy-start.1 = (bf16[1,128,6144]{2,1,0:T(8,128)(2,1)S(1)}, bf16[1,128,6144]{2,1,0:T(8,128)(2,1)}, u32[]{:S(2)}) copy-start(bf16[1,128,6144]{2,1,0:T(8,128)(2,1)} %param.12) | copy-start | bytes 4718596
Sparse Core Ops, SparseCore 0:
  15.8 40.3 all-gather.11
  58.0 35.6 all-gather.7
  100.0 44.4 all-gather.9

commit v13 on v12

--- a/solution.py
+++ b/solution.py
@@ -126,8 +126,6 @@
     gate_back = jnp.sum(rows_back * update, axis=-1) * weights * (1.0 - weights)
     router_part = jnp.dot(gate_back, rows, precision=HIGHEST_PRECISION)
     router_group = jnp.sum(lax.all_gather(router_part, "ctx", axis=0, tiled=False), axis=0)
-    router_high = router_group.astype(jnp.bfloat16)
-    router_low = (router_group - router_high.astype(jnp.float32)).astype(jnp.bfloat16)
     factors = lax.all_gather(
         jnp.concatenate([query_back, key_back, value_back], axis=1), "dp", axis=0, tiled=False
     ).reshape(n_dp * slots, 3 * inner)
@@ -159,17 +157,15 @@
             preferred_element_type=jnp.float32,
         )
     grad_out = out_total.astype(jnp.bfloat16)
-    router_pair = jnp.stack([router_high, router_low])
     router_pieces = lax.dynamic_update_index_in_dim(
-        jnp.zeros((n_dp,) + router_pair.shape, jnp.bfloat16), router_pair, dp_index, 0
+        jnp.zeros((n_dp,) + router_group.shape, jnp.float32), router_group, dp_index, 0
     )
     for shift in range(1, n_dp):
-        arrived = lax.ppermute(router_pair, "dp", [(i, (i + shift) % n_dp) for i in range(n_dp)])
+        arrived = lax.ppermute(router_group, "dp", [(i, (i + shift) % n_dp) for i in range(n_dp)])
         router_pieces = lax.dynamic_update_index_in_dim(
             router_pieces, arrived, (dp_index + n_dp - shift) % n_dp, 0
         )
-    router_pieces = router_pieces.astype(jnp.float32)
-    grad_router = jnp.sum(router_pieces[:, 0] + router_pieces[:, 1], axis=0)
+    grad_router = jnp.sum(router_pieces, axis=0)
     return (layer_out, grad_query, grad_key, grad_value, grad_out, grad_router)
 
 

time: 166 us -> 165 us (level)
  no operation moved by 1% of the time
where the time goes in v13:
time: 165 us; the launch traced here: 163 us
  matrix products  49 us (30%)
  blocking collectives  27.8 us (17%)
  waiting for transfers between devices  25.2 us (15%)
  local copies, waits for them, and re-layouts  22.5 us (14%)
  starting transfers between devices  14.8 us (9%)
  between operations  14.8 us (9%)
  other arithmetic  8.98 us (5%)
    all_gather x1, waiting for transfers between devices, body(): lax.all_gather(jnp.concatenate([normed, delta, flag_cols], axis=1), 'ctx'...  21.7 us
    all_to_all x1, blocking collectives, body(): lax.all_to_all(jnp.concatenate([normed, delta], axis=0), 'dp', 1, 0, tile...  18.6 us
    dot_general x3, matrix products, project(): lax.dot_general(chunk_normed, weight, (((2,), (0,)), ((), ())), preferred...  14.8 us
    all_gather x1, blocking collectives, body(): lax.all_gather(router_part, 'ctx', axis=0, tiled=False)  9.27 us
    dot_general x1, matrix products, body(): lax.dot_general(chunk_delta, w_out, (((2,), (1,)), ((), ())), preferred_e...  6.34 us
    dot_general x1, matrix products, contract(): lax.dot_general(left, right, (((0,), (0,)), ((), ())), preferred_element_...  6.13 us
    dot_general x1, matrix products, body(): lax.dot_general(mixed_late.reshape(n_ctx, capacity, inner), w_out, (((2,)...  5.71 us
    ppermute x3, starting transfers between devices, body(): lax.ppermute(router_group, 'dp', [(i, (i + shift) % n_dp) for i in range(...  5.39 us
  transfers between devices with their start and end apart: 10, of which 2 were waited for; matrix products, arithmetic and copies ran while one was open for 39% of the time, Pallas kernels for 0%

profile of v13, /device:TPU:2, one launch (start us, length us, event | category | flops | bytes accessed | tf_op | source)
XLA Modules:
  0.0 163.1 jit_solution(2579473443318761461)
XLA Ops:
  7.2 0.6 compare_reduce_fusion.1
  8.5 0.7 compare_and_fusion
  9.2 1.9 %multiply_reduce_fusion.2 = (f32[20]{0:T(128)S(1)}, f32[20,6144]{1,0:T(8,128)S(1)}) fusion(bf16[1,128,6144]{2,1,0:T(8,128)(2,1)} %param.11, s32[20]{0:T(128)S(1)} %bitcast.142, pred[20]{0:T(512)(128)(4,1)S(1)} %get-tuple-element.26), kind=kOutput, calls=%fused_computation.61 | convolution fusion | flops 31708140 | bytes 2064564 | tf_op jit(solution)/shard_map/dot_general | solution.py:41
  11.1 1.4 fusion.44
  12.6 0.1 multiply_convert_fusion.1
  12.7 0.1 copy.127
  12.8 0.1 copy.128
  12.9 1.2 multiply_convert_fusion
  14.1 0.7 fusion.91
  14.8 0.9 fusion.50
  15.7 0.1 pad_maximum_fusion
  15.8 18.6 %all_to_all.21 = bf16[40,4,1536]{2,0,1:T(8,128)(2,1)} all-to-all(bf16[40,4,1536]{2,0,1:T(8,128)(2,1)S(1)} %bitcast.130), channel_id=1, replica_groups=mesh['dp'=4,'ctx'=8] {'dp'}, dimensions={1} | all-to-all | bytes 983040 | tf_op jit(solution)/shard_map/all_to_all | solution.py:60
  34.5 21.7 %all-gather.12.cloned.1.call-done = bf16[8,20,12416]{2,1,0:T(8,128)(2,1)} async-done(((bf16[1,20,12416]{2,1,0:T(8,128)(2,1)}), bf16[8,20,12416]{2,1,0:T(8,128)(2,1)}) %all-gather.12.cloned.1.call-update) | async-done | bytes 3973136 | tf_op jit(solution)/shard_map/all_gather | solution.py:52
  56.2 4.9 %fusion.8 = f32[8,20,512]{2,1,0:T(8,128)S(1)} fusion(bf16[6144,512]{1,0:T(8,128)(2,1)} %param.14, bf16[8,20,12416]{2,1,0:T(8,128)(2,1)} %all-gather.12.cloned.1.call-done), kind=kOutput, calls=%fused_computation.11 | convolution fusion | flops 1006632960 | bytes 8978432 | tf_op jit(solution)/shard_map/dot_general | solution.py:69
  61.1 0.1 reshape_reshape.10
  61.2 0.2 multiply_reduce_fusion.6
  61.5 4.9 %fusion.6 = f32[8,20,512]{2,1,0:T(8,128)S(1)} fusion(bf16[6144,512]{1,0:T(8,128)(2,1)} %param.15, bf16[8,20,12416]{2,1,0:T(8,128)(2,1)} %all-gather.12.cloned.1.call-done), kind=kOutput, calls=%fused_computation.9 | convolution fusion | flops 1006632960 | bytes 8978432 | tf_op jit(solution)/shard_map/dot_general | solution.py:69
  66.4 0.1 reshape_reshape.11
  66.6 0.2 multiply_reduce_fusion.5
  66.9 1.0 compare_reduce_fusion
  68.0 4.9 %fusion.29 = bf16[8,20,512]{2,1,0:T(8,128)(2,1)S(1)} fusion(bf16[6144,512]{1,0:T(8,128)(2,1)} %param.16, bf16[8,20,12416]{2,1,0:T(8,128)(2,1)} %all-gather.12.cloned.1.call-done), kind=kOutput, calls=%fused_computation.41 | convolution fusion | flops 1006714880 | bytes 8814592 | tf_op jit(solution)/shard_map/dot_general | solution.py:69
  73.0 0.1 fusion.73
  73.1 0.4 fusion.63
  73.6 0.3 fusion.39
  73.9 1.5 collective-permute-start
  75.5 2.3 %collective-permute-start.2 = (bf16[160,512]{1,0:T(8,128)(2,1)S(1)}, bf16[160,512]{1,0:T(8,128)(2,1)}, u32[]{:S(2)}, u32[]{:S(2)}) collective-permute-start(bf16[160,512]{1,0:T(8,128)(2,1)S(1)} %bitcast.132), channel_id=1, source_target_pairs={{0,24},{8,0},{16,8},{24,16},{1,25},{9,1},{17,9},{25,17},{2,26},{10... | collective-permute-start | bytes 491528 | tf_op jit(solution)/shard_map/ppermute | solution.py:151
  77.8 0.6 collective-permute-start.1
  78.4 6.3 %fusion.34 = bf16[8,20,512]{2,1,0:T(8,128)(2,1)S(1)} fusion(bf16[512,6144]{1,0:T(8,128)(2,1)} %param.17, bf16[8,20,12416]{2,1,0:T(8,128)(2,1)} %all-gather.12.cloned.1.call-done), kind=kOutput, calls=%fused_computation.42 | convolution fusion | flops 1006714880 | bytes 8814592 | tf_op jit(solution)/shard_map/dot_general | solution.py:91
  84.8 0.2 fusion.40
  85.1 0.3 fusion.76
  85.3 0.5 multiply_reduce_fusion.3
  85.9 0.7 multiply_reduce_fusion.4
  86.6 0.2 copy_bitcast_fusion.2
  86.8 0.2 copy_bitcast_fusion.3
  87.1 5.7 %convolution_convert_fusion.1 = bf16[8,20,6144]{2,1,0:T(8,128)(2,1)} fusion(bf16[8,20,512]{2,1,0:T(8,128)(2,1)S(1)} %reshape.193, bf16[512,6144]{1,0:T(8,128)(2,1)} %param.17), kind=kOutput, calls=%fused_computation.2 | convolution fusion | flops 1007616000 | bytes 8421376 | tf_op jit(solution)/shard_map/dot_general | solution.py:113
  92.8 4.8 %all-to-all-start = ((bf16[8,20,6144]{2,1,0:T(8,128)(2,1)}), bf16[8,20,6144]{2,1,0:T(8,128)(2,1)}, u32[]{:S(2)}, u32[]{:S(2)}) async-start(bf16[8,20,6144]{2,1,0:T(8,128)(2,1)} %convolution_convert_fusion.1), calls=%async_computation | async-start | bytes 4718592 | tf_op jit(solution)/shard_map/all_to_all | solution.py:119
  97.6 0.8 pad_maximum_fusion.1
  98.5 4.3 %copy.144 = bf16[8,160,1536]{2,0,1:T(8,128)(2,1)S(1)} copy(bf16[8,160,1536]{2,1,0:T(8,128)(2,1)} %all-gather.8.cloned.1.call-done) | data formatting | bytes 7864320 | tf_op jit(solution)/shard_map/all_gather | solution.py:63
  102.8 0.3 slice_bitcast_fusion
  103.0 1.5 copy.146
  104.6 5.0 %constant_dynamic-slice_fusion.1 = (bf16[1,160,1536]{2,0,1:T(2,128)(2,1)}, bf16[1,160,1536]{2,0,1:T(2,128)(2,1)}, bf16[1,160,1536]{2,0,1:T(2,128)(2,1)S(1)}, bf16[1,160,1536]{2,0,1:T(2,128)(2,1)S(1)}) fusion(bf16[4,160,1536]{2,0,1:T(4,128)(2,1)S(1)} %bitcast.126, s32[]{:T(128)S(6)} %select_n.48, s32[]{:T(128)S(6)} %select_n.50, s32[]{:T(128)S(6)} %select_n.46, ...), kind=kLoop, calls=%fused_computation.130 | loop fusion | bytes 3932176 | tf_op jit(solution)/shard_map/jit(dynamic_index_in_dim)/dynamic_slice | solution.py:155
  109.6 0.6 fusion.59
  110.2 0.7 copy-done.7
  110.9 1.5 convolution_add_fusion.2
  112.4 2.0 %copy.145 = bf16[4,8,20,1536]{3,2,1,0:T(8,128)(2,1)} copy(bf16[4,8,20,1536]{3,1,2,0:T(8,128)(2,1)S(1)} %get-tuple-element.32) | data formatting | bytes 3932160 | tf_op jit(solution)/shard_map/transpose | solution.py:66
  114.4 4.0 %reshape.195 = bf16[640,1536]{1,0:T(8,128)(2,1)} reshape(bf16[4,8,20,1536]{3,2,1,0:T(8,128)(2,1)} %copy.145) | data formatting | bytes 3932160 | tf_op jit(solution)/shard_map/reshape | solution.py:66
  118.4 2.0 %fusion.52 = f32[512,1536]{1,0:T(8,128)S(1)} fusion(bf16[160,512]{1,0:T(8,128)(2,1)} %collective-permute-done.2, bf16[1,160,1536]{2,0,1:T(2,128)(2,1)} %get-tuple-element.34), kind=kOutput, calls=%fused_computation.65 | convolution fusion | flops 251658240 | bytes 3801088 | tf_op jit(solution)/shard_map/dot_general | solution.py:153
  120.4 1.8 %fusion.13 = bf16[512,1536]{1,0:T(8,128)(2,1)} fusion(f32[512,1536]{1,0:T(8,128)S(1)} %fusion.52, f32[512,1536]{1,0:T(8,128)S(1)} %convolution_add_fusion.2, bf16[160,512]{1,0:T(8,128)(2,1)S(1)} %collective-permute-done.1, bf16[1,160,1536]{2,0,1:T(2,128)(2,1)S(1)} %copy-done.6), kind=kOutput, calls=%fused_computation.19 | convolution fusion | flops 254017536 | bytes 8519680 | tf_op jit(solution)/shard_map/dot_general | solution.py:153
  122.3 3.4 %all-to-all-done = bf16[8,20,6144]{2,1,0:T(8,128)(2,1)} async-done(((bf16[8,20,6144]{2,1,0:T(8,128)(2,1)}), bf16[8,20,6144]{2,1,0:T(8,128)(2,1)}, u32[]{:S(2)}, u32[]{:S(2)}) %all-to-all-start) | async-done | bytes 1966112 | tf_op jit(solution)/shard_map/all_to_all | solution.py:119
  125.7 2.1 %convert_reduce_fusion = f32[20,6144]{1,0:T(8,128)S(1)} fusion(bf16[8,20,6144]{2,1,0:T(8,128)(2,1)} %all-to-all-done), kind=kLoop, calls=%fused_computation.15 | loop fusion | flops 1843200 | bytes 2457600 | tf_op jit(solution)/shard_map/reduce_sum | solution.py:122
  127.8 0.2 multiply_reduce_fusion.1
  128.0 0.4 fusion.98
  128.4 9.3 %all-gather.2 = f32[49152]{0:T(1024)S(1)} all-gather(f32[6144]{0:T(1024)S(1)} %bitcast.136), channel_id=4, replica_groups=mesh['dp'=4,'ctx'=8] {'ctx'}, dimensions={0}, use_global_device_ids=true | all-gather | bytes 221184 | tf_op jit(solution)/shard_map/all_gather | solution.py:128
  137.8 1.6 collective-permute-start.3
  139.3 1.0 collective-permute-start.4
  140.3 2.8 %collective-permute-start.5 = (f32[6144]{0:T(1024)S(1)}, f32[6144]{0:T(1024)S(1)}, u32[]{:S(2)}, u32[]{:S(2)}) collective-permute-start(f32[6144]{0:T(1024)S(1)} %reduce_sum.108), channel_id=1, source_target_pairs={{0,24},{8,0},{16,8},{24,16},{1,25},{9,1},{17,9},{25,17},{2,26},{10... | collective-permute-start | bytes 73736 | tf_op jit(solution)/shard_map/ppermute | solution.py:164
  143.2 2.8 %fusion.2 = bf16[1,128,6144]{2,1,0:T(8,128)(2,1)} fusion(bf16[1,128,6144]{2,1,0:T(8,128)(2,1)S(1)} %copy-done.4, f32[20,6144]{1,0:T(8,128)S(1)} %convert_reduce_fusion, f32[20]{0:T(128)S(1)} %fusion.44, s32[20]{0:T(128)S(1)} %bitcast.144, pred[20]{0:T(512)(128)(4,1)S(1)} %get-tuple-element.26), kind=kOutput, calls=%fused_computation.5 | convolution fusion | flops 191230976 | bytes 3637428 | tf_op jit(solution)/shard_map/dot_general | solution.py:124
  145.9 0.4 dynamic_update_slice.13
  146.3 0.4 dynamic_update_slice.14
  146.7 0.4 dynamic_update_slice.15
  147.1 0.4 dynamic_update_slice.16
  147.5 0.7 reduce_sum.109
  148.2 6.1 %convolution_convert_fusion = bf16[1536,1536]{1,0:T(8,128)(2,1)S(1)} fusion(bf16[640,1536]{1,0:T(8,128)(2,1)} %reshape.195, bf16[640,1536]{1,0:T(8,128)(2,1)} %all-gather.10.cloned.1.call-done), kind=kOutput, calls=%fused_computation.1 | convolution fusion | flops 3022258176 | bytes 8650752 | tf_op jit(solution)/shard_map/dot_general | solution.py:134
  154.3 2.3 %fusion.109 = (bf16[1536,512]{1,0:T(8,128)(2,1)}, bf16[1536,512]{1,0:T(8,128)(2,1)}, bf16[1536,512]{1,0:T(8,128)(2,1)}) fusion(bf16[1536,1536]{1,0:T(8,128)(2,1)S(1)} %convolution_convert_fusion), kind=kLoop, calls=%fused_computation.146 | loop fusion | bytes 9437184 | tf_op jit(solution)/shard_map/slice | solution.py:141
  (46 shorter events, 0.8 us)
Async XLA Ops:
  7.2 5.8 %copy-start = (bf16[1,128,6144]{2,1,0:T(8,128)(2,1)S(1)}, bf16[1,128,6144]{2,1,0:T(8,128)(2,1)}, u32[]{:S(2)}) copy-start(bf16[1,128,6144]{2,1,0:T(8,128)(2,1)} %param.12) | copy-start | bytes 4718596
  7.2 49.0 %all-gather.12.cloned.1.call-start = ((), (), s32[]{:S(2)}) async-start(), calls=%async_computation.4 | async-start | bytes 5363712 | tf_op jit(solution)/shard_map/all_gather | solution.py:52
  11.1 1.5 copy-start.2
  15.7 82.8 %all-gather.8.cloned.1.call-start = ((), (), s32[]{:S(2)}) async-start(), calls=%async_computation.2 | async-start | bytes 4423680 | tf_op jit(solution)/shard_map/all_gather | solution.py:63
  73.9 36.3 %collective-permute-start = (bf16[160,512]{1,0:T(8,128)(2,1)S(1)}, bf16[160,512]{1,0:T(8,128)(2,1)S(1)}, u32[]{:S(2)}, u32[]{:S(2)}) collective-permute-start(bf16[160,512]{1,0:T(8,128)(2,1)S(1)} %bitcast.131), channel_id=1, source_target_pairs={{0,8},{8,16},{16,24},{24,0},{1,9},{9,17},{17,25},{25,1},{2,10},{10... | collective-permute-start | bytes 491528 | tf_op jit(solution)/shard_map/ppermute | solution.py:151
  75.5 43.0 %collective-permute-start.2 = (bf16[160,512]{1,0:T(8,128)(2,1)S(1)}, bf16[160,512]{1,0:T(8,128)(2,1)}, u32[]{:S(2)}, u32[]{:S(2)}) collective-permute-start(bf16[160,512]{1,0:T(8,128)(2,1)S(1)} %bitcast.132), channel_id=1, source_target_pairs={{0,24},{8,0},{16,8},{24,16},{1,25},{9,1},{17,9},{25,17},{2,26},{10... | collective-permute-start | bytes 491528 | tf_op jit(solution)/shard_map/ppermute | solution.py:151
  77.8 42.6 %collective-permute-start.1 = (bf16[160,512]{1,0:T(8,128)(2,1)S(1)}, bf16[160,512]{1,0:T(8,128)(2,1)S(1)}, u32[]{:S(2)}, u32[]{:S(2)}) collective-permute-start(bf16[160,512]{1,0:T(8,128)(2,1)S(1)} %bitcast.133), channel_id=1, source_target_pairs={{0,16},{8,24},{16,0},{24,8},{1,17},{9,25},{17,1},{25,9},{2,18},{10... | collective-permute-start | bytes 491528 | tf_op jit(solution)/shard_map/ppermute | solution.py:151
  92.8 32.9 %all-to-all-start = ((bf16[8,20,6144]{2,1,0:T(8,128)(2,1)}), bf16[8,20,6144]{2,1,0:T(8,128)(2,1)}, u32[]{:S(2)}, u32[]{:S(2)}) async-start(bf16[8,20,6144]{2,1,0:T(8,128)(2,1)} %convolution_convert_fusion.1), calls=%async_computation | async-start | bytes 4718592 | tf_op jit(solution)/shard_map/all_to_all | solution.py:119
  97.6 50.5 %all-gather.10.cloned.1.call-start = ((), (), s32[]{:S(2)}) async-start(), calls=%async_computation.3 | async-start | bytes 2457600 | tf_op jit(solution)/shard_map/all_gather | solution.py:129
  110.2 0.7 copy-start.7
  118.4 2.0 %copy-start.6 = (bf16[1,160,1536]{2,0,1:T(2,128)(2,1)S(1)}, bf16[1,160,1536]{2,0,1:T(2,128)(2,1)}, u32[]{:S(2)}) copy-start(bf16[1,160,1536]{2,0,1:T(2,128)(2,1)} %get-tuple-element.33) | copy-start | bytes 1474564
  122.3 5.5 %copy-start.5 = (f32[20,6144]{1,0:T(8,128)S(1)}, f32[20,6144]{1,0:T(8,128)}, u32[]{:S(2)}) copy-start(f32[20,6144]{1,0:T(8,128)} %get-tuple-element.40) | copy-start | bytes 1474564
  122.3 5.7 %copy-start.3 = (f32[20,6144]{1,0:T(8,128)S(1)}, f32[20,6144]{1,0:T(8,128)}, u32[]{:S(2)}) copy-start(f32[20,6144]{1,0:T(8,128)} %copy-done.2) | copy-start | bytes 1474564
  122.3 20.9 %copy-start.4 = (bf16[1,128,6144]{2,1,0:T(8,128)(2,1)S(1)}, bf16[1,128,6144]{2,1,0:T(8,128)(2,1)}, u32[]{:S(2)}) copy-start(bf16[1,128,6144]{2,1,0:T(8,128)(2,1)} %param.11) | copy-start | bytes 4718596
  137.8 8.6 %collective-permute-start.3 = (f32[6144]{0:T(1024)S(1)}, f32[6144]{0:T(1024)S(1)}, u32[]{:S(2)}, u32[]{:S(2)}) collective-permute-start(f32[6144]{0:T(1024)S(1)} %reduce_sum.108), channel_id=1, source_target_pairs={{0,8},{8,16},{16,24},{24,0},{1,9},{9,17},{17,25},{25,1},{2,10},{10... | collective-permute-start | bytes 73736 | tf_op jit(solution)/shard_map/ppermute | solution.py:164
  139.3 7.4 %collective-permute-start.4 = (f32[6144]{0:T(1024)S(1)}, f32[6144]{0:T(1024)S(1)}, u32[]{:S(2)}, u32[]{:S(2)}) collective-permute-start(f32[6144]{0:T(1024)S(1)} %reduce_sum.108), channel_id=1, source_target_pairs={{0,16},{8,24},{16,0},{24,8},{1,17},{9,25},{17,1},{25,9},{2,18},{10... | collective-permute-start | bytes 73736 | tf_op jit(solution)/shard_map/ppermute | solution.py:164
  140.3 6.8 %collective-permute-start.5 = (f32[6144]{0:T(1024)S(1)}, f32[6144]{0:T(1024)S(1)}, u32[]{:S(2)}, u32[]{:S(2)}) collective-permute-start(f32[6144]{0:T(1024)S(1)} %reduce_sum.108), channel_id=1, source_target_pairs={{0,24},{8,0},{16,8},{24,16},{1,25},{9,1},{17,9},{25,17},{2,26},{10... | collective-permute-start | bytes 73736 | tf_op jit(solution)/shard_map/ppermute | solution.py:164
  148.1 8.4 %copy-start.1 = (bf16[1,128,6144]{2,1,0:T(8,128)(2,1)S(1)}, bf16[1,128,6144]{2,1,0:T(8,128)(2,1)}, u32[]{:S(2)}) copy-start(bf16[1,128,6144]{2,1,0:T(8,128)(2,1)} %param.12) | copy-start | bytes 4718596
Sparse Core Ops, SparseCore 0:
  15.8 40.3 all-gather.11
  58.0 35.6 all-gather.7
  100.0 44.6 all-gather.9
